TPU v7x, 512 devices: a whole 4x4x16 slice. The times are simulated.
512 devices in a mesh: tm: 32 (over z, x_hi), fsdp: 16 (over y, x_lo, core).
Axes of the slice: x: 4 (x_hi: 2, x_lo: 2; x = x_hi * 2 + x_lo), y: 4, z: 16, core: 2. Of those that a mesh axis runs over, the one named last changes fastest.
Arguments:
- latents: bfloat16 [32768, 3072], P(('tm', 'fsdp')), may hold values from -6 to 6
- projected: bfloat16 [32768, 3, 2048], P(('tm', 'fsdp')), may hold values from -20 to 20
- out_weight: bfloat16 [2048, 3072], P(None, 'fsdp'), may hold values from -0.5 to 0.5
- gate_table: float32 [40, 3072], replicated, may hold values from 0.25 to 2
- timesteps: int32 [128], P('tm'), may hold values from 0 to 39
Outputs:
- updated: bfloat16 [32768, 3072], P(('tm', 'fsdp'))
All inputs are finite; a program needn't handle non-finite values.
Results may differ from a plain program's by a relative error of at most 0.0085.
Values may be sent and summed in bfloat16 or wider, within the bound.
No kernel may reach another device: no remote copies, remote signals or barrier semaphores. Data moves between devices by JAX's collectives and lax.ppermute only.
A program may use at most 64 MiB of HBM per device.

v0:
```python
import jax
import jax.numpy as jnp
from jax import lax
from jax.sharding import PartitionSpec as P

FRAME_TOK = 256


def passed_along(value, axis, steps):
    count = lax.axis_size(axis)
    initial, last = (max(0, -steps), min(count, count - steps))
    return lax.ppermute(value, axis, [(source, source + steps) for source in range(initial, last)])


def attend(queries, extended, first_frame, frame_count):
    pair_rows = 2 * FRAME_TOK
    key_count = 5 * FRAME_TOK
    score_scale = queries.shape[1] ** (-0.5)
    row_frame = jnp.arange(pair_rows, dtype=jnp.int32) // FRAME_TOK
    col_frame = jnp.arange(key_count, dtype=jnp.int32) // FRAME_TOK

    def frame_pair(pair_index):
        offset = pair_index * pair_rows
        query_block = lax.dynamic_slice_in_dim(queries, offset, pair_rows, 0)
        window = lax.dynamic_slice_in_dim(extended, offset, key_count, 0)
        key_block = window[:, 0]
        value_block = window[:, 1]
        scores = (
            lax.dot_general(
                query_block, key_block, (((1,), (1,)), ((), ())), preferred_element_type=jnp.float32
            )
            * score_scale
        )
        distance = col_frame[None, :] - row_frame[:, None]
        existing = first_frame + 2 * pair_index + col_frame - 3 >= 0
        allowed = (distance >= 0) & (distance <= 3) & existing[None, :]
        scores = jnp.where(allowed, scores, -1e30)
        row_max = jnp.max(scores, axis=-1, keepdims=True)
        weights = jnp.exp(scores - row_max)
        row_sum = jnp.sum(weights, axis=-1, keepdims=True)
        probability = (weights / row_sum).astype(jnp.bfloat16)
        return jnp.dot(probability, value_block, preferred_element_type=jnp.float32).astype(
            jnp.bfloat16
        )

    blocks = lax.map(frame_pair, jnp.arange(frame_count // 2, dtype=jnp.int32))
    return blocks.reshape(frame_count * FRAME_TOK, queries.shape[1])


def body(latents, projected, out_weight, gate_table, timesteps):
    row_count = latents.shape[0]
    frame_count = timesteps.shape[0]
    group_tokens = frame_count * FRAME_TOK
    head_view = lax.all_to_all(projected, "fsdp", split_axis=2, concat_axis=0, tiled=True)
    queries = head_view[:, 0]
    key_values = head_view[:, 1:3]
    trailing = passed_along(key_values[group_tokens - 3 * FRAME_TOK :], "tm", 1)
    extended = jnp.concatenate([trailing, key_values], axis=0)
    first_frame = lax.axis_index("tm") * frame_count
    attended = attend(queries, extended, first_frame, frame_count)
    gathered_heads = lax.all_to_all(attended, "fsdp", split_axis=0, concat_axis=1, tiled=True)
    update = jnp.dot(
        gathered_heads,
        lax.all_gather(out_weight, "fsdp", axis=1, tiled=True),
        preferred_element_type=jnp.float32,
    )
    step_count = gate_table.shape[0]
    step_onehot = (timesteps[:, None] == jnp.arange(step_count, dtype=jnp.int32)[None, :]).astype(
        jnp.float32
    )
    frame_gates = jnp.dot(step_onehot, gate_table, precision=lax.Precision.HIGHEST)
    row_frame = (
        lax.axis_index("fsdp") * row_count + jnp.arange(row_count, dtype=jnp.int32)
    ) // FRAME_TOK
    row_onehot = (row_frame[:, None] == jnp.arange(frame_count, dtype=jnp.int32)[None, :]).astype(
        jnp.float32
    )
    row_gates = jnp.dot(row_onehot, frame_gates, precision=lax.Precision.HIGHEST)
    return (latents.astype(jnp.float32) + row_gates * update).astype(jnp.bfloat16)


def solution(mesh):
    in_specs = (
        P(("tm", "fsdp"), None),
        P(("tm", "fsdp"), None, None),
        P(None, "fsdp"),
        P(),
        P("tm"),
    )
    out_specs = P(("tm", "fsdp"), None)
    return jax.shard_map(body, mesh=mesh, in_specs=in_specs, out_specs=out_specs, check_vma=False)
```

profile of v0, /device:TPU:1, one launch (start us, length us, event | category | flops | bytes accessed | tf_op | source)
XLA Modules:
  0.0 122.3 jit_solution(10871948725285879211)
XLA Ops:
  6.5 0.0 copy-start
  6.5 0.0 all-gather.2.cloned.1.call-start
  6.5 0.7 all-gather.2.cloned.1.call-update
  7.3 2.9 %copy.9 = bf16[64,3,2048]{0,1,2:T(4,128)(2,1)S(1)} copy(bf16[64,3,2048]{2,0,1:T(8,128)(2,1)} %param.8) | data formatting | bytes 1572864 | tf_op args[1]
  10.1 2.5 %reshape.39 = bf16[16,2,12288]{2,1,0:T(2,128)(2,1)} reshape(bf16[2048,3,64]{2,1,0:T(4,128)(2,1)S(1)} %bitcast.45) | data formatting | bytes 1572864
  12.6 10.3 %all-to-all-start = ((bf16[16,2,12288]{2,1,0:T(2,128)(2,1)}), bf16[16,2,12288]{2,1,0:T(2,128)(2,1)S(1)}, u32[]{:S(2)}, u32[]{:S(2)}) async-start(bf16[16,2,12288]{2,1,0:T(2,128)(2,1)} %reshape.39), calls=%async_computation | async-start | bytes 1572864 | tf_op jit(solution)/shard_map/all_to_all | solution.py:54
  22.9 0.0 copy-start.3
  22.9 13.0 %all-to-all-done = bf16[16,2,12288]{2,1,0:T(2,128)(2,1)S(1)} async-done(((bf16[16,2,12288]{2,1,0:T(2,128)(2,1)}), bf16[16,2,12288]{2,1,0:T(2,128)(2,1)S(1)}, u32[]{:S(2)}, u32[]{:S(2)}) %all-to-all-start) | async-done | bytes 786464 | tf_op jit(solution)/shard_map/all_to_all | solution.py:54
  36.0 1.3 %reshape.40 = bf16[2048,3,64]{2,1,0:T(4,128)(2,1)S(1)} reshape(bf16[16,2,12288]{2,1,0:T(2,128)(2,1)S(1)} %all-to-all-done) | data formatting | bytes 1572864
  37.2 1.2 copy.10
  38.5 1.3 %collective-permute-start = (bf16[768,2,128]{2,0,1:T(8,128)(2,1)S(1)}, bf16[768,2,128]{2,0,1:T(8,128)(2,1)S(1)}, u32[]{:S(2)}, u32[]{:S(2)}) collective-permute-start(bf16[768,2,128]{2,0,1:T(8,128)(2,1)S(1)} %slice.30), channel_id=1, source_target_pairs={{0,16},{16,32},{32,48},{48,64},{64,80},{80,96},{96,112},{112,128},... | collective-permute-start | bytes 1179656 | tf_op jit(solution)/shard_map/ppermute | solution.py:12
  39.8 0.0 copy-done
  39.8 0.0 copy-done.3
  39.8 0.3 fusion.27
  40.1 0.7 slice_bitcast_fusion
  40.9 15.6 %collective-permute-done = bf16[768,2,128]{2,0,1:T(8,128)(2,1)S(1)} collective-permute-done((bf16[768,2,128]{2,0,1:T(8,128)(2,1)S(1)}, bf16[768,2,128]{2,0,1:T(8,128)(2,1)S(1)}, u32[]{:S(2)}, u32[]{:S(2)}) %collective-permute-start) | collective-permute-done | bytes 393248 | tf_op jit(solution)/shard_map/ppermute | solution.py:12
  56.5 1.1 pad_maximum_fusion
  57.5 0.5 iota.27
  58.1 0.0 copy-start.1
  58.1 16.9 %while.14 = (s32[]{:T(128)}, bf16[2,512,128]{2,1,0:T(8,128)(2,1)}, s32[2]{0:T(128)}, s32[]{:T(128)}, bf16[1024,128]{1,0:T(8,128)(2,1)}, /*index=5*/bf16[1792,2,1...) while((s32[]{:T(128)}, bf16[2,512,128]{2,1,0:T(8,128)(2,1)}, ...), condition=%wide.region_3.4_spmd.clone.clone, body=%wide.region_0.3_spmd.clone.clone.sunk | while | flops 344156928 | bytes 8817956 | solution.py:46
  58.1 1.2 dynamic_slice.32
  60.4 2.1 %fusion.37 = (f32[512]{0:T(512)S(1)}, f32[512,1280]{1,0:T(8,128)S(1)}) fusion(bf16[1792,2,128]{2,0,1:T(8,128)(2,1)} %get-tuple-element.231, s32[]{:T(128)S(6)} %select_n.71, bf16[1024,128]{1,0:T(8,128)(2,1)} %get-tuple-element.230, s32[]{:T(128)S(6)} %select_n.72, pred[1280]{0:T(1024)(128)(4,1)S(1)} %add_compare_fusion.2, ...), kind=kOutput, calls=%fused_computation.52.clone.1 | convolution fusion | flops 173014528 | bytes 3090696 | tf_op jit(solution)/shard_map/while/body/eval_jaxpr/dot_general | solution.py:29
  62.6 0.0 copy-start.2
  62.6 0.6 copy-done.2
  63.2 1.1 fusion.38
  64.3 2.3 %fusion.39 = bf16[2,512,128]{2,1,0:T(8,128)(2,1)} fusion(bf16[2,512,128]{2,1,0:T(8,128)(2,1)} %get-tuple-element.214, s32[]{:T(128)} %get-tuple-element.213, f32[512,1280]{1,0:T(8,128)S(1)} %get-tuple-element.198, f32[512]{0:T(512)} %fusion.38, f32[512]{0:T(512)} %copy-done.2, bf16[1792,2,128]{2,0,1:T(8,128)(2,1)} %get-tuple-element.231, ...), kind=kOutput, calls=%fused_computation.14.clone.1 | convolution fusion | flops 169803776 | bytes 3084808 | tf_op jit(solution)/shard_map/while/body/eval_jaxpr/dot_general | solution.py:42
  66.5 1.2 dynamic_slice.32
  68.8 2.1 %fusion.37 = (f32[512]{0:T(512)S(1)}, f32[512,1280]{1,0:T(8,128)S(1)}) fusion(bf16[1792,2,128]{2,0,1:T(8,128)(2,1)} %get-tuple-element.231, s32[]{:T(128)S(6)} %select_n.71, bf16[1024,128]{1,0:T(8,128)(2,1)} %get-tuple-element.230, s32[]{:T(128)S(6)} %select_n.72, pred[1280]{0:T(1024)(128)(4,1)S(1)} %add_compare_fusion.2, ...), kind=kOutput, calls=%fused_computation.52.clone.1 | convolution fusion | flops 173014528 | bytes 3090696 | tf_op jit(solution)/shard_map/while/body/eval_jaxpr/dot_general | solution.py:29
  71.0 0.0 copy-start.2
  71.0 0.6 copy-done.2
  71.6 1.1 fusion.38
  72.7 2.3 %fusion.39 = bf16[2,512,128]{2,1,0:T(8,128)(2,1)} fusion(bf16[2,512,128]{2,1,0:T(8,128)(2,1)} %get-tuple-element.214, s32[]{:T(128)} %get-tuple-element.213, f32[512,1280]{1,0:T(8,128)S(1)} %get-tuple-element.198, f32[512]{0:T(512)} %fusion.38, f32[512]{0:T(512)} %copy-done.2, bf16[1792,2,128]{2,0,1:T(8,128)(2,1)} %get-tuple-element.231, ...), kind=kOutput, calls=%fused_computation.14.clone.1 | convolution fusion | flops 169803776 | bytes 3084808 | tf_op jit(solution)/shard_map/while/body/eval_jaxpr/dot_general | solution.py:42
  74.9 5.4 %all-to-all-start.1 = ((bf16[16,64,128]{2,1,0:T(8,128)(2,1)}), bf16[16,64,128]{2,1,0:T(8,128)(2,1)S(1)}, u32[]{:S(2)}, u32[]{:S(2)}) async-start(bf16[16,64,128]{2,1,0:T(8,128)(2,1)} %bitcast.49), calls=%async_computation.1 | async-start | bytes 524288 | tf_op jit(solution)/shard_map/all_to_all | solution.py:61
  80.4 0.5 fusion.25
  80.9 9.6 %all-to-all-done.1 = bf16[16,64,128]{2,1,0:T(8,128)(2,1)S(1)} async-done(((bf16[16,64,128]{2,1,0:T(8,128)(2,1)}), bf16[16,64,128]{2,1,0:T(8,128)(2,1)S(1)}, u32[]{:S(2)}, u32[]{:S(2)}) %all-to-all-start.1) | async-done | bytes 262176 | tf_op jit(solution)/shard_map/all_to_all | solution.py:61
  90.5 15.7 %all-gather.2.cloned.1.call-done = bf16[2048,3072]{0,1:T(8,128)(2,1)} async-done(((bf16[2048,192]{0,1:T(8,128)(2,1)}), bf16[2048,3072]{0,1:T(8,128)(2,1)}) %all-gather.2.cloned.1.call-update) | async-done | bytes 12582928 | tf_op jit(solution)/shard_map/all_gather | solution.py:64
  106.2 0.0 copy-done.1
  106.2 9.2 %fusion.22 = bf16[64,3072]{1,0:T(8,128)(2,1)} fusion(f32[64,3072]{1,0:T(8,128)S(1)} %fusion.25, bf16[2048,3072]{0,1:T(8,128)(2,1)} %all-gather.2.cloned.1.call-done, bf16[64,3072]{1,0:T(8,128)(2,1)S(1)} %copy-done.1, bf16[16,64,128]{2,1,0:T(8,128)(2,1)S(1)} %all-to-all-done.1), kind=kOutput, calls=%fused_computation.37 | convolution fusion | flops 806092800 | bytes 14417920 | tf_op jit(solution)/shard_map/dot_general | solution.py:62
  (10 shorter events, 0.1 us)
Async XLA Ops:
  6.5 33.3 %copy-start = (f32[40,3072]{1,0:T(8,128)S(1)}, f32[40,3072]{1,0:T(8,128)}, u32[]{:S(2)}) copy-start(f32[40,3072]{1,0:T(8,128)} %param.10) | copy-start | bytes 1474564
  6.5 99.7 %all-gather.2.cloned.1.call-start = ((), (), s32[]{:S(2)}) async-start(), calls=%async_computation.2 | async-start | bytes 13369344 | tf_op jit(solution)/shard_map/all_gather | solution.py:64
  12.6 23.3 %all-to-all-start = ((bf16[16,2,12288]{2,1,0:T(2,128)(2,1)}), bf16[16,2,12288]{2,1,0:T(2,128)(2,1)S(1)}, u32[]{:S(2)}, u32[]{:S(2)}) async-start(bf16[16,2,12288]{2,1,0:T(2,128)(2,1)} %reshape.39), calls=%async_computation | async-start | bytes 1572864 | tf_op jit(solution)/shard_map/all_to_all | solution.py:54
  22.9 16.9 %copy-start.3 = (s32[4]{0:T(128)S(1)}, s32[4]{0:T(128)}, u32[]{:S(2)}) copy-start(s32[4]{0:T(128)} %param.11) | copy-start | bytes 52
  38.5 18.0 %collective-permute-start = (bf16[768,2,128]{2,0,1:T(8,128)(2,1)S(1)}, bf16[768,2,128]{2,0,1:T(8,128)(2,1)S(1)}, u32[]{:S(2)}, u32[]{:S(2)}) collective-permute-start(bf16[768,2,128]{2,0,1:T(8,128)(2,1)S(1)} %slice.30), channel_id=1, source_target_pairs={{0,16},{16,32},{32,48},{48,64},{64,80},{80,96},{96,112},{112,128},... | collective-permute-start | bytes 1179656 | tf_op jit(solution)/shard_map/ppermute | solution.py:12
  58.1 48.2 %copy-start.1 = (bf16[64,3072]{1,0:T(8,128)(2,1)S(1)}, bf16[64,3072]{1,0:T(8,128)(2,1)}, u32[]{:S(2)}) copy-start(bf16[64,3072]{1,0:T(8,128)(2,1)} %param.7) | copy-start | bytes 1179652
  62.6 0.6 copy-start.2
  71.0 0.6 copy-start.2
  74.9 15.6 %all-to-all-start.1 = ((bf16[16,64,128]{2,1,0:T(8,128)(2,1)}), bf16[16,64,128]{2,1,0:T(8,128)(2,1)S(1)}, u32[]{:S(2)}, u32[]{:S(2)}) async-start(bf16[16,64,128]{2,1,0:T(8,128)(2,1)} %bitcast.49), calls=%async_computation.1 | async-start | bytes 524288 | tf_op jit(solution)/shard_map/all_to_all | solution.py:61
Sparse Core Ops, SparseCore 0:
  9.5 96.6 all-gather.1
where the time goes:
time: 123 us; the launch traced here: 122 us
  waiting for transfers between devices  54.7 us (44%)
  matrix products  18.8 us (15%)
  starting transfers between devices  17 us (14%)
  between operations  13.5 us (11%)
  local copies, waits for them, and re-layouts  12.7 us (10%)
  other arithmetic  3.28 us (3%)
  loops' own time  2.28 us (2%)
    all_gather x1, waiting for transfers between devices, body(): lax.all_gather(out_weight, 'fsdp', axis=1, tiled=True)  15.7 us
    ppermute x1, waiting for transfers between devices, passed_along(): lax.ppermute(value, axis, [(source, source + steps) for source in range(i...  15.6 us
    all_to_all x1, waiting for transfers between devices, body(): lax.all_to_all(projected, 'fsdp', split_axis=2, concat_axis=0, tiled=True)  13 us
    all_to_all x1, starting transfers between devices, body(): lax.all_to_all(projected, 'fsdp', split_axis=2, concat_axis=0, tiled=True)  10.3 us
    all_to_all x1, waiting for transfers between devices, body(): lax.all_to_all(attended, 'fsdp', split_axis=0, concat_axis=1, tiled=True)  9.62 us
    dot_general x1, matrix products, body(): jnp.dot(gathered_heads, lax.all_gather(out_weight, 'fsdp', axis=1, tiled=...  9.25 us
    unnamed x9, local copies, waits for them, and re-layouts  6.63 us
    all_to_all x1, starting transfers between devices, body(): lax.all_to_all(attended, 'fsdp', split_axis=0, concat_axis=1, tiled=True)  5.45 us
  transfers between devices with their start and end apart: 4, of which 4 were waited for; matrix products, arithmetic and copies ran while one was open for 20% of the time, Pallas kernels for 0%

commit v1 on v0

v1 whole, which is shorter than its diff:
```python
import jax
import jax.numpy as jnp
from jax import lax
from jax.experimental import pallas as pl
from jax.experimental.pallas import tpu as pltpu
from jax.sharding import Mesh
from jax.sharding import PartitionSpec as P

FRAME_TOK = 256
WINDOW = 4


def passed_along(value, axis, steps):
    count = lax.axis_size(axis)
    initial, last = (max(0, -steps), min(count, count - steps))
    return lax.ppermute(value, axis, [(source, source + steps) for source in range(initial, last)])


def attention_kernel(flag_ref, qkv_ref, halo_ref, out_ref):
    frame_count = qkv_ref.shape[1] // FRAME_TOK
    score_scale = qkv_ref.shape[2] ** (-0.5)
    has_prev = flag_ref[0] > 0
    for frame in range(frame_count):
        query = qkv_ref[0, pl.ds(frame * FRAME_TOK, FRAME_TOK), :]
        blocks = []
        for back in range(WINDOW):
            source = frame - (WINDOW - 1) + back
            if source >= 0:
                rows = pl.ds(source * FRAME_TOK, FRAME_TOK)
                key, value = qkv_ref[1, rows, :], qkv_ref[2, rows, :]
            else:
                rows = pl.ds((source + WINDOW - 1) * FRAME_TOK, FRAME_TOK)
                key, value = halo_ref[0, rows, :], halo_ref[1, rows, :]
            scores = (
                lax.dot_general(
                    query, key, (((1,), (1,)), ((), ())), preferred_element_type=jnp.float32
                )
                * score_scale
            )
            if source < 0:
                scores = jnp.where(has_prev, scores, -1e30)
            blocks.append((scores, value))
        row_max = blocks[0][0].max(axis=1, keepdims=True)
        for scores, _ in blocks[1:]:
            row_max = jnp.maximum(row_max, scores.max(axis=1, keepdims=True))
        weights = [jnp.exp(scores - row_max) for scores, _ in blocks]
        row_sum = weights[0].sum(axis=1, keepdims=True)
        for w in weights[1:]:
            row_sum = row_sum + w.sum(axis=1, keepdims=True)
        inverse = 1.0 / row_sum
        total = None
        for w, (_, value) in zip(weights, blocks):
            probability = (w * inverse).astype(jnp.bfloat16)
            part = jnp.dot(probability, value, preferred_element_type=jnp.float32)
            total = part if total is None else total + part
        out_ref[pl.ds(frame * FRAME_TOK, FRAME_TOK), :] = total.astype(out_ref.dtype)


def attend(flag, qkv, halo):
    tokens, width = qkv.shape[1], qkv.shape[2]
    vmem = pl.BlockSpec(memory_space=pltpu.VMEM)
    return pl.pallas_call(
        attention_kernel,
        out_shape=jax.ShapeDtypeStruct((tokens, width), jnp.bfloat16),
        in_specs=[pl.BlockSpec(memory_space=pltpu.SMEM), vmem, vmem],
        out_specs=vmem,
    )(flag, qkv, halo)


def body(latents, projected, out_weight, gate_table, timesteps):
    row_count = latents.shape[0]
    frame_count = timesteps.shape[0]
    outer = lax.axis_size("fo")
    inner = lax.axis_size("fc")
    head_dim = projected.shape[2] // (outer * inner)
    shard = lax.axis_index("fo") * inner + lax.axis_index("fc")

    head_view = lax.all_to_all(projected, ("fo", "fc"), split_axis=2, concat_axis=0, tiled=True)
    qkv = jnp.transpose(head_view, (1, 0, 2))
    halo = passed_along(qkv[1:3, FRAME_TOK:], "tm", 1)
    flag = (lax.axis_index("tm") > 0).astype(jnp.int32).reshape(1)
    attended = attend(flag, qkv, halo)

    split = attended.reshape(outer, inner, row_count, head_dim)
    split = lax.all_to_all(split, "fc", split_axis=1, concat_axis=1, tiled=True)
    gathered = lax.all_gather(split, "fo", axis=0, tiled=False)
    columns = lax.all_gather(out_weight, "fc", axis=1, tiled=True)
    columns = columns.reshape(outer, inner, head_dim, columns.shape[1])
    partial = jnp.einsum(
        "aibrd,abdn->irn", gathered, columns, preferred_element_type=jnp.float32
    ).astype(jnp.bfloat16)
    returned = lax.all_to_all(partial, "fo", split_axis=0, concat_axis=0, tiled=True)
    branch = jnp.transpose(returned, (1, 0, 2)).reshape(row_count, -1)

    frame_index = (shard * row_count) // FRAME_TOK
    gate_row = gate_table[timesteps[frame_index]]
    updated = latents.astype(jnp.float32) + gate_row[None, :] * branch.astype(jnp.float32)
    return updated.astype(jnp.bfloat16)


def solution(mesh):
    tm_size, fsdp_size = mesh.devices.shape
    split_mesh = Mesh(mesh.devices.reshape(tm_size, fsdp_size // 2, 2), ("tm", "fo", "fc"))
    rows = ("tm", "fo", "fc")
    in_specs = (
        P(rows, None),
        P(rows, None, None),
        P(None, ("fo", "fc")),
        P(),
        P("tm"),
    )
    out_specs = P(rows, None)
    return jax.shard_map(
        body, mesh=split_mesh, in_specs=in_specs, out_specs=out_specs, check_vma=False
    )
```

time: 123 us -> 145 us (1.18)
  blocking collectives: 0 us -> 27.6 us
  waiting for transfers between devices: 54.7 us -> 75 us
  matrix products: 18.8 us -> 3.6 us
  starting transfers between devices: 17 us -> 5.36 us
  Pallas kernels: 0 us -> 4.58 us
  other arithmetic: 3.28 us -> 0.9 us
  loops' own time: 2.28 us -> 0 us
  between operations: 13.5 us -> 15.3 us
    all_gather x1 -> x2, waiting for transfers between devices: 15.7 us -> 61.5 us  [the longest x1 61.5 us: body(): gathered = lax.all_gather(split, 'fo', axis=0, tiled=False)]
    all_to_all x0 -> x2, blocking collectives: none -> 27.6 us  [the longest x1 22.1 us: body(): lax.all_to_all(projected, ('fo', 'fc'), split_axis=2, concat_axis=0, tile...]
    all_to_all x2 -> x1, waiting for transfers between devices: 22.7 us -> 5.42 us  [body(): lax.all_to_all(partial, 'fo', split_axis=0, concat_axis=0, tiled=True)]
    dot_general x7 -> x1, matrix products: 18.8 us -> 3.6 us  [body(): jnp.einsum('aibrd,abdn->irn', gathered, columns, preferred_element_type=j...]
    all_to_all x2 -> x1, starting transfers between devices: 15.7 us -> 3.58 us  [body(): lax.all_to_all(partial, 'fo', split_axis=0, concat_axis=0, tiled=True)]
    ppermute x1, waiting for transfers between devices: 15.6 us -> 7.38 us  [passed_along(): lax.ppermute(value, axis, [(source, source + steps) for source in range(i...]
    pallas_call x0 -> x1, Pallas kernels: none -> 4.58 us  [attend(): pl.pallas_call(attention_kernel, out_shape=jax.ShapeDtypeStruct((tokens,...]
    another operation x1 -> x0, loops' own time: 2.28 us -> none  [attend(): blocks = lax.map(frame_pair, jnp.arange(frame_count // 2, dtype=jnp.int32))]
  transfers between devices with their start and end apart: 4 -> 4, of which waited for: 4 -> 3; matrix products, arithmetic and copies ran while one was open for 20% -> 8% of each run, Pallas kernels for 0% -> 3%
where the time goes in v1:
time: 145 us; the launch traced here: 144 us
  waiting for transfers between devices  75 us (52%)
  blocking collectives  27.6 us (19%)
  between operations  15.3 us (11%)
  local copies, waits for them, and re-layouts  11.8 us (8%)
  starting transfers between devices  5.36 us (4%)
  Pallas kernels  4.58 us (3%)
  matrix products  3.6 us (2%)
    all_gather x1, waiting for transfers between devices, body(): gathered = lax.all_gather(split, 'fo', axis=0, tiled=False)  61.5 us
    all_to_all x1, blocking collectives, body(): lax.all_to_all(projected, ('fo', 'fc'), split_axis=2, concat_axis=0, tile...  22.1 us
    ppermute x1, waiting for transfers between devices, passed_along(): lax.ppermute(value, axis, [(source, source + steps) for source in range(i...  7.38 us
    unnamed x13, local copies, waits for them, and re-layouts  6.34 us
    all_to_all x1, blocking collectives, body(): split = lax.all_to_all(split, 'fc', split_axis=1, concat_axis=1, tiled=True)  5.49 us
    all_to_all x1, waiting for transfers between devices, body(): lax.all_to_all(partial, 'fo', split_axis=0, concat_axis=0, tiled=True)  5.42 us
    pallas_call x1, Pallas kernels, attend(): pl.pallas_call(attention_kernel, out_shape=jax.ShapeDtypeStruct((tokens,...  4.58 us
    dot_general x1, matrix products, body(): jnp.einsum('aibrd,abdn->irn', gathered, columns, preferred_element_type=j...  3.6 us
  transfers between devices with their start and end apart: 4, of which 3 were waited for; matrix products, arithmetic and copies ran while one was open for 8% of the time, Pallas kernels for 3%

profile of v1, /device:TPU:1, one launch (start us, length us, event | category | flops | bytes accessed | tf_op | source)
XLA Modules:
  0.0 144.1 jit_solution(1723013708941360081)
XLA Ops:
  6.5 0.0 copy-start
  6.5 0.0 all-gather.4.cloned.1.call-start
  6.5 0.7 all-gather.4.cloned.1.call-update
  7.3 0.0 all-gather.6.cloned.1.call-start
  7.3 2.9 %copy.12 = bf16[64,3,2048]{0,1,2:T(4,128)(2,1)S(1)} copy(bf16[64,3,2048]{2,0,1:T(8,128)(2,1)} %param.6) | data formatting | bytes 1572864 | tf_op args[1]
  10.2 1.5 %reshape.24 = bf16[16,2,12288]{2,1,0:T(2,128)(2,1)S(1)} reshape(bf16[2048,3,64]{2,1,0:T(4,128)(2,1)S(1)} %bitcast.31) | data formatting | bytes 1572864
  11.6 22.1 %all_to_all.28 = bf16[16,2,12288]{2,1,0:T(2,128)(2,1)S(1)} all-to-all(bf16[16,2,12288]{2,1,0:T(2,128)(2,1)S(1)} %reshape.24), channel_id=1, replica_groups=mesh['tm'=32,'fo'=8,'fc'=2] {'fo','fc'}, dimensions={0} | all-to-all | bytes 1572864 | tf_op jit(solution)/shard_map/all_to_all | solution.py:78
  33.8 1.3 reshape.25
  35.1 1.2 copy.13
  36.2 0.0 copy-start.1
  36.3 1.7 %collective-permute-start = (bf16[2,768,128]{2,1,0:T(8,128)(2,1)S(1)}, bf16[2,768,128]{2,1,0:T(8,128)(2,1)S(1)}, u32[]{:S(2)}, u32[]{:S(2)}) collective-permute-start(bf16[2,768,128]{2,1,0:T(8,128)(2,1)S(1)} %slice.4), channel_id=1, source_target_pairs={{0,16},{16,32},{32,48},{48,64},{64,80},{80,96},{96,112},{112,128},... | collective-permute-start | bytes 1179656 | tf_op jit(solution)/shard_map/ppermute | solution.py:16
  38.0 7.4 %collective-permute-done.halo_ref = bf16[2,768,128]{2,1,0:T(8,128)(2,1)S(1)} collective-permute-done((bf16[2,768,128]{2,1,0:T(8,128)(2,1)S(1)}, bf16[2,768,128]{2,1,0:T(8,128)(2,1)S(1)}, u32[]{:S(2)}, u32[]{:S(2)}) %collective-permute-start) | collective-permute-done | bytes 393248 | tf_op jit(solution)/shard_map/ppermute | solution.py:16
  45.4 0.0 copy-start.3
  45.4 0.0 copy-done.1
  45.4 0.7 copy-done.3
  46.2 4.6 %shard_map.55 = bf16[1024,128]{1,0:T(8,128)(2,1)} custom-call(s32[1]{0:T(128)} %bitcast.2.flag_ref, bf16[3,1024,128]{2,1,0:T(8,128)(2,1)} %bitcast.33, bf16[2,768,128]{2,1,0:T(8,128)(2,1)} %copy-done.3), custom_call_target="tpu_custom_call" | custom-call | tf_op jit(solution)/shard_map/pallas_call | solution.py:62
  50.7 1.0 copy.14
  51.7 5.5 %all_to_all.29 = bf16[8,2,64,128]{3,2,0,1:T(8,128)(2,1)S(1)} all-to-all(bf16[8,2,64,128]{3,2,0,1:T(8,128)(2,1)S(1)} %copy.14), channel_id=1, replica_groups=mesh['tm'=32,'fo'=8,'fc'=2] {'fc'}, dimensions={1} | all-to-all | bytes 524288 | tf_op jit(solution)/shard_map/all_to_all | solution.py:85
  57.2 0.7 copy.15
  57.9 0.0 all-gather.6.cloned.1.call-update
  57.9 0.0 all-gather.4.cloned.1.call-done
  58.0 1.9 %copy.16 = bf16[2048,384]{1,0:T(8,128)(2,1)S(1)} copy(bf16[2048,384]{0,1:T(8,128)(2,1)} %all-gather.4.cloned.1.call-done) | data formatting | bytes 3145728 | tf_op jit(solution)/shard_map/all_gather | solution.py:87
  59.9 61.5 %all-gather.6.cloned.1.call-done = bf16[64,2,64,128]{3,2,1,0:T(8,128)(2,1)} async-done(((bf16[8,2,64,128]{3,2,1,0:T(8,128)(2,1)}), bf16[64,2,64,128]{3,2,1,0:T(8,128)(2,1)}) %all-gather.6.cloned.1.call-update) | async-done | bytes 2097168 | tf_op jit(solution)/shard_map/all_gather | solution.py:86
  121.3 0.0 copy-start.4
  121.3 3.6 %fusion = bf16[8,64,384]{2,1,0:T(8,128)(2,1)} fusion(bf16[8,8,2,64,128]{4,3,2,1,0:T(8,128)(2,1)} %bitcast.38, bf16[8,2,128,384,1]{3,2,1,4,0:T(8,128)(2,1)S(1)} %bitcast.35), kind=kOutput, calls=%fused_computation.1 | convolution fusion | flops 805502976 | bytes 4063232 | tf_op jit(solution)/shard_map/aibrd,abdn->irn/dot_general | solution.py:89
  124.9 0.0 copy-start.2
  124.9 3.6 %all-to-all-start.2 = ((bf16[8,64,384]{2,1,0:T(8,128)(2,1)}), bf16[8,64,384]{2,1,0:T(8,128)(2,1)S(1)}, u32[]{:S(2)}, u32[]{:S(2)}) async-start(bf16[8,64,384]{2,1,0:T(8,128)(2,1)} %fusion), calls=%async_computation.2 | async-start | bytes 786432 | tf_op jit(solution)/shard_map/all_to_all | solution.py:92
  128.5 0.0 copy-done.4
  128.5 0.6 dynamic_slice.6
  130.8 0.0 copy-done
  130.8 5.4 %all-to-all-done.2 = bf16[8,64,384]{2,1,0:T(8,128)(2,1)S(1)} async-done(((bf16[8,64,384]{2,1,0:T(8,128)(2,1)}), bf16[8,64,384]{2,1,0:T(8,128)(2,1)S(1)}, u32[]{:S(2)}, u32[]{:S(2)}) %all-to-all-start.2) | async-done | bytes 393248 | tf_op jit(solution)/shard_map/all_to_all | solution.py:92
  136.3 0.1 convert_bitcast_fusion
  136.3 0.1 copy.20
  136.4 0.0 copy-done.2
  136.4 0.8 add_convert_fusion
  (2 shorter events, 0.0 us)
Async XLA Ops:
  6.5 124.3 %copy-start = (f32[40,3072]{1,0:T(8,128)S(1)}, f32[40,3072]{1,0:T(8,128)}, u32[]{:S(2)}) copy-start(f32[40,3072]{1,0:T(8,128)} %param.8) | copy-start | bytes 1474564
  6.5 51.4 %all-gather.4.cloned.1.call-start = ((), (), s32[]{:S(2)}) async-start(), calls=%async_computation.3 | async-start | bytes 2359296 | tf_op jit(solution)/shard_map/all_gather | solution.py:87
  7.3 114.0 %all-gather.6.cloned.1.call-start = ((), (), s32[]{:S(2)}) async-start(), calls=%async_computation.4 | async-start | bytes 2359296 | tf_op jit(solution)/shard_map/all_gather | solution.py:86
  36.2 9.2 %copy-start.1 = (bf16[64,3,16,128]{3,0,2,1:T(8,128)(2,1)}, bf16[64,3,16,128]{3,0,2,1:T(8,128)(2,1)S(1)}, u32[]{:S(2)}) copy-start(bf16[64,3,16,128]{3,0,2,1:T(8,128)(2,1)S(1)} %copy.13) | copy-start | bytes 2359300
  36.3 9.1 %collective-permute-start = (bf16[2,768,128]{2,1,0:T(8,128)(2,1)S(1)}, bf16[2,768,128]{2,1,0:T(8,128)(2,1)S(1)}, u32[]{:S(2)}, u32[]{:S(2)}) collective-permute-start(bf16[2,768,128]{2,1,0:T(8,128)(2,1)S(1)} %slice.4), channel_id=1, source_target_pairs={{0,16},{16,32},{32,48},{48,64},{64,80},{80,96},{96,112},{112,128},... | collective-permute-start | bytes 1179656 | tf_op jit(solution)/shard_map/ppermute | solution.py:16
  45.4 0.7 copy-start.3
  121.3 7.2 %copy-start.4 = (s32[4]{0:T(128)S(1)}, s32[4]{0:T(128)}, u32[]{:S(2)}) copy-start(s32[4]{0:T(128)} %param.9) | copy-start | bytes 52
  124.9 11.5 %copy-start.2 = (bf16[64,3072]{1,0:T(8,128)(2,1)S(1)}, bf16[64,3072]{1,0:T(8,128)(2,1)}, u32[]{:S(2)}) copy-start(bf16[64,3072]{1,0:T(8,128)(2,1)} %param.5) | copy-start | bytes 1179652
  124.9 11.4 %all-to-all-start.2 = ((bf16[8,64,384]{2,1,0:T(8,128)(2,1)}), bf16[8,64,384]{2,1,0:T(8,128)(2,1)S(1)}, u32[]{:S(2)}, u32[]{:S(2)}) async-start(bf16[8,64,384]{2,1,0:T(8,128)(2,1)} %fusion), calls=%async_computation.2 | async-start | bytes 786432 | tf_op jit(solution)/shard_map/all_to_all | solution.py:92
Sparse Core Ops, SparseCore 0:
  9.4 27.0 all-gather.3
  58.1 63.2 all-gather.5

commit v2 on v1

--- a/solution.py
+++ b/solution.py
@@ -67,29 +67,41 @@
     )(flag, qkv, halo)
 
 
+def shifted_copies(value, axis):
+    count = lax.axis_size(axis)
+    copies = [value]
+    for shift in range(1, count):
+        pairs = [(source, (source + shift) % count) for source in range(count)]
+        copies.append(lax.ppermute(value, axis, pairs))
+    return copies
+
+
 def body(latents, projected, out_weight, gate_table, timesteps):
     row_count = latents.shape[0]
-    frame_count = timesteps.shape[0]
-    outer = lax.axis_size("fo")
-    inner = lax.axis_size("fc")
+    outer = lax.axis_size("fy")
+    inner = lax.axis_size("fp")
     head_dim = projected.shape[2] // (outer * inner)
-    shard = lax.axis_index("fo") * inner + lax.axis_index("fc")
+    me_outer = lax.axis_index("fy")
+    shard = me_outer * inner + lax.axis_index("fp")
 
-    head_view = lax.all_to_all(projected, ("fo", "fc"), split_axis=2, concat_axis=0, tiled=True)
+    columns = lax.all_gather(out_weight, "fp", axis=1, tiled=True)
+    columns = columns.reshape(outer, inner, head_dim, columns.shape[1])
+
+    head_view = lax.all_to_all(projected, ("fy", "fp"), split_axis=2, concat_axis=0, tiled=True)
     qkv = jnp.transpose(head_view, (1, 0, 2))
     halo = passed_along(qkv[1:3, FRAME_TOK:], "tm", 1)
     flag = (lax.axis_index("tm") > 0).astype(jnp.int32).reshape(1)
     attended = attend(flag, qkv, halo)
 
     split = attended.reshape(outer, inner, row_count, head_dim)
-    split = lax.all_to_all(split, "fc", split_axis=1, concat_axis=1, tiled=True)
-    gathered = lax.all_gather(split, "fo", axis=0, tiled=False)
-    columns = lax.all_gather(out_weight, "fc", axis=1, tiled=True)
-    columns = columns.reshape(outer, inner, head_dim, columns.shape[1])
-    partial = jnp.einsum(
-        "aibrd,abdn->irn", gathered, columns, preferred_element_type=jnp.float32
-    ).astype(jnp.bfloat16)
-    returned = lax.all_to_all(partial, "fo", split_axis=0, concat_axis=0, tiled=True)
+    split = lax.all_to_all(split, "fp", split_axis=1, concat_axis=1, tiled=True)
+    total = None
+    for shift, part in enumerate(shifted_copies(split, "fy")):
+        source = (me_outer - shift) % outer
+        weight = lax.dynamic_index_in_dim(columns, source, 0, keepdims=False)
+        piece = jnp.einsum("ibrd,bdn->irn", part, weight, preferred_element_type=jnp.float32)
+        total = piece if total is None else total + piece
+    returned = lax.all_to_all(total.astype(jnp.bfloat16), "fy", split_axis=0, concat_axis=0, tiled=True)
     branch = jnp.transpose(returned, (1, 0, 2)).reshape(row_count, -1)
 
     frame_index = (shard * row_count) // FRAME_TOK
@@ -100,12 +112,12 @@
 
 def solution(mesh):
     tm_size, fsdp_size = mesh.devices.shape
-    split_mesh = Mesh(mesh.devices.reshape(tm_size, fsdp_size // 2, 2), ("tm", "fo", "fc"))
-    rows = ("tm", "fo", "fc")
+    split_mesh = Mesh(mesh.devices.reshape(tm_size, fsdp_size // 4, 4), ("tm", "fy", "fp"))
+    rows = ("tm", "fy", "fp")
     in_specs = (
         P(rows, None),
         P(rows, None, None),
-        P(None, ("fo", "fc")),
+        P(None, ("fy", "fp")),
         P(),
         P("tm"),
     )

time: 145 us -> 113 us (0.78)
  waiting for transfers between devices: 75 us -> 23.7 us
  starting transfers between devices: 5.36 us -> 15.3 us
  blocking collectives: 27.6 us -> 32.7 us
  local copies, waits for them, and re-layouts: 11.8 us -> 13.9 us
    all_gather x2 -> x1, waiting for transfers between devices: 61.5 us -> 0.02 us  [body(): columns = lax.all_gather(out_weight, 'fp', axis=1, tiled=True)]
    ppermute x0 -> x3, starting transfers between devices: none -> 10.1 us  [shifted_copies(): copies.append(lax.ppermute(value, axis, pairs))]
    ppermute x1, waiting for transfers between devices: 7.38 us -> 16.8 us  [passed_along(): lax.ppermute(value, axis, [(source, source + steps) for source in range(i...]
    all_to_all x2, blocking collectives: 27.6 us -> 32.7 us  [the longest x1 22.1 us: body(): lax.all_to_all(projected, ('fy', 'fp'), split_axis=2, concat_axis=0, tile...]
    reshape x0 -> x1, local copies, waits for them, and re-layouts: none -> 4.67 us  [body(): columns = columns.reshape(outer, inner, head_dim, columns.shape[1])]
    all_gather x1 -> x0, local copies, waits for them, and re-layouts: 1.88 us -> none  [body(): columns = lax.all_gather(out_weight, 'fc', axis=1, tiled=True)]
    dot_general x1 -> x4, matrix products: 3.6 us -> 4.65 us  [body(): jnp.einsum('ibrd,bdn->irn', part, weight, preferred_element_type=jnp.floa...]
    unnamed x13 -> x15, local copies, waits for them, and re-layouts: 6.34 us -> 6.35 us
  transfers between devices with their start and end apart: 4 -> 6, of which waited for: 3 -> 2; matrix products, arithmetic and copies ran while one was open for 8% -> 15% of each run, Pallas kernels for 3% -> 4%
where the time goes in v2:
time: 113 us; the launch traced here: 111 us
  blocking collectives  32.7 us (29%)
  waiting for transfers between devices  23.7 us (21%)
  between operations  15.7 us (14%)
  starting transfers between devices  15.3 us (14%)
  local copies, waits for them, and re-layouts  13.9 us (12%)
  matrix products  4.65 us (4%)
  Pallas kernels  4.56 us (4%)
    all_to_all x1, blocking collectives, body(): lax.all_to_all(projected, ('fy', 'fp'), split_axis=2, concat_axis=0, tile...  22.1 us
    ppermute x1, waiting for transfers between devices, passed_along(): lax.ppermute(value, axis, [(source, source + steps) for source in range(i...  16.8 us
    all_to_all x1, blocking collectives, body(): split = lax.all_to_all(split, 'fp', split_axis=1, concat_axis=1, tiled=True)  10.6 us
    ppermute x3, starting transfers between devices, shifted_copies(): copies.append(lax.ppermute(value, axis, pairs))  10.1 us
    unnamed x15, local copies, waits for them, and re-layouts  6.35 us
    all_to_all x1, waiting for transfers between devices, body(): lax.all_to_all(total.astype(jnp.bfloat16), 'fy', split_axis=0, concat_axi...  6.19 us
    reshape x1, local copies, waits for them, and re-layouts, body(): columns = columns.reshape(outer, inner, head_dim, columns.shape[1])  4.67 us
    dot_general x4, matrix products, body(): jnp.einsum('ibrd,bdn->irn', part, weight, preferred_element_type=jnp.floa...  4.65 us
  transfers between devices with their start and end apart: 6, of which 2 were waited for; matrix products, arithmetic and copies ran while one was open for 15% of the time, Pallas kernels for 4%

profile of v2, /device:TPU:1, one launch (start us, length us, event | category | flops | bytes accessed | tf_op | source)
XLA Modules:
  0.0 111.4 jit_solution(17020699171709134477)
XLA Ops:
  6.5 0.0 copy-start
  6.5 0.0 all-gather.2.cloned.1.call-start
  6.5 0.7 all-gather.2.cloned.1.call-update
  7.3 2.9 %copy.17 = bf16[64,3,2048]{0,1,2:T(4,128)(2,1)S(1)} copy(bf16[64,3,2048]{2,0,1:T(8,128)(2,1)} %param.6) | data formatting | bytes 1572864 | tf_op args[1]
  10.1 1.5 %reshape.29 = bf16[16,2,12288]{2,1,0:T(2,128)(2,1)S(1)} reshape(bf16[2048,3,64]{2,1,0:T(4,128)(2,1)S(1)} %bitcast.63) | data formatting | bytes 1572864
  11.6 22.1 %all_to_all.28 = bf16[16,2,12288]{2,1,0:T(2,128)(2,1)S(1)} all-to-all(bf16[16,2,12288]{2,1,0:T(2,128)(2,1)S(1)} %reshape.29), channel_id=1, replica_groups=mesh['tm'=32,'fy'=4,'fp'=4] {'fy','fp'}, dimensions={0} | all-to-all | bytes 1572864 | tf_op jit(solution)/shard_map/all_to_all | solution.py:90
  33.7 1.3 %reshape.30 = bf16[2048,3,64]{2,1,0:T(4,128)(2,1)S(1)} reshape(bf16[16,2,12288]{2,1,0:T(2,128)(2,1)S(1)} %all_to_all.28) | data formatting | bytes 1572864
  35.0 0.0 copy-start.5
  35.0 1.2 %copy.18 = bf16[64,3,16,128]{3,0,2,1:T(8,128)(2,1)S(1)} copy(bf16[64,3,16,128]{0,1,3,2:T(4,128)(2,1)S(1)} %bitcast.62) | data formatting | bytes 1572864 | tf_op jit(solution)/shard_map/all_to_all | solution.py:90
  36.2 0.0 copy-start.2
  36.3 1.7 %collective-permute-start = (bf16[2,768,128]{2,1,0:T(8,128)(2,1)S(1)}, bf16[2,768,128]{2,1,0:T(8,128)(2,1)S(1)}, u32[]{:S(2)}, u32[]{:S(2)}) collective-permute-start(bf16[2,768,128]{2,1,0:T(8,128)(2,1)S(1)} %slice.4), channel_id=1, source_target_pairs={{0,16},{16,32},{32,48},{48,64},{64,80},{80,96},{96,112},{112,128},... | collective-permute-start | bytes 1179656 | tf_op jit(solution)/shard_map/ppermute | solution.py:16
  38.0 16.8 %collective-permute-done.halo_ref = bf16[2,768,128]{2,1,0:T(8,128)(2,1)S(1)} collective-permute-done((bf16[2,768,128]{2,1,0:T(8,128)(2,1)S(1)}, bf16[2,768,128]{2,1,0:T(8,128)(2,1)S(1)}, u32[]{:S(2)}, u32[]{:S(2)}) %collective-permute-start) | collective-permute-done | bytes 393248 | tf_op jit(solution)/shard_map/ppermute | solution.py:16
  54.8 0.0 copy-start.4
  54.8 0.0 copy-done.2
  54.8 0.7 copy-done.4
  55.5 4.6 %shard_map.55 = bf16[1024,128]{1,0:T(8,128)(2,1)} custom-call(s32[1]{0:T(128)} %bitcast.2.flag_ref, bf16[3,1024,128]{2,1,0:T(8,128)(2,1)} %bitcast.65, bf16[2,768,128]{2,1,0:T(8,128)(2,1)} %copy-done.4), custom_call_target="tpu_custom_call" | custom-call | tf_op jit(solution)/shard_map/pallas_call | solution.py:62
  60.1 1.0 copy.19
  61.1 10.6 %all_to_all.29 = bf16[4,4,64,128]{3,2,0,1:T(8,128)(2,1)S(1)} all-to-all(bf16[4,4,64,128]{3,2,0,1:T(8,128)(2,1)S(1)} %copy.19), channel_id=1, replica_groups=mesh['tm'=32,'fy'=4,'fp'=4] {'fp'}, dimensions={1} | all-to-all | bytes 524288 | tf_op jit(solution)/shard_map/all_to_all | solution.py:97
  71.7 2.8 %collective-permute-start.1 = (bf16[4,4,64,128]{3,2,1,0:T(8,128)(2,1)S(1)}, bf16[4,4,64,128]{3,2,1,0:T(8,128)(2,1)S(1)}, u32[]{:S(2)}, u32[]{:S(2)}) collective-permute-start(bf16[4,4,64,128]{3,2,1,0:T(8,128)(2,1)S(1)} %copy.22), channel_id=1, source_target_pairs={{0,4},{4,8},{8,12},{12,0},{1,5},{5,9},{9,13},{13,1},{2,6},{6,10},{... | collective-permute-start | bytes 786440 | tf_op jit(solution)/shard_map/ppermute | solution.py:75
  74.5 4.3 %collective-permute-start.2 = (bf16[4,4,64,128]{3,2,1,0:T(8,128)(2,1)S(1)}, bf16[4,4,64,128]{3,2,1,0:T(8,128)(2,1)S(1)}, u32[]{:S(2)}, u32[]{:S(2)}) collective-permute-start(bf16[4,4,64,128]{3,2,1,0:T(8,128)(2,1)S(1)} %copy.22), channel_id=1, source_target_pairs={{0,8},{4,12},{8,0},{12,4},{1,9},{5,13},{9,1},{13,5},{2,10},{6,14},... | collective-permute-start | bytes 786440 | tf_op jit(solution)/shard_map/ppermute | solution.py:75
  78.9 0.0 copy-done.5
  79.0 0.6 dynamic_slice.19
  81.5 3.0 %collective-permute-start.3 = (bf16[4,4,64,128]{3,2,1,0:T(8,128)(2,1)S(1)}, bf16[4,4,64,128]{3,2,1,0:T(8,128)(2,1)S(1)}, u32[]{:S(2)}, u32[]{:S(2)}) collective-permute-start(bf16[4,4,64,128]{3,2,1,0:T(8,128)(2,1)S(1)} %copy.22), channel_id=1, source_target_pairs={{0,12},{4,0},{8,4},{12,8},{1,13},{5,1},{9,5},{13,9},{2,14},{6,2},{... | collective-permute-start | bytes 786440 | tf_op jit(solution)/shard_map/ppermute | solution.py:75
  84.5 0.0 all-gather.2.cloned.1.call-done
  84.5 4.7 %copy.34 = bf16[2048,768]{1,0:T(8,128)(2,1)} copy(bf16[2048,768]{0,1:T(8,128)(2,1)} %all-gather.2.cloned.1.call-done) | data formatting | bytes 6291456 | tf_op jit(solution)/shard_map/reshape | solution.py:88
  89.2 0.0 copy-start.1
  89.2 0.0 collective-permute-done.1
  89.2 1.6 %convolution_bitcast_fusion.2 = f32[4,64,768]{2,1,0:T(8,128)S(1)} fusion(bf16[4,4,64,128]{3,2,1,0:T(8,128)(2,1)S(1)} %collective-permute-done.1, bf16[4,4,128,768]{3,2,1,0:T(8,128)(2,1)} %bitcast.58, s32[]{:T(128)S(6)} %select_n.48), kind=kOutput, calls=%fused_computation.2 | convolution fusion | flops 201326592 | bytes 1835012 | tf_op jit(solution)/shard_map/ibrd,bdn->irn/dot_general | solution.py:102
  90.8 0.0 collective-permute-done.2
  90.9 1.5 %convolution_bitcast_fusion.1 = f32[4,64,768]{2,1,0:T(8,128)S(1)} fusion(bf16[4,4,64,128]{3,2,1,0:T(8,128)(2,1)S(1)} %collective-permute-done.2, bf16[4,4,128,768]{3,2,1,0:T(8,128)(2,1)} %bitcast.59, s32[]{:T(128)S(6)} %select_n.50), kind=kOutput, calls=%fused_computation.1 | convolution fusion | flops 201326592 | bytes 1835012 | tf_op jit(solution)/shard_map/ibrd,bdn->irn/dot_general | solution.py:102
  92.4 0.0 collective-permute-done.3
  92.4 0.0 copy-done.1
  92.4 0.4 convolution_bitcast_fusion
  92.8 0.0 copy-start.3
  92.8 1.1 %fusion.3 = bf16[4,64,768]{2,1,0:T(8,128)(2,1)} fusion(f32[4,64,768]{2,1,0:T(8,128)S(1)} %convolution_bitcast_fusion, f32[4,64,768]{2,1,0:T(8,128)S(1)} %convolution_bitcast_fusion.1, f32[4,64,768]{2,1,0:T(8,128)S(1)} %convolution_bitcast_fusion.2, bf16[4,4,64,128]{3,2,0,1:T(8,128)(2,1)S(1)} %all_to_all.29, bf16[4,4,128,768]{3,2,1,0:T(8,128)(2,1)S(1)} %bitcast.61, ...), kind=kOutput, calls=%fused_computation.7 | convolution fusion | flops 202113024 | bytes 3801092 | tf_op jit(solution)/shard_map/ibrd,bdn->irn/dot_general | solution.py:102
  93.9 3.5 %all-to-all-start.2 = ((bf16[4,64,768]{2,1,0:T(8,128)(2,1)}), bf16[4,64,768]{2,1,0:T(8,128)(2,1)S(1)}, u32[]{:S(2)}, u32[]{:S(2)}) async-start(bf16[4,64,768]{2,1,0:T(8,128)(2,1)} %fusion.3), calls=%async_computation.2 | async-start | bytes 786432 | tf_op jit(solution)/shard_map/all_to_all | solution.py:104
  97.4 0.0 copy-done
  97.4 6.2 %all-to-all-done.2 = bf16[4,64,768]{2,1,0:T(8,128)(2,1)S(1)} async-done(((bf16[4,64,768]{2,1,0:T(8,128)(2,1)}), bf16[4,64,768]{2,1,0:T(8,128)(2,1)S(1)}, u32[]{:S(2)}, u32[]{:S(2)}) %all-to-all-start.2) | async-done | bytes 393248 | tf_op jit(solution)/shard_map/all_to_all | solution.py:104
  103.6 0.1 convert_bitcast_fusion
  103.7 0.1 copy.35
  103.7 0.0 copy-done.3
  103.8 0.8 add_convert_fusion
  (3 shorter events, 0.1 us)
Async XLA Ops:
  6.5 90.9 %copy-start = (f32[40,3072]{1,0:T(8,128)S(1)}, f32[40,3072]{1,0:T(8,128)}, u32[]{:S(2)}) copy-start(f32[40,3072]{1,0:T(8,128)} %param.8) | copy-start | bytes 1474564
  6.5 78.0 %all-gather.2.cloned.1.call-start = ((), (), s32[]{:S(2)}) async-start(), calls=%async_computation.3 | async-start | bytes 3932160 | tf_op jit(solution)/shard_map/all_gather | solution.py:87
  35.0 43.9 %copy-start.5 = (s32[4]{0:T(128)S(1)}, s32[4]{0:T(128)}, u32[]{:S(2)}) copy-start(s32[4]{0:T(128)} %param.9) | copy-start | bytes 52
  36.2 18.6 %copy-start.2 = (bf16[64,3,16,128]{3,0,2,1:T(8,128)(2,1)}, bf16[64,3,16,128]{3,0,2,1:T(8,128)(2,1)S(1)}, u32[]{:S(2)}) copy-start(bf16[64,3,16,128]{3,0,2,1:T(8,128)(2,1)S(1)} %copy.18) | copy-start | bytes 2359300
  36.3 18.5 %collective-permute-start = (bf16[2,768,128]{2,1,0:T(8,128)(2,1)S(1)}, bf16[2,768,128]{2,1,0:T(8,128)(2,1)S(1)}, u32[]{:S(2)}, u32[]{:S(2)}) collective-permute-start(bf16[2,768,128]{2,1,0:T(8,128)(2,1)S(1)} %slice.4), channel_id=1, source_target_pairs={{0,16},{16,32},{32,48},{48,64},{64,80},{80,96},{96,112},{112,128},... | collective-permute-start | bytes 1179656 | tf_op jit(solution)/shard_map/ppermute | solution.py:16
  54.8 0.7 copy-start.4
  71.7 17.5 %collective-permute-start.1 = (bf16[4,4,64,128]{3,2,1,0:T(8,128)(2,1)S(1)}, bf16[4,4,64,128]{3,2,1,0:T(8,128)(2,1)S(1)}, u32[]{:S(2)}, u32[]{:S(2)}) collective-permute-start(bf16[4,4,64,128]{3,2,1,0:T(8,128)(2,1)S(1)} %copy.22), channel_id=1, source_target_pairs={{0,4},{4,8},{8,12},{12,0},{1,5},{5,9},{9,13},{13,1},{2,6},{6,10},{... | collective-permute-start | bytes 786440 | tf_op jit(solution)/shard_map/ppermute | solution.py:75
  74.5 16.3 %collective-permute-start.2 = (bf16[4,4,64,128]{3,2,1,0:T(8,128)(2,1)S(1)}, bf16[4,4,64,128]{3,2,1,0:T(8,128)(2,1)S(1)}, u32[]{:S(2)}, u32[]{:S(2)}) collective-permute-start(bf16[4,4,64,128]{3,2,1,0:T(8,128)(2,1)S(1)} %copy.22), channel_id=1, source_target_pairs={{0,8},{4,12},{8,0},{12,4},{1,9},{5,13},{9,1},{13,5},{2,10},{6,14},... | collective-permute-start | bytes 786440 | tf_op jit(solution)/shard_map/ppermute | solution.py:75
  81.5 10.9 %collective-permute-start.3 = (bf16[4,4,64,128]{3,2,1,0:T(8,128)(2,1)S(1)}, bf16[4,4,64,128]{3,2,1,0:T(8,128)(2,1)S(1)}, u32[]{:S(2)}, u32[]{:S(2)}) collective-permute-start(bf16[4,4,64,128]{3,2,1,0:T(8,128)(2,1)S(1)} %copy.22), channel_id=1, source_target_pairs={{0,12},{4,0},{8,4},{12,8},{1,13},{5,1},{9,5},{13,9},{2,14},{6,2},{... | collective-permute-start | bytes 786440 | tf_op jit(solution)/shard_map/ppermute | solution.py:75
  89.2 3.2 %copy-start.1 = (bf16[2048,768]{1,0:T(8,128)(2,1)S(1)}, bf16[2048,768]{1,0:T(8,128)(2,1)}, u32[]{:S(2)}) copy-start(bf16[2048,768]{1,0:T(8,128)(2,1)} %copy.34) | copy-start | bytes 9437188
  92.8 11.0 %copy-start.3 = (bf16[64,3072]{1,0:T(8,128)(2,1)S(1)}, bf16[64,3072]{1,0:T(8,128)(2,1)}, u32[]{:S(2)}) copy-start(bf16[64,3072]{1,0:T(8,128)(2,1)} %param.5) | copy-start | bytes 1179652
  93.9 9.7 %all-to-all-start.2 = ((bf16[4,64,768]{2,1,0:T(8,128)(2,1)}), bf16[4,64,768]{2,1,0:T(8,128)(2,1)S(1)}, u32[]{:S(2)}, u32[]{:S(2)}) async-start(bf16[4,64,768]{2,1,0:T(8,128)(2,1)} %fusion.3), calls=%async_computation.2 | async-start | bytes 786432 | tf_op jit(solution)/shard_map/all_to_all | solution.py:104
Sparse Core Ops, SparseCore 0:
  9.5 61.2 all-gather.1

commit v3 on v2

v3 whole, which is shorter than its diff:
```python
import jax
import jax.numpy as jnp
from jax import lax
from jax.experimental import pallas as pl
from jax.experimental.pallas import tpu as pltpu
from jax.sharding import Mesh
from jax.sharding import PartitionSpec as P

FRAME_TOK = 256
WINDOW = 4


def passed_along(value, axis, steps):
    count = lax.axis_size(axis)
    initial, last = (max(0, -steps), min(count, count - steps))
    return lax.ppermute(value, axis, [(source, source + steps) for source in range(initial, last)])


def attention_kernel(flag_ref, qkv_ref, halo_ref, out_ref):
    row_count = qkv_ref.shape[2]
    per_frame = FRAME_TOK // row_count
    frame_count = qkv_ref.shape[0] // per_frame
    score_scale = qkv_ref.shape[3] ** (-0.5)
    outer, inner = out_ref.shape[0] // out_ref.shape[1], out_ref.shape[1]
    has_prev = flag_ref[0] > 0

    def frame_rows(ref, block, plane):
        return ref[pl.ds(block, per_frame), plane].reshape(FRAME_TOK, ref.shape[3])

    for frame in range(frame_count):
        query = frame_rows(qkv_ref, frame * per_frame, 0)
        blocks = []
        for back in range(WINDOW):
            source = frame - (WINDOW - 1) + back
            if source >= 0:
                key = frame_rows(qkv_ref, source * per_frame, 1)
                value = frame_rows(qkv_ref, source * per_frame, 2)
            else:
                block = (source + WINDOW - 1) * per_frame
                key, value = frame_rows(halo_ref, block, 0), frame_rows(halo_ref, block, 1)
            scores = (
                lax.dot_general(
                    query, key, (((1,), (1,)), ((), ())), preferred_element_type=jnp.float32
                )
                * score_scale
            )
            if source < 0:
                scores = jnp.where(has_prev, scores, -1e30)
            blocks.append((scores, value))
        row_max = blocks[0][0].max(axis=1, keepdims=True)
        for scores, _ in blocks[1:]:
            row_max = jnp.maximum(row_max, scores.max(axis=1, keepdims=True))
        weights = [jnp.exp(scores - row_max) for scores, _ in blocks]
        row_sum = weights[0].sum(axis=1, keepdims=True)
        for w in weights[1:]:
            row_sum = row_sum + w.sum(axis=1, keepdims=True)
        inverse = 1.0 / row_sum
        total = None
        for w, (_, value) in zip(weights, blocks):
            probability = (w * inverse).astype(jnp.bfloat16)
            part = jnp.dot(probability, value, preferred_element_type=jnp.float32)
            total = part if total is None else total + part
        total = total.astype(out_ref.dtype)
        for piece in range(per_frame):
            row_outer, row_inner = divmod(frame * per_frame + piece, inner)
            rows = total[piece * row_count : (piece + 1) * row_count]
            for dest_outer in range(outer):
                out_ref[dest_outer * inner + row_inner, row_outer] = rows


def attend(flag, qkv, halo, outer, inner):
    row_count, width = qkv.shape[2], qkv.shape[3]
    vmem = pl.BlockSpec(memory_space=pltpu.VMEM)
    return pl.pallas_call(
        attention_kernel,
        out_shape=jax.ShapeDtypeStruct((outer * inner, outer, row_count, width), jnp.bfloat16),
        in_specs=[pl.BlockSpec(memory_space=pltpu.SMEM), vmem, vmem],
        out_specs=vmem,
    )(flag, qkv, halo)


def chunk_kernel(rows_ref, out_ref):
    width = out_ref.shape[3]
    for head in range(out_ref.shape[0]):
        out_ref[head] = rows_ref[:, :, head * width : (head + 1) * width]


def head_chunks(planes, heads):
    lanes, row_count, features = planes.shape
    vmem = pl.BlockSpec(memory_space=pltpu.VMEM)
    return pl.pallas_call(
        chunk_kernel,
        out_shape=jax.ShapeDtypeStruct((heads, lanes, row_count, features // heads), planes.dtype),
        in_specs=[vmem],
        out_specs=vmem,
    )(planes)


def body(latents, projected, out_weight, gate_table, timesteps):
    row_count = latents.shape[0]
    outer = lax.axis_size("fy")
    inner = lax.axis_size("fp")
    heads = outer * inner
    head_dim = projected.shape[2] // heads
    per_frame = FRAME_TOK // row_count
    shard = lax.axis_index("fy") * inner + lax.axis_index("fp")

    columns = lax.all_gather(out_weight, "fp", axis=1, tiled=True)
    columns = columns.reshape(heads, head_dim, columns.shape[1])

    chunks = head_chunks(jnp.transpose(projected, (1, 0, 2)), heads)
    qkv = lax.all_to_all(chunks, ("fy", "fp"), split_axis=0, concat_axis=0, tiled=True)
    halo = passed_along(qkv[per_frame:, 1:3], "tm", 1)
    flag = (lax.axis_index("tm") > 0).astype(jnp.int32).reshape(1)
    spread = attend(flag, qkv, halo, outer, inner)

    gathered = lax.all_to_all(spread, ("fy", "fp"), split_axis=0, concat_axis=0, tiled=True)
    total = jnp.einsum("jird,jdn->irn", gathered, columns, preferred_element_type=jnp.float32)
    returned = lax.all_to_all(total.astype(jnp.bfloat16), "fy", split_axis=0, concat_axis=0, tiled=True)
    branch = jnp.transpose(returned, (1, 0, 2)).reshape(row_count, -1)

    frame_index = (shard * row_count) // FRAME_TOK
    gate_row = gate_table[timesteps[frame_index]]
    updated = latents.astype(jnp.float32) + gate_row[None, :] * branch.astype(jnp.float32)
    return updated.astype(jnp.bfloat16)


def solution(mesh):
    tm_size, fsdp_size = mesh.devices.shape
    split_mesh = Mesh(mesh.devices.reshape(tm_size, fsdp_size // 4, 4), ("tm", "fy", "fp"))
    rows = ("tm", "fy", "fp")
    in_specs = (
        P(rows, None),
        P(rows, None, None),
        P(None, ("fy", "fp")),
        P(),
        P("tm"),
    )
    out_specs = P(rows, None)
    return jax.shard_map(
        body, mesh=split_mesh, in_specs=in_specs, out_specs=out_specs, check_vma=False
    )
```

time: 113 us -> 104 us (0.920); the launches traced: 111 us -> 104 us
  waiting for transfers between devices: 23.7 us -> 37.6 us
  blocking collectives: 32.7 us -> 23.2 us
  local copies, waits for them, and re-layouts: 13.9 us -> 6.11 us
  starting transfers between devices: 15.3 us -> 9.99 us
  Pallas kernels: 4.56 us -> 7.02 us
    all_gather x1, waiting for transfers between devices: 0.02 us -> 11.3 us  [body(): columns = lax.all_gather(out_weight, 'fp', axis=1, tiled=True)]
    ppermute x3 -> x0, starting transfers between devices: 10.1 us -> none  [shifted_copies(): copies.append(lax.ppermute(value, axis, pairs))]
    all_to_all x2 -> x1, blocking collectives: 32.7 us -> 23.2 us  [body(): lax.all_to_all(chunks, ('fy', 'fp'), split_axis=0, concat_axis=0, tiled=T...]
    reshape x2 -> x0, local copies, waits for them, and re-layouts: 5.64 us -> none  [the longest x1 4.67 us: body(): columns = columns.reshape(outer, inner, head_dim, columns.shape[1])]
    unnamed x15 -> x10, local copies, waits for them, and re-layouts: 6.35 us -> 0.76 us
    all_to_all x0 -> x1, starting transfers between devices: none -> 5.08 us  [body(): lax.all_to_all(spread, ('fy', 'fp'), split_axis=0, concat_axis=0, tiled=T...]
    all_gather x0 -> x1, local copies, waits for them, and re-layouts: none -> 4.66 us  [body(): columns = lax.all_gather(out_weight, 'fp', axis=1, tiled=True)]
    pallas_call x1 -> x2, Pallas kernels: 4.56 us -> 7.02 us  [the longest x1 4.85 us: attend(): pl.pallas_call(attention_kernel, out_shape=jax.ShapeDtypeStruct((outer *...]
  transfers between devices with their start and end apart: 6 -> 4, of which waited for: 2 -> 4; matrix products, arithmetic and copies ran while one was open for 15% -> 5% of each run, Pallas kernels for 4% -> 7%
where the time goes in v3:
time: 104 us
  waiting for transfers between devices  37.6 us (36%)
  blocking collectives  23.2 us (22%)
  between operations  15.4 us (15%)
  starting transfers between devices  9.99 us (10%)
  Pallas kernels  7.02 us (7%)
  local copies, waits for them, and re-layouts  6.11 us (6%)
  matrix products  3.61 us (3%)
    all_to_all x1, blocking collectives, body(): lax.all_to_all(chunks, ('fy', 'fp'), split_axis=0, concat_axis=0, tiled=T...  23.2 us
    ppermute x1, waiting for transfers between devices, passed_along(): lax.ppermute(value, axis, [(source, source + steps) for source in range(i...  16.4 us
    all_gather x1, waiting for transfers between devices, body(): columns = lax.all_gather(out_weight, 'fp', axis=1, tiled=True)  11.3 us
    all_to_all x1, waiting for transfers between devices, body(): lax.all_to_all(total.astype(jnp.bfloat16), 'fy', split_axis=0, concat_axi...  7.52 us
    all_to_all x1, starting transfers between devices, body(): lax.all_to_all(spread, ('fy', 'fp'), split_axis=0, concat_axis=0, tiled=T...  5.08 us
    pallas_call x1, Pallas kernels, attend(): pl.pallas_call(attention_kernel, out_shape=jax.ShapeDtypeStruct((outer *...  4.85 us
    all_gather x1, local copies, waits for them, and re-layouts, body(): columns = lax.all_gather(out_weight, 'fp', axis=1, tiled=True)  4.66 us
    dot_general x1, matrix products, body(): jnp.einsum('jird,jdn->irn', gathered, columns, preferred_element_type=jnp...  3.61 us
  transfers between devices with their start and end apart: 4, of which 4 were waited for; matrix products, arithmetic and copies ran while one was open for 5% of the time, Pallas kernels for 7%

profile of v3, /device:TPU:1, one launch (start us, length us, event | category | flops | bytes accessed | tf_op | source)
XLA Modules:
  0.0 103.9 jit_solution(689124172704893290)
XLA Ops:
  6.5 0.0 copy-start
  6.5 0.0 all-gather.2.cloned.1.call-start
  6.5 0.7 all-gather.2.cloned.1.call-update
  7.3 2.2 %shard_map.55 = bf16[16,3,64,128]{3,2,1,0:T(8,128)(2,1)} custom-call(bf16[3,64,2048]{2,1,0:T(8,128)(2,1)} %bitcast.21), custom_call_target="tpu_custom_call" | custom-call | tf_op jit(solution)/shard_map/pallas_call | solution.py:91
  9.4 0.0 copy-start.4
  9.4 23.2 %all_to_all.15.qkv_ref = bf16[16,3,64,128]{3,2,1,0:T(8,128)(2,1)S(1)} all-to-all(bf16[16,3,64,128]{3,2,1,0:T(8,128)(2,1)} %shard_map.55), channel_id=1, replica_groups=mesh['tm'=32,'fy'=4,'fp'=4] {'fy','fp'}, dimensions={0} | all-to-all | bytes 1572864 | tf_op jit(solution)/shard_map/all_to_all | solution.py:112
  32.7 0.0 copy-start.1
  32.7 1.3 %collective-permute-start = (bf16[12,2,64,128]{3,2,1,0:T(8,128)(2,1)S(1)}, bf16[12,2,64,128]{3,2,1,0:T(8,128)(2,1)S(1)}, u32[]{:S(2)}, u32[]{:S(2)}) collective-permute-start(bf16[12,2,64,128]{3,2,1,0:T(8,128)(2,1)S(1)} %slice.4), channel_id=1, source_target_pairs={{0,16},{16,32},{32,48},{48,64},{64,80},{80,96},{96,112},{112,128},... | collective-permute-start | bytes 1179656 | tf_op jit(solution)/shard_map/ppermute | solution.py:16
  34.0 16.4 %collective-permute-done.halo_ref = bf16[12,2,64,128]{3,2,1,0:T(8,128)(2,1)S(1)} collective-permute-done((bf16[12,2,64,128]{3,2,1,0:T(8,128)(2,1)S(1)}, bf16[12,2,64,128]{3,2,1,0:T(8,128)(2,1)S(1)}, u32[]{:S(2)}, u32[]{:S(2)}) %collective-permute-start) | collective-permute-done | bytes 393248 | tf_op jit(solution)/shard_map/ppermute | solution.py:16
  50.5 0.0 copy-start.2
  50.5 0.0 copy-done.1
  50.5 0.7 copy-done.2
  51.2 4.8 %shard_map.56 = bf16[16,4,64,128]{3,2,1,0:T(8,128)(2,1)} custom-call(s32[1]{0:T(128)} %bitcast.2.flag_ref, bf16[16,3,64,128]{3,2,1,0:T(8,128)(2,1)} %copy-done.1, bf16[12,2,64,128]{3,2,1,0:T(8,128)(2,1)} %copy-done.2), custom_call_target="tpu_custom_call" | custom-call | tf_op jit(solution)/shard_map/pallas_call | solution.py:74
  56.1 5.1 %all-to-all-start.1 = ((bf16[16,4,64,128]{3,2,1,0:T(8,128)(2,1)}), bf16[16,4,64,128]{3,2,1,0:T(8,128)(2,1)S(1)}, u32[]{:S(2)}, u32[]{:S(2)}) async-start(bf16[16,4,64,128]{3,2,1,0:T(8,128)(2,1)} %shard_map.56), calls=%async_computation.1 | async-start | bytes 2097152 | tf_op jit(solution)/shard_map/all_to_all | solution.py:117
  61.1 0.0 copy-done.4
  61.1 0.6 dynamic_slice.6
  63.7 11.3 %all-gather.2.cloned.1.call-done = bf16[2048,768]{0,1:T(8,128)(2,1)} async-done(((bf16[2048,192]{0,1:T(8,128)(2,1)}), bf16[2048,768]{0,1:T(8,128)(2,1)}) %all-gather.2.cloned.1.call-update) | async-done | bytes 3145744 | tf_op jit(solution)/shard_map/all_gather | solution.py:108
  75.0 4.7 %copy.8 = bf16[2048,768]{1,0:T(8,128)(2,1)} copy(bf16[2048,768]{0,1:T(8,128)(2,1)} %all-gather.2.cloned.1.call-done) | data formatting | bytes 6291456 | tf_op jit(solution)/shard_map/all_gather | solution.py:108
  79.7 1.6 %all-to-all-done.1 = bf16[16,4,64,128]{3,2,1,0:T(8,128)(2,1)S(1)} async-done(((bf16[16,4,64,128]{3,2,1,0:T(8,128)(2,1)}), bf16[16,4,64,128]{3,2,1,0:T(8,128)(2,1)S(1)}, u32[]{:S(2)}, u32[]{:S(2)}) %all-to-all-start.1) | async-done | bytes 1048608 | tf_op jit(solution)/shard_map/all_to_all | solution.py:117
  81.3 3.6 %fusion = bf16[4,64,768]{2,1,0:T(8,128)(2,1)} fusion(bf16[16,4,64,128]{3,2,1,0:T(8,128)(2,1)S(1)} %all-to-all-done.1, bf16[16,128,768,1]{2,1,3,0:T(8,128)(2,1)} %bitcast.19), kind=kOutput, calls=%fused_computation.1 | convolution fusion | flops 805502976 | bytes 4587520 | tf_op jit(solution)/shard_map/jird,jdn->irn/dot_general | solution.py:118
  84.9 0.0 copy-start.3
  84.9 3.6 %all-to-all-start.2 = ((bf16[4,64,768]{2,1,0:T(8,128)(2,1)}), bf16[4,64,768]{2,1,0:T(8,128)(2,1)S(1)}, u32[]{:S(2)}, u32[]{:S(2)}) async-start(bf16[4,64,768]{2,1,0:T(8,128)(2,1)} %fusion), calls=%async_computation.2 | async-start | bytes 786432 | tf_op jit(solution)/shard_map/all_to_all | solution.py:119
  88.5 0.0 copy-done
  88.5 7.5 %all-to-all-done.2 = bf16[4,64,768]{2,1,0:T(8,128)(2,1)S(1)} async-done(((bf16[4,64,768]{2,1,0:T(8,128)(2,1)}), bf16[4,64,768]{2,1,0:T(8,128)(2,1)S(1)}, u32[]{:S(2)}, u32[]{:S(2)}) %all-to-all-start.2) | async-done | bytes 393248 | tf_op jit(solution)/shard_map/all_to_all | solution.py:119
  96.0 0.1 convert_bitcast_fusion
  96.1 0.1 copy.13
  96.2 0.0 copy-done.3
  96.2 0.8 add_convert_fusion
  (2 shorter events, 0.0 us)
Async XLA Ops:
  6.5 81.9 %copy-start = (f32[40,3072]{1,0:T(8,128)S(1)}, f32[40,3072]{1,0:T(8,128)}, u32[]{:S(2)}) copy-start(f32[40,3072]{1,0:T(8,128)} %param.8) | copy-start | bytes 1474564
  6.5 68.5 %all-gather.2.cloned.1.call-start = ((), (), s32[]{:S(2)}) async-start(), calls=%async_computation.3 | async-start | bytes 3932160 | tf_op jit(solution)/shard_map/all_gather | solution.py:108
  9.4 51.7 %copy-start.4 = (s32[4]{0:T(128)S(1)}, s32[4]{0:T(128)}, u32[]{:S(2)}) copy-start(s32[4]{0:T(128)} %param.9) | copy-start | bytes 52
  32.7 17.8 %copy-start.1 = (bf16[16,3,64,128]{3,2,1,0:T(8,128)(2,1)}, bf16[16,3,64,128]{3,2,1,0:T(8,128)(2,1)S(1)}, u32[]{:S(2)}) copy-start(bf16[16,3,64,128]{3,2,1,0:T(8,128)(2,1)S(1)} %all_to_all.15.qkv_ref) | copy-start | bytes 2359300
  32.7 17.7 %collective-permute-start = (bf16[12,2,64,128]{3,2,1,0:T(8,128)(2,1)S(1)}, bf16[12,2,64,128]{3,2,1,0:T(8,128)(2,1)S(1)}, u32[]{:S(2)}, u32[]{:S(2)}) collective-permute-start(bf16[12,2,64,128]{3,2,1,0:T(8,128)(2,1)S(1)} %slice.4), channel_id=1, source_target_pairs={{0,16},{16,32},{32,48},{48,64},{64,80},{80,96},{96,112},{112,128},... | collective-permute-start | bytes 1179656 | tf_op jit(solution)/shard_map/ppermute | solution.py:16
  50.5 0.7 copy-start.2
  56.1 25.2 %all-to-all-start.1 = ((bf16[16,4,64,128]{3,2,1,0:T(8,128)(2,1)}), bf16[16,4,64,128]{3,2,1,0:T(8,128)(2,1)S(1)}, u32[]{:S(2)}, u32[]{:S(2)}) async-start(bf16[16,4,64,128]{3,2,1,0:T(8,128)(2,1)} %shard_map.56), calls=%async_computation.1 | async-start | bytes 2097152 | tf_op jit(solution)/shard_map/all_to_all | solution.py:117
  84.9 11.3 %copy-start.3 = (bf16[64,3072]{1,0:T(8,128)(2,1)S(1)}, bf16[64,3072]{1,0:T(8,128)(2,1)}, u32[]{:S(2)}) copy-start(bf16[64,3072]{1,0:T(8,128)(2,1)} %param.5) | copy-start | bytes 1179652
  84.9 11.2 %all-to-all-start.2 = ((bf16[4,64,768]{2,1,0:T(8,128)(2,1)}), bf16[4,64,768]{2,1,0:T(8,128)(2,1)S(1)}, u32[]{:S(2)}, u32[]{:S(2)}) async-start(bf16[4,64,768]{2,1,0:T(8,128)(2,1)} %fusion), calls=%async_computation.2 | async-start | bytes 786432 | tf_op jit(solution)/shard_map/all_to_all | solution.py:119
Sparse Core Ops, SparseCore 0:
  9.5 65.5 all-gather.1

commit v4 on v3

--- a/solution.py
+++ b/solution.py
@@ -21,7 +21,7 @@
     per_frame = FRAME_TOK // row_count
     frame_count = qkv_ref.shape[0] // per_frame
     score_scale = qkv_ref.shape[3] ** (-0.5)
-    outer, inner = out_ref.shape[0] // out_ref.shape[1], out_ref.shape[1]
+    inner = out_ref.shape[0] // frame_count
     has_prev = flag_ref[0] > 0
 
     def frame_rows(ref, block, plane):
@@ -61,19 +61,16 @@
             part = jnp.dot(probability, value, preferred_element_type=jnp.float32)
             total = part if total is None else total + part
         total = total.astype(out_ref.dtype)
-        for piece in range(per_frame):
-            row_outer, row_inner = divmod(frame * per_frame + piece, inner)
-            rows = total[piece * row_count : (piece + 1) * row_count]
-            for dest_outer in range(outer):
-                out_ref[dest_outer * inner + row_inner, row_outer] = rows
+        for dest in range(frame * inner, (frame + 1) * inner):
+            out_ref[dest] = total
 
 
 def attend(flag, qkv, halo, outer, inner):
-    row_count, width = qkv.shape[2], qkv.shape[3]
+    width = qkv.shape[3]
     vmem = pl.BlockSpec(memory_space=pltpu.VMEM)
     return pl.pallas_call(
         attention_kernel,
-        out_shape=jax.ShapeDtypeStruct((outer * inner, outer, row_count, width), jnp.bfloat16),
+        out_shape=jax.ShapeDtypeStruct((outer * inner, FRAME_TOK, width), jnp.bfloat16),
         in_specs=[pl.BlockSpec(memory_space=pltpu.SMEM), vmem, vmem],
         out_specs=vmem,
     )(flag, qkv, halo)
@@ -96,17 +93,39 @@
     )(planes)
 
 
+def projection_kernel(gathered_ref, weight_ref, out_ref):
+    heads, head_dim = gathered_ref.shape[0], gathered_ref.shape[2]
+    total = None
+    for head in range(heads):
+        part = lax.dot_general(
+            gathered_ref[head],
+            weight_ref[:, head * head_dim : (head + 1) * head_dim],
+            (((1,), (1,)), ((), ())),
+            preferred_element_type=jnp.float32,
+        )
+        total = part if total is None else total + part
+    out_ref[...] = total.astype(out_ref.dtype)
+
+
+def project(gathered, weight_t):
+    vmem = pl.BlockSpec(memory_space=pltpu.VMEM)
+    return pl.pallas_call(
+        projection_kernel,
+        out_shape=jax.ShapeDtypeStruct((gathered.shape[1], weight_t.shape[0]), jnp.bfloat16),
+        in_specs=[vmem, vmem],
+        out_specs=vmem,
+    )(gathered, weight_t)
+
+
 def body(latents, projected, out_weight, gate_table, timesteps):
     row_count = latents.shape[0]
     outer = lax.axis_size("fy")
     inner = lax.axis_size("fp")
     heads = outer * inner
-    head_dim = projected.shape[2] // heads
     per_frame = FRAME_TOK // row_count
     shard = lax.axis_index("fy") * inner + lax.axis_index("fp")
 
-    columns = lax.all_gather(out_weight, "fp", axis=1, tiled=True)
-    columns = columns.reshape(heads, head_dim, columns.shape[1])
+    columns = lax.all_gather(out_weight, "fy", axis=1, tiled=True)
 
     chunks = head_chunks(jnp.transpose(projected, (1, 0, 2)), heads)
     qkv = lax.all_to_all(chunks, ("fy", "fp"), split_axis=0, concat_axis=0, tiled=True)
@@ -115,9 +134,12 @@
     spread = attend(flag, qkv, halo, outer, inner)
 
     gathered = lax.all_to_all(spread, ("fy", "fp"), split_axis=0, concat_axis=0, tiled=True)
-    total = jnp.einsum("jird,jdn->irn", gathered, columns, preferred_element_type=jnp.float32)
-    returned = lax.all_to_all(total.astype(jnp.bfloat16), "fy", split_axis=0, concat_axis=0, tiled=True)
-    branch = jnp.transpose(returned, (1, 0, 2)).reshape(row_count, -1)
+    total = project(gathered, jnp.transpose(columns))
+    total = total.reshape(inner, row_count, total.shape[1])
+    returned = lax.all_to_all(total, "fp", split_axis=0, concat_axis=0, tiled=True)
+    width = out_weight.shape[1]
+    branch = returned.reshape(inner, row_count, outer, width)
+    branch = jnp.transpose(branch, (1, 2, 0, 3)).reshape(row_count, -1)
 
     frame_index = (shard * row_count) // FRAME_TOK
     gate_row = gate_table[timesteps[frame_index]]

time: 104 us -> 100 us (0.962)
  Pallas kernels: 7.02 us -> 11.8 us
  waiting for transfers between devices: 37.6 us -> 33.2 us
  matrix products: 3.61 us -> 0 us
  local copies, waits for them, and re-layouts: 6.11 us -> 4.78 us
    all_to_all x1, waiting for transfers between devices: 1.58 us -> 18.3 us  [body(): lax.all_to_all(spread, ('fy', 'fp'), split_axis=0, concat_axis=0, tiled=T...]
    all_gather x1, waiting for transfers between devices: 11.3 us -> 0.01 us  [body(): columns = lax.all_gather(out_weight, 'fy', axis=1, tiled=True)]
    ppermute x1, waiting for transfers between devices: 16.4 us -> 7.66 us  [passed_along(): lax.ppermute(value, axis, [(source, source + steps) for source in range(i...]
    pallas_call x0 -> x1, Pallas kernels: none -> 4.75 us  [project(): pl.pallas_call(projection_kernel, out_shape=jax.ShapeDtypeStruct((gathere...]
    all_gather x1 -> x0, local copies, waits for them, and re-layouts: 4.66 us -> none  [body(): columns = lax.all_gather(out_weight, 'fp', axis=1, tiled=True)]
    dot_general x1 -> x0, matrix products: 3.61 us -> none  [body(): jnp.einsum('jird,jdn->irn', gathered, columns, preferred_element_type=jnp...]
    convert_element_type x1 -> x3, local copies, waits for them, and re-layouts: 0.06 us -> 2.4 us  [body(): branch.astype(jnp.float32)]
  transfers between devices with their start and end apart: 4 -> 4, of which waited for: 4 -> 3; matrix products, arithmetic and copies ran while one was open for 5% -> 1% of each run, Pallas kernels for 7% -> 7%
where the time goes in v4:
time: 100 us; the launch traced here: 99.6 us
  waiting for transfers between devices  33.2 us (33%)
  blocking collectives  23.2 us (23%)
  between operations  15.4 us (15%)
  Pallas kernels  11.8 us (12%)
  starting transfers between devices  10.3 us (10%)
  local copies, waits for them, and re-layouts  4.78 us (5%)
    all_to_all x1, blocking collectives, body(): lax.all_to_all(chunks, ('fy', 'fp'), split_axis=0, concat_axis=0, tiled=T...  23.2 us
    all_to_all x1, waiting for transfers between devices, body(): lax.all_to_all(spread, ('fy', 'fp'), split_axis=0, concat_axis=0, tiled=T...  18.3 us
    ppermute x1, waiting for transfers between devices, passed_along(): lax.ppermute(value, axis, [(source, source + steps) for source in range(i...  7.66 us
    all_to_all x1, waiting for transfers between devices, body(): lax.all_to_all(total, 'fp', split_axis=0, concat_axis=0, tiled=True)  6.56 us
    all_to_all x1, starting transfers between devices, body(): lax.all_to_all(spread, ('fy', 'fp'), split_axis=0, concat_axis=0, tiled=T...  5.08 us
    pallas_call x1, Pallas kernels, attend(): pl.pallas_call(attention_kernel, out_shape=jax.ShapeDtypeStruct((outer *...  4.87 us
    pallas_call x1, Pallas kernels, project(): pl.pallas_call(projection_kernel, out_shape=jax.ShapeDtypeStruct((gathere...  4.75 us
    all_to_all x1, starting transfers between devices, body(): lax.all_to_all(total, 'fp', split_axis=0, concat_axis=0, tiled=True)  3.95 us
  transfers between devices with their start and end apart: 4, of which 3 were waited for; matrix products, arithmetic and copies ran while one was open for 1% of the time, Pallas kernels for 7%

profile of v4, /device:TPU:1, one launch (start us, length us, event | category | flops | bytes accessed | tf_op | source)
XLA Modules:
  0.0 99.6 jit_solution(18253022994973017537)
XLA Ops:
  6.5 0.0 copy-start
  6.5 0.0 all-gather.2.cloned.1.call-start
  6.5 0.7 all-gather.2.cloned.1.call-update
  7.3 2.2 %shard_map.55 = bf16[16,3,64,128]{3,2,1,0:T(8,128)(2,1)} custom-call(bf16[3,64,2048]{2,1,0:T(8,128)(2,1)} %bitcast.12), custom_call_target="tpu_custom_call" | custom-call | tf_op jit(solution)/shard_map/pallas_call | solution.py:88
  9.4 0.0 copy-start.5
  9.4 23.2 %all_to_all.15.qkv_ref = bf16[16,3,64,128]{3,2,1,0:T(8,128)(2,1)S(1)} all-to-all(bf16[16,3,64,128]{3,2,1,0:T(8,128)(2,1)} %shard_map.55), channel_id=1, replica_groups=mesh['tm'=32,'fy'=4,'fp'=4] {'fy','fp'}, dimensions={0} | all-to-all | bytes 1572864 | tf_op jit(solution)/shard_map/all_to_all | solution.py:131
  32.7 0.0 copy-start.1
  32.7 1.3 %collective-permute-start = (bf16[12,2,64,128]{3,2,1,0:T(8,128)(2,1)S(1)}, bf16[12,2,64,128]{3,2,1,0:T(8,128)(2,1)S(1)}, u32[]{:S(2)}, u32[]{:S(2)}) collective-permute-start(bf16[12,2,64,128]{3,2,1,0:T(8,128)(2,1)S(1)} %slice.4), channel_id=1, source_target_pairs={{0,16},{16,32},{32,48},{48,64},{64,80},{80,96},{96,112},{112,128},... | collective-permute-start | bytes 1179656 | tf_op jit(solution)/shard_map/ppermute | solution.py:16
  34.0 7.7 %collective-permute-done.halo_ref = bf16[12,2,64,128]{3,2,1,0:T(8,128)(2,1)S(1)} collective-permute-done((bf16[12,2,64,128]{3,2,1,0:T(8,128)(2,1)S(1)}, bf16[12,2,64,128]{3,2,1,0:T(8,128)(2,1)S(1)}, u32[]{:S(2)}, u32[]{:S(2)}) %collective-permute-start) | collective-permute-done | bytes 393248 | tf_op jit(solution)/shard_map/ppermute | solution.py:16
  41.7 0.0 copy-start.3
  41.7 0.0 copy-done.1
  41.7 0.7 copy-done.3
  42.4 4.9 %shard_map.56 = bf16[16,256,128]{2,1,0:T(8,128)(2,1)} custom-call(s32[1]{0:T(128)} %bitcast.2.flag_ref, bf16[16,3,64,128]{3,2,1,0:T(8,128)(2,1)} %copy-done.1, bf16[12,2,64,128]{3,2,1,0:T(8,128)(2,1)} %copy-done.3), custom_call_target="tpu_custom_call" | custom-call | tf_op jit(solution)/shard_map/pallas_call | solution.py:71
  47.3 5.1 %all-to-all-start.1 = ((bf16[16,256,128]{2,1,0:T(8,128)(2,1)}), bf16[16,256,128]{2,1,0:T(8,128)(2,1)S(1)}, u32[]{:S(2)}, u32[]{:S(2)}) async-start(bf16[16,256,128]{2,1,0:T(8,128)(2,1)} %shard_map.56), calls=%async_computation.1 | async-start | bytes 2097152 | tf_op jit(solution)/shard_map/all_to_all | solution.py:136
  52.4 0.0 copy-done.5
  52.4 0.6 dynamic_slice.6
  54.9 18.3 %all-to-all-done.1.gathered_ref = bf16[16,256,128]{2,1,0:T(8,128)(2,1)S(1)} async-done(((bf16[16,256,128]{2,1,0:T(8,128)(2,1)}), bf16[16,256,128]{2,1,0:T(8,128)(2,1)S(1)}, u32[]{:S(2)}, u32[]{:S(2)}) %all-to-all-start.1) | async-done | bytes 1048608 | tf_op jit(solution)/shard_map/all_to_all | solution.py:136
  73.2 0.0 copy-start.2
  73.2 0.0 all-gather.2.cloned.1.call-done
  73.2 1.0 copy-done.2
  74.2 4.8 %shard_map.57 = bf16[256,768]{1,0:T(8,128)(2,1)} custom-call(bf16[16,256,128]{2,1,0:T(8,128)(2,1)} %copy-done.2, bf16[768,2048]{1,0:T(8,128)(2,1)} %bitcast.10), custom_call_target="tpu_custom_call" | custom-call | tf_op jit(solution)/shard_map/pallas_call | solution.py:112
  79.0 0.0 copy-start.4
  79.0 4.0 %all-to-all-start.2 = ((bf16[4,64,768]{2,1,0:T(8,128)(2,1)}), bf16[4,64,768]{2,1,0:T(8,128)(2,1)S(1)}, u32[]{:S(2)}, u32[]{:S(2)}) async-start(bf16[4,64,768]{2,1,0:T(8,128)(2,1)} %bitcast.11), calls=%async_computation.2 | async-start | bytes 786432 | tf_op jit(solution)/shard_map/all_to_all | solution.py:139
  82.9 0.0 copy-done
  83.0 6.6 %all-to-all-done.2 = bf16[4,64,768]{2,1,0:T(8,128)(2,1)S(1)} async-done(((bf16[4,64,768]{2,1,0:T(8,128)(2,1)}), bf16[4,64,768]{2,1,0:T(8,128)(2,1)S(1)}, u32[]{:S(2)}, u32[]{:S(2)}) %all-to-all-start.2) | async-done | bytes 393248 | tf_op jit(solution)/shard_map/all_to_all | solution.py:139
  89.5 0.8 reshape.20
  90.3 0.7 copy.8
  91.0 0.9 reshape.19
  91.9 0.0 copy-done.4
  91.9 0.8 add_convert_fusion
  (2 shorter events, 0.0 us)
Async XLA Ops:
  6.5 76.4 %copy-start = (f32[40,3072]{1,0:T(8,128)S(1)}, f32[40,3072]{1,0:T(8,128)}, u32[]{:S(2)}) copy-start(f32[40,3072]{1,0:T(8,128)} %param.8) | copy-start | bytes 1474564
  6.5 66.7 %all-gather.2.cloned.1.call-start = ((), (), s32[]{:S(2)}) async-start(), calls=%async_computation.3 | async-start | bytes 3932160 | tf_op jit(solution)/shard_map/all_gather | solution.py:128
  9.4 43.0 %copy-start.5 = (s32[4]{0:T(128)S(1)}, s32[4]{0:T(128)}, u32[]{:S(2)}) copy-start(s32[4]{0:T(128)} %param.9) | copy-start | bytes 52
  32.7 9.0 %copy-start.1 = (bf16[16,3,64,128]{3,2,1,0:T(8,128)(2,1)}, bf16[16,3,64,128]{3,2,1,0:T(8,128)(2,1)S(1)}, u32[]{:S(2)}) copy-start(bf16[16,3,64,128]{3,2,1,0:T(8,128)(2,1)S(1)} %all_to_all.15.qkv_ref) | copy-start | bytes 2359300
  32.7 9.0 %collective-permute-start = (bf16[12,2,64,128]{3,2,1,0:T(8,128)(2,1)S(1)}, bf16[12,2,64,128]{3,2,1,0:T(8,128)(2,1)S(1)}, u32[]{:S(2)}, u32[]{:S(2)}) collective-permute-start(bf16[12,2,64,128]{3,2,1,0:T(8,128)(2,1)S(1)} %slice.4), channel_id=1, source_target_pairs={{0,16},{16,32},{32,48},{48,64},{64,80},{80,96},{96,112},{112,128},... | collective-permute-start | bytes 1179656 | tf_op jit(solution)/shard_map/ppermute | solution.py:16
  41.7 0.7 copy-start.3
  47.3 25.9 %all-to-all-start.1 = ((bf16[16,256,128]{2,1,0:T(8,128)(2,1)}), bf16[16,256,128]{2,1,0:T(8,128)(2,1)S(1)}, u32[]{:S(2)}, u32[]{:S(2)}) async-start(bf16[16,256,128]{2,1,0:T(8,128)(2,1)} %shard_map.56), calls=%async_computation.1 | async-start | bytes 2097152 | tf_op jit(solution)/shard_map/all_to_all | solution.py:136
  73.2 1.0 %copy-start.2 = (bf16[16,256,128]{2,1,0:T(8,128)(2,1)}, bf16[16,256,128]{2,1,0:T(8,128)(2,1)S(1)}, u32[]{:S(2)}) copy-start(bf16[16,256,128]{2,1,0:T(8,128)(2,1)S(1)} %all-to-all-done.1.gathered_ref) | copy-start | bytes 3145732
  79.0 13.0 %copy-start.4 = (bf16[64,3072]{1,0:T(8,128)(2,1)S(1)}, bf16[64,3072]{1,0:T(8,128)(2,1)}, u32[]{:S(2)}) copy-start(bf16[64,3072]{1,0:T(8,128)(2,1)} %param.5) | copy-start | bytes 1179652
  79.0 10.5 %all-to-all-start.2 = ((bf16[4,64,768]{2,1,0:T(8,128)(2,1)}), bf16[4,64,768]{2,1,0:T(8,128)(2,1)S(1)}, u32[]{:S(2)}, u32[]{:S(2)}) async-start(bf16[4,64,768]{2,1,0:T(8,128)(2,1)} %bitcast.11), calls=%async_computation.2 | async-start | bytes 786432 | tf_op jit(solution)/shard_map/all_to_all | solution.py:139
Sparse Core Ops, SparseCore 0:
  9.5 62.9 all-gather.1

commit v5 on v4

--- a/solution.py
+++ b/solution.py
@@ -21,7 +21,8 @@
     per_frame = FRAME_TOK // row_count
     frame_count = qkv_ref.shape[0] // per_frame
     score_scale = qkv_ref.shape[3] ** (-0.5)
-    inner = out_ref.shape[0] // frame_count
+    outer = out_ref.shape[1]
+    inner = out_ref.shape[0] // outer
     has_prev = flag_ref[0] > 0
 
     def frame_rows(ref, block, plane):
@@ -61,16 +62,19 @@
             part = jnp.dot(probability, value, preferred_element_type=jnp.float32)
             total = part if total is None else total + part
         total = total.astype(out_ref.dtype)
-        for dest in range(frame * inner, (frame + 1) * inner):
-            out_ref[dest] = total
+        for piece in range(per_frame):
+            row_outer, row_inner = divmod(frame * per_frame + piece, inner)
+            rows = total[piece * row_count : (piece + 1) * row_count]
+            for dest_outer in range(outer):
+                out_ref[dest_outer * inner + row_inner, row_outer] = rows
 
 
 def attend(flag, qkv, halo, outer, inner):
-    width = qkv.shape[3]
+    row_count, width = qkv.shape[2], qkv.shape[3]
     vmem = pl.BlockSpec(memory_space=pltpu.VMEM)
     return pl.pallas_call(
         attention_kernel,
-        out_shape=jax.ShapeDtypeStruct((outer * inner, FRAME_TOK, width), jnp.bfloat16),
+        out_shape=jax.ShapeDtypeStruct((outer * inner, outer, row_count, width), jnp.bfloat16),
         in_specs=[pl.BlockSpec(memory_space=pltpu.SMEM), vmem, vmem],
         out_specs=vmem,
     )(flag, qkv, halo)
@@ -94,11 +98,11 @@
 
 
 def projection_kernel(gathered_ref, weight_ref, out_ref):
-    heads, head_dim = gathered_ref.shape[0], gathered_ref.shape[2]
+    heads, head_dim = gathered_ref.shape[0], gathered_ref.shape[3]
     total = None
     for head in range(heads):
         part = lax.dot_general(
-            gathered_ref[head],
+            gathered_ref[head].reshape(-1, head_dim),
             weight_ref[:, head * head_dim : (head + 1) * head_dim],
             (((1,), (1,)), ((), ())),
             preferred_element_type=jnp.float32,
@@ -111,7 +115,9 @@
     vmem = pl.BlockSpec(memory_space=pltpu.VMEM)
     return pl.pallas_call(
         projection_kernel,
-        out_shape=jax.ShapeDtypeStruct((gathered.shape[1], weight_t.shape[0]), jnp.bfloat16),
+        out_shape=jax.ShapeDtypeStruct(
+            (gathered.shape[1] * gathered.shape[2], weight_t.shape[0]), jnp.bfloat16
+        ),
         in_specs=[vmem, vmem],
         out_specs=vmem,
     )(gathered, weight_t)
@@ -119,27 +125,25 @@
 
 def body(latents, projected, out_weight, gate_table, timesteps):
     row_count = latents.shape[0]
-    outer = lax.axis_size("fy")
-    inner = lax.axis_size("fp")
+    outer = lax.axis_size("fo")
+    inner = lax.axis_size("fc")
     heads = outer * inner
     per_frame = FRAME_TOK // row_count
-    shard = lax.axis_index("fy") * inner + lax.axis_index("fp")
+    shard = lax.axis_index("fo") * inner + lax.axis_index("fc")
 
-    columns = lax.all_gather(out_weight, "fy", axis=1, tiled=True)
+    columns = lax.all_gather(out_weight, "fc", axis=1, tiled=True)
 
     chunks = head_chunks(jnp.transpose(projected, (1, 0, 2)), heads)
-    qkv = lax.all_to_all(chunks, ("fy", "fp"), split_axis=0, concat_axis=0, tiled=True)
+    qkv = lax.all_to_all(chunks, ("fo", "fc"), split_axis=0, concat_axis=0, tiled=True)
     halo = passed_along(qkv[per_frame:, 1:3], "tm", 1)
     flag = (lax.axis_index("tm") > 0).astype(jnp.int32).reshape(1)
     spread = attend(flag, qkv, halo, outer, inner)
 
-    gathered = lax.all_to_all(spread, ("fy", "fp"), split_axis=0, concat_axis=0, tiled=True)
+    gathered = lax.all_to_all(spread, ("fo", "fc"), split_axis=0, concat_axis=0, tiled=True)
     total = project(gathered, jnp.transpose(columns))
-    total = total.reshape(inner, row_count, total.shape[1])
-    returned = lax.all_to_all(total, "fp", split_axis=0, concat_axis=0, tiled=True)
-    width = out_weight.shape[1]
-    branch = returned.reshape(inner, row_count, outer, width)
-    branch = jnp.transpose(branch, (1, 2, 0, 3)).reshape(row_count, -1)
+    total = total.reshape(outer, row_count, total.shape[1])
+    returned = lax.all_to_all(total, "fo", split_axis=0, concat_axis=0, tiled=True)
+    branch = jnp.transpose(returned, (1, 0, 2)).reshape(row_count, -1)
 
     frame_index = (shard * row_count) // FRAME_TOK
     gate_row = gate_table[timesteps[frame_index]]
@@ -149,12 +153,12 @@
 
 def solution(mesh):
     tm_size, fsdp_size = mesh.devices.shape
-    split_mesh = Mesh(mesh.devices.reshape(tm_size, fsdp_size // 4, 4), ("tm", "fy", "fp"))
-    rows = ("tm", "fy", "fp")
+    split_mesh = Mesh(mesh.devices.reshape(tm_size, fsdp_size // 2, 2), ("tm", "fo", "fc"))
+    rows = ("tm", "fo", "fc")
     in_specs = (
         P(rows, None),
         P(rows, None, None),
-        P(None, ("fy", "fp")),
+        P(None, ("fo", "fc")),
         P(),
         P("tm"),
     )

time: 100 us -> 109 us (1.090)
  waiting for transfers between devices: 33.2 us -> 43.9 us
  local copies, waits for them, and re-layouts: 4.78 us -> 2.77 us
    all_gather x1, waiting for transfers between devices: 0.01 us -> 29.6 us  [body(): columns = lax.all_gather(out_weight, 'fc', axis=1, tiled=True)]
    all_to_all x2, waiting for transfers between devices: 24.9 us -> 5.98 us  [the longest x1 5.97 us: body(): lax.all_to_all(total, 'fo', split_axis=0, concat_axis=0, tiled=True)]
    convert_element_type x3 -> x1, local copies, waits for them, and re-layouts: 2.4 us -> 0.05 us  [body(): branch.astype(jnp.float32)]
  transfers between devices with their start and end apart: 4 -> 4, of which waited for: 3 -> 3; matrix products, arithmetic and copies ran while one was open for 1% -> 1% of each run, Pallas kernels for 7% -> 0%
where the time goes in v5:
time: 109 us; the launch traced here: 108 us
  waiting for transfers between devices  43.9 us (40%)
  blocking collectives  23.1 us (21%)
  between operations  15.2 us (14%)
  Pallas kernels  12 us (11%)
  starting transfers between devices  10.5 us (10%)
  local copies, waits for them, and re-layouts  2.77 us (3%)
    all_gather x1, waiting for transfers between devices, body(): columns = lax.all_gather(out_weight, 'fc', axis=1, tiled=True)  29.6 us
    all_to_all x1, blocking collectives, body(): lax.all_to_all(chunks, ('fo', 'fc'), split_axis=0, concat_axis=0, tiled=T...  23.1 us
    ppermute x1, waiting for transfers between devices, passed_along(): lax.ppermute(value, axis, [(source, source + steps) for source in range(i...  7.66 us
    all_to_all x1, waiting for transfers between devices, body(): lax.all_to_all(total, 'fo', split_axis=0, concat_axis=0, tiled=True)  5.97 us
    pallas_call x1, Pallas kernels, attend(): pl.pallas_call(attention_kernel, out_shape=jax.ShapeDtypeStruct((outer *...  5.2 us
    all_to_all x1, starting transfers between devices, body(): lax.all_to_all(spread, ('fo', 'fc'), split_axis=0, concat_axis=0, tiled=T...  5.13 us
    pallas_call x1, Pallas kernels, project(): pl.pallas_call(projection_kernel, out_shape=jax.ShapeDtypeStruct((gathere...  4.58 us
    all_to_all x1, starting transfers between devices, body(): lax.all_to_all(total, 'fo', split_axis=0, concat_axis=0, tiled=True)  4.05 us
  transfers between devices with their start and end apart: 4, of which 3 were waited for; matrix products, arithmetic and copies ran while one was open for 1% of the time, Pallas kernels for 0%

profile of v5, /device:TPU:1, one launch (start us, length us, event | category | flops | bytes accessed | tf_op | source)
XLA Modules:
  0.0 108.4 jit_solution(925835068406718156)
XLA Ops:
  6.5 0.0 copy-start
  6.5 2.2 %shard_map.55 = bf16[16,3,64,128]{3,2,1,0:T(8,128)(2,1)} custom-call(bf16[3,64,2048]{2,1,0:T(8,128)(2,1)} %bitcast.13), custom_call_target="tpu_custom_call" | custom-call | tf_op jit(solution)/shard_map/pallas_call | solution.py:92
  8.8 23.1 %all_to_all.15.qkv_ref = bf16[16,3,64,128]{3,2,1,0:T(8,128)(2,1)S(1)} all-to-all(bf16[16,3,64,128]{3,2,1,0:T(8,128)(2,1)} %shard_map.55), channel_id=1, replica_groups=mesh['tm'=32,'fo'=8,'fc'=2] {'fo','fc'}, dimensions={0} | all-to-all | bytes 1572864 | tf_op jit(solution)/shard_map/all_to_all | solution.py:137
  31.9 0.0 copy-start.2
  31.9 1.3 %collective-permute-start = (bf16[12,2,64,128]{3,2,1,0:T(8,128)(2,1)S(1)}, bf16[12,2,64,128]{3,2,1,0:T(8,128)(2,1)S(1)}, u32[]{:S(2)}, u32[]{:S(2)}) collective-permute-start(bf16[12,2,64,128]{3,2,1,0:T(8,128)(2,1)S(1)} %slice.4), channel_id=1, source_target_pairs={{0,16},{16,32},{32,48},{48,64},{64,80},{80,96},{96,112},{112,128},... | collective-permute-start | bytes 1179656 | tf_op jit(solution)/shard_map/ppermute | solution.py:16
  33.2 7.7 %collective-permute-done.halo_ref = bf16[12,2,64,128]{3,2,1,0:T(8,128)(2,1)S(1)} collective-permute-done((bf16[12,2,64,128]{3,2,1,0:T(8,128)(2,1)S(1)}, bf16[12,2,64,128]{3,2,1,0:T(8,128)(2,1)S(1)}, u32[]{:S(2)}, u32[]{:S(2)}) %collective-permute-start) | collective-permute-done | bytes 393248 | tf_op jit(solution)/shard_map/ppermute | solution.py:16
  40.9 0.0 copy-start.4
  40.9 0.0 copy-done.2
  40.9 0.7 copy-done.4
  41.6 5.2 %shard_map.56 = bf16[16,8,64,128]{3,2,1,0:T(8,128)(2,1)} custom-call(s32[1]{0:T(128)} %bitcast.2.flag_ref, bf16[16,3,64,128]{3,2,1,0:T(8,128)(2,1)} %copy-done.2, bf16[12,2,64,128]{3,2,1,0:T(8,128)(2,1)} %copy-done.4), custom_call_target="tpu_custom_call" | custom-call | tf_op jit(solution)/shard_map/pallas_call | solution.py:75
  46.8 5.1 %all-to-all-start.1 = ((bf16[16,8,64,128]{3,2,1,0:T(8,128)(2,1)}), bf16[16,8,64,128]{3,2,1,0:T(8,128)(2,1)S(1)}, u32[]{:S(2)}, u32[]{:S(2)}) async-start(bf16[16,8,64,128]{3,2,1,0:T(8,128)(2,1)} %shard_map.56), calls=%async_computation.1 | async-start | bytes 4194304 | tf_op jit(solution)/shard_map/all_to_all | solution.py:142
  52.0 0.0 all-gather.2.cloned.1.call-start
  52.0 0.7 all-gather.2.cloned.1.call-update
  52.7 29.6 %all-gather.2.cloned.1.call-done = bf16[2048,384]{0,1:T(8,128)(2,1)} async-done(((bf16[2048,192]{0,1:T(8,128)(2,1)}), bf16[2048,384]{0,1:T(8,128)(2,1)}) %all-gather.2.cloned.1.call-update) | async-done | bytes 1572880 | tf_op jit(solution)/shard_map/all_gather | solution.py:134
  82.3 0.0 all-to-all-done.1.gathered_ref
  82.3 0.0 copy-start.1
  82.3 1.3 %copy-done.1 = bf16[16,8,64,128]{3,2,1,0:T(8,128)(2,1)} copy-done((bf16[16,8,64,128]{3,2,1,0:T(8,128)(2,1)}, bf16[16,8,64,128]{3,2,1,0:T(8,128)(2,1)S(1)}, u32[]{:S(2)}) %copy-start.1) | copy-done | bytes 2097176
  83.6 0.0 copy-start.5
  83.6 4.6 %shard_map.57 = bf16[512,384]{1,0:T(8,128)(2,1)} custom-call(bf16[16,8,64,128]{3,2,1,0:T(8,128)(2,1)} %copy-done.1, bf16[384,2048]{1,0:T(8,128)(2,1)} %bitcast.11), custom_call_target="tpu_custom_call" | custom-call | tf_op jit(solution)/shard_map/pallas_call | solution.py:116
  88.2 0.0 copy-start.3
  88.2 4.0 %all-to-all-start.2 = ((bf16[8,64,384]{2,1,0:T(8,128)(2,1)}), bf16[8,64,384]{2,1,0:T(8,128)(2,1)S(1)}, u32[]{:S(2)}, u32[]{:S(2)}) async-start(bf16[8,64,384]{2,1,0:T(8,128)(2,1)} %bitcast.12), calls=%async_computation.2 | async-start | bytes 786432 | tf_op jit(solution)/shard_map/all_to_all | solution.py:145
  92.3 0.0 copy-done.5
  92.3 0.6 dynamic_slice.6
  94.5 0.0 copy-done
  94.6 6.0 %all-to-all-done.2 = bf16[8,64,384]{2,1,0:T(8,128)(2,1)S(1)} async-done(((bf16[8,64,384]{2,1,0:T(8,128)(2,1)}), bf16[8,64,384]{2,1,0:T(8,128)(2,1)S(1)}, u32[]{:S(2)}, u32[]{:S(2)}) %all-to-all-start.2) | async-done | bytes 393248 | tf_op jit(solution)/shard_map/all_to_all | solution.py:145
  100.6 0.1 convert_bitcast_fusion
  100.6 0.1 copy.7
  100.7 0.0 copy-done.3
  100.7 0.8 add_convert_fusion
  (2 shorter events, 0.0 us)
Async XLA Ops:
  6.5 88.0 %copy-start = (f32[40,3072]{1,0:T(8,128)S(1)}, f32[40,3072]{1,0:T(8,128)}, u32[]{:S(2)}) copy-start(f32[40,3072]{1,0:T(8,128)} %param.8) | copy-start | bytes 1474564
  31.9 9.0 %copy-start.2 = (bf16[16,3,64,128]{3,2,1,0:T(8,128)(2,1)}, bf16[16,3,64,128]{3,2,1,0:T(8,128)(2,1)S(1)}, u32[]{:S(2)}) copy-start(bf16[16,3,64,128]{3,2,1,0:T(8,128)(2,1)S(1)} %all_to_all.15.qkv_ref) | copy-start | bytes 2359300
  31.9 9.0 %collective-permute-start = (bf16[12,2,64,128]{3,2,1,0:T(8,128)(2,1)S(1)}, bf16[12,2,64,128]{3,2,1,0:T(8,128)(2,1)S(1)}, u32[]{:S(2)}, u32[]{:S(2)}) collective-permute-start(bf16[12,2,64,128]{3,2,1,0:T(8,128)(2,1)S(1)} %slice.4), channel_id=1, source_target_pairs={{0,16},{16,32},{32,48},{48,64},{64,80},{80,96},{96,112},{112,128},... | collective-permute-start | bytes 1179656 | tf_op jit(solution)/shard_map/ppermute | solution.py:16
  40.9 0.7 copy-start.4
  46.8 35.5 %all-to-all-start.1 = ((bf16[16,8,64,128]{3,2,1,0:T(8,128)(2,1)}), bf16[16,8,64,128]{3,2,1,0:T(8,128)(2,1)S(1)}, u32[]{:S(2)}, u32[]{:S(2)}) async-start(bf16[16,8,64,128]{3,2,1,0:T(8,128)(2,1)} %shard_map.56), calls=%async_computation.1 | async-start | bytes 4194304 | tf_op jit(solution)/shard_map/all_to_all | solution.py:142
  52.0 30.3 %all-gather.2.cloned.1.call-start = ((), (), s32[]{:S(2)}) async-start(), calls=%async_computation.3 | async-start | bytes 2359296 | tf_op jit(solution)/shard_map/all_gather | solution.py:134
  82.3 1.3 %copy-start.1 = (bf16[16,8,64,128]{3,2,1,0:T(8,128)(2,1)}, bf16[16,8,64,128]{3,2,1,0:T(8,128)(2,1)S(1)}, u32[]{:S(2)}) copy-start(bf16[16,8,64,128]{3,2,1,0:T(8,128)(2,1)S(1)} %all-to-all-done.1.gathered_ref) | copy-start | bytes 6291460
  83.6 8.6 %copy-start.5 = (s32[4]{0:T(128)S(1)}, s32[4]{0:T(128)}, u32[]{:S(2)}) copy-start(s32[4]{0:T(128)} %param.9) | copy-start | bytes 52
  88.2 12.5 %copy-start.3 = (bf16[64,3072]{1,0:T(8,128)(2,1)S(1)}, bf16[64,3072]{1,0:T(8,128)(2,1)}, u32[]{:S(2)}) copy-start(bf16[64,3072]{1,0:T(8,128)(2,1)} %param.5) | copy-start | bytes 1179652
  88.2 12.3 %all-to-all-start.2 = ((bf16[8,64,384]{2,1,0:T(8,128)(2,1)}), bf16[8,64,384]{2,1,0:T(8,128)(2,1)S(1)}, u32[]{:S(2)}, u32[]{:S(2)}) async-start(bf16[8,64,384]{2,1,0:T(8,128)(2,1)} %bitcast.12), calls=%async_computation.2 | async-start | bytes 786432 | tf_op jit(solution)/shard_map/all_to_all | solution.py:145
Sparse Core Ops, SparseCore 0:
  54.9 27.3 all-gather.1

commit v6 on v5

--- a/solution.py
+++ b/solution.py
@@ -136,6 +136,7 @@
     chunks = head_chunks(jnp.transpose(projected, (1, 0, 2)), heads)
     qkv = lax.all_to_all(chunks, ("fo", "fc"), split_axis=0, concat_axis=0, tiled=True)
     halo = passed_along(qkv[per_frame:, 1:3], "tm", 1)
+    halo, columns = lax.optimization_barrier((halo, columns))
     flag = (lax.axis_index("tm") > 0).astype(jnp.int32).reshape(1)
     spread = attend(flag, qkv, halo, outer, inner)
 

time: 109 us -> 108 us (level)
  the two profiles are of different devices: /device:TPU:1 before, /device:TPU:384 now
where the time goes in v6:
time: 108 us; the launch traced here: 107 us
  blocking collectives  51.3 us (48%)
  waiting for transfers between devices  17.9 us (17%)
  between operations  15.4 us (14%)
  Pallas kernels  11.9 us (11%)
  starting transfers between devices  8.23 us (8%)
  local copies, waits for them, and re-layouts  1.46 us (1%)
    all_to_all x1, blocking collectives, body(): lax.all_to_all(spread, ('fo', 'fc'), split_axis=0, concat_axis=0, tiled=T...  32.2 us
    all_to_all x1, blocking collectives, body(): lax.all_to_all(chunks, ('fo', 'fc'), split_axis=0, concat_axis=0, tiled=T...  19.2 us
    ppermute x1, waiting for transfers between devices, passed_along(): lax.ppermute(value, axis, [(source, source + steps) for source in range(i...  11.4 us
    all_to_all x1, waiting for transfers between devices, body(): lax.all_to_all(total, 'fo', split_axis=0, concat_axis=0, tiled=True)  5.82 us
    pallas_call x1, Pallas kernels, attend(): pl.pallas_call(attention_kernel, out_shape=jax.ShapeDtypeStruct((outer *...  5.2 us
    ppermute x1, starting transfers between devices, passed_along(): lax.ppermute(value, axis, [(source, source + steps) for source in range(i...  4.64 us
    pallas_call x1, Pallas kernels, project(): pl.pallas_call(projection_kernel, out_shape=jax.ShapeDtypeStruct((gathere...  4.59 us
    all_to_all x1, starting transfers between devices, body(): lax.all_to_all(total, 'fo', split_axis=0, concat_axis=0, tiled=True)  3.58 us
  transfers between devices with their start and end apart: 3, of which 2 were waited for; matrix products, arithmetic and copies ran while one was open for 1% of the time, Pallas kernels for 2%

profile of v6, /device:TPU:384, one launch (start us, length us, event | category | flops | bytes accessed | tf_op | source)
XLA Modules:
  0.0 107.2 jit_solution(4016327298531661966)
XLA Ops:
  6.5 0.0 copy-start
  6.5 0.0 all-gather.2.cloned.1.call-start
  6.5 0.7 all-gather.2.cloned.1.call-update
  7.3 2.1 %shard_map.55 = bf16[16,3,64,128]{3,2,1,0:T(8,128)(2,1)} custom-call(bf16[3,64,2048]{2,1,0:T(8,128)(2,1)} %bitcast.13), custom_call_target="tpu_custom_call" | custom-call | tf_op jit(solution)/shard_map/pallas_call | solution.py:92
  9.4 19.2 %all_to_all.15.qkv_ref = bf16[16,3,64,128]{3,2,1,0:T(8,128)(2,1)S(1)} all-to-all(bf16[16,3,64,128]{3,2,1,0:T(8,128)(2,1)} %shard_map.55), channel_id=1, replica_groups=mesh['tm'=32,'fo'=8,'fc'=2] {'fo','fc'}, dimensions={0} | all-to-all | bytes 1572864 | tf_op jit(solution)/shard_map/all_to_all | solution.py:137
  28.6 0.0 copy-start.1
  28.6 4.6 %collective-permute-start = (bf16[12,2,64,128]{3,2,1,0:T(8,128)(2,1)S(1)}, bf16[12,2,64,128]{3,2,1,0:T(8,128)(2,1)S(1)}, u32[]{:S(2)}, u32[]{:S(2)}) collective-permute-start(bf16[12,2,64,128]{3,2,1,0:T(8,128)(2,1)S(1)} %slice.4), channel_id=1, source_target_pairs={{0,16},{16,32},{32,48},{48,64},{64,80},{80,96},{96,112},{112,128},... | collective-permute-start | bytes 1179656 | tf_op jit(solution)/shard_map/ppermute | solution.py:16
  33.3 11.4 %collective-permute-done.halo_ref = bf16[12,2,64,128]{3,2,1,0:T(8,128)(2,1)S(1)} collective-permute-done((bf16[12,2,64,128]{3,2,1,0:T(8,128)(2,1)S(1)}, bf16[12,2,64,128]{3,2,1,0:T(8,128)(2,1)S(1)}, u32[]{:S(2)}, u32[]{:S(2)}) %collective-permute-start) | collective-permute-done | bytes 393248 | tf_op jit(solution)/shard_map/ppermute | solution.py:16
  44.7 0.0 copy-start.3
  44.7 0.0 all-gather.2.cloned.1.call-done
  44.7 0.0 copy-done.1
  44.7 0.7 copy-done.3
  45.4 5.2 %shard_map.56 = bf16[16,8,64,128]{3,2,1,0:T(8,128)(2,1)} custom-call(s32[1]{0:T(128)} %bitcast.2.flag_ref, bf16[16,3,64,128]{3,2,1,0:T(8,128)(2,1)} %copy-done.1, bf16[12,2,64,128]{3,2,1,0:T(8,128)(2,1)} %copy-done.3), custom_call_target="tpu_custom_call" | custom-call | tf_op jit(solution)/shard_map/pallas_call | solution.py:75
  50.6 32.2 %all_to_all.16.gathered_ref = bf16[16,8,64,128]{3,2,1,0:T(8,128)(2,1)} all-to-all(bf16[16,8,64,128]{3,2,1,0:T(8,128)(2,1)} %shard_map.56), channel_id=1, replica_groups=mesh['tm'=32,'fo'=8,'fc'=2] {'fo','fc'}, dimensions={0} | all-to-all | bytes 4194304 | tf_op jit(solution)/shard_map/all_to_all | solution.py:143
  82.8 0.0 copy-start.4
  82.8 4.6 %shard_map.57 = bf16[512,384]{1,0:T(8,128)(2,1)} custom-call(bf16[16,8,64,128]{3,2,1,0:T(8,128)(2,1)} %all_to_all.16.gathered_ref, bf16[384,2048]{1,0:T(8,128)(2,1)} %bitcast.11), custom_call_target="tpu_custom_call" | custom-call | tf_op jit(solution)/shard_map/pallas_call | solution.py:116
  87.4 0.0 copy-start.2
  87.4 3.6 %all-to-all-start.2 = ((bf16[8,64,384]{2,1,0:T(8,128)(2,1)}), bf16[8,64,384]{2,1,0:T(8,128)(2,1)S(1)}, u32[]{:S(2)}, u32[]{:S(2)}) async-start(bf16[8,64,384]{2,1,0:T(8,128)(2,1)} %bitcast.12), calls=%async_computation.2 | async-start | bytes 786432 | tf_op jit(solution)/shard_map/all_to_all | solution.py:146
  91.0 0.0 copy-done.4
  91.0 0.6 dynamic_slice.6
  93.5 0.0 copy-done
  93.5 5.8 %all-to-all-done.2 = bf16[8,64,384]{2,1,0:T(8,128)(2,1)S(1)} async-done(((bf16[8,64,384]{2,1,0:T(8,128)(2,1)}), bf16[8,64,384]{2,1,0:T(8,128)(2,1)S(1)}, u32[]{:S(2)}, u32[]{:S(2)}) %all-to-all-start.2) | async-done | bytes 393248 | tf_op jit(solution)/shard_map/all_to_all | solution.py:146
  99.4 0.1 convert_bitcast_fusion
  99.4 0.1 copy.7
  99.5 0.0 copy-done.2
  99.5 0.8 add_convert_fusion
  (2 shorter events, 0.0 us)
Async XLA Ops:
  6.5 87.0 %copy-start = (f32[40,3072]{1,0:T(8,128)S(1)}, f32[40,3072]{1,0:T(8,128)}, u32[]{:S(2)}) copy-start(f32[40,3072]{1,0:T(8,128)} %param.8) | copy-start | bytes 1474564
  6.5 38.1 %all-gather.2.cloned.1.call-start = ((), (), s32[]{:S(2)}) async-start(), calls=%async_computation.3 | async-start | bytes 2359296 | tf_op jit(solution)/shard_map/all_gather | solution.py:134
  28.6 16.1 %copy-start.1 = (bf16[16,3,64,128]{3,2,1,0:T(8,128)(2,1)}, bf16[16,3,64,128]{3,2,1,0:T(8,128)(2,1)S(1)}, u32[]{:S(2)}) copy-start(bf16[16,3,64,128]{3,2,1,0:T(8,128)(2,1)S(1)} %all_to_all.15.qkv_ref) | copy-start | bytes 2359300
  28.6 16.1 %collective-permute-start = (bf16[12,2,64,128]{3,2,1,0:T(8,128)(2,1)S(1)}, bf16[12,2,64,128]{3,2,1,0:T(8,128)(2,1)S(1)}, u32[]{:S(2)}, u32[]{:S(2)}) collective-permute-start(bf16[12,2,64,128]{3,2,1,0:T(8,128)(2,1)S(1)} %slice.4), channel_id=1, source_target_pairs={{0,16},{16,32},{32,48},{48,64},{64,80},{80,96},{96,112},{112,128},... | collective-permute-start | bytes 1179656 | tf_op jit(solution)/shard_map/ppermute | solution.py:16
  44.7 0.7 copy-start.3
  82.8 8.2 %copy-start.4 = (s32[4]{0:T(128)S(1)}, s32[4]{0:T(128)}, u32[]{:S(2)}) copy-start(s32[4]{0:T(128)} %param.9) | copy-start | bytes 52
  87.4 12.1 %copy-start.2 = (bf16[64,3072]{1,0:T(8,128)(2,1)S(1)}, bf16[64,3072]{1,0:T(8,128)(2,1)}, u32[]{:S(2)}) copy-start(bf16[64,3072]{1,0:T(8,128)(2,1)} %param.5) | copy-start | bytes 1179652
  87.4 12.0 %all-to-all-start.2 = ((bf16[8,64,384]{2,1,0:T(8,128)(2,1)}), bf16[8,64,384]{2,1,0:T(8,128)(2,1)S(1)}, u32[]{:S(2)}, u32[]{:S(2)}) async-start(bf16[8,64,384]{2,1,0:T(8,128)(2,1)} %bitcast.12), calls=%async_computation.2 | async-start | bytes 786432 | tf_op jit(solution)/shard_map/all_to_all | solution.py:146
Sparse Core Ops, SparseCore 0:
  9.4 20.3 all-gather.1

commit v7 on v4

--- a/solution.py
+++ b/solution.py
@@ -16,7 +16,8 @@
     return lax.ppermute(value, axis, [(source, source + steps) for source in range(initial, last)])
 
 
-def attention_kernel(flag_ref, qkv_ref, halo_ref, out_ref):
+def attention_kernel(flag_ref, q_ref, kv_ref, halo_ref, out_ref):
+    qkv_ref = kv_ref
     row_count = qkv_ref.shape[2]
     per_frame = FRAME_TOK // row_count
     frame_count = qkv_ref.shape[0] // per_frame
@@ -28,13 +29,13 @@
         return ref[pl.ds(block, per_frame), plane].reshape(FRAME_TOK, ref.shape[3])
 
     for frame in range(frame_count):
-        query = frame_rows(qkv_ref, frame * per_frame, 0)
+        query = frame_rows(q_ref, frame * per_frame, 0)
         blocks = []
         for back in range(WINDOW):
             source = frame - (WINDOW - 1) + back
             if source >= 0:
-                key = frame_rows(qkv_ref, source * per_frame, 1)
-                value = frame_rows(qkv_ref, source * per_frame, 2)
+                key = frame_rows(kv_ref, source * per_frame, 0)
+                value = frame_rows(kv_ref, source * per_frame, 1)
             else:
                 block = (source + WINDOW - 1) * per_frame
                 key, value = frame_rows(halo_ref, block, 0), frame_rows(halo_ref, block, 1)
@@ -65,21 +66,23 @@
             out_ref[dest] = total
 
 
-def attend(flag, qkv, halo, outer, inner):
-    width = qkv.shape[3]
+def attend(flag, q, kv, halo, outer, inner):
+    width = kv.shape[3]
     vmem = pl.BlockSpec(memory_space=pltpu.VMEM)
     return pl.pallas_call(
         attention_kernel,
         out_shape=jax.ShapeDtypeStruct((outer * inner, FRAME_TOK, width), jnp.bfloat16),
-        in_specs=[pl.BlockSpec(memory_space=pltpu.SMEM), vmem, vmem],
+        in_specs=[pl.BlockSpec(memory_space=pltpu.SMEM), vmem, vmem, vmem],
         out_specs=vmem,
-    )(flag, qkv, halo)
+    )(flag, q, kv, halo)
 
 
-def chunk_kernel(rows_ref, out_ref):
-    width = out_ref.shape[3]
-    for head in range(out_ref.shape[0]):
-        out_ref[head] = rows_ref[:, :, head * width : (head + 1) * width]
+def chunk_kernel(rows_ref, query_ref, key_value_ref):
+    width = query_ref.shape[3]
+    for head in range(query_ref.shape[0]):
+        columns = pl.ds(head * width, width)
+        query_ref[head] = rows_ref[0:1, :, columns]
+        key_value_ref[head] = rows_ref[1:3, :, columns]
 
 
 def head_chunks(planes, heads):
@@ -87,9 +90,12 @@
     vmem = pl.BlockSpec(memory_space=pltpu.VMEM)
     return pl.pallas_call(
         chunk_kernel,
-        out_shape=jax.ShapeDtypeStruct((heads, lanes, row_count, features // heads), planes.dtype),
+        out_shape=(
+            jax.ShapeDtypeStruct((heads, 1, row_count, features // heads), planes.dtype),
+            jax.ShapeDtypeStruct((heads, lanes - 1, row_count, features // heads), planes.dtype),
+        ),
         in_specs=[vmem],
-        out_specs=vmem,
+        out_specs=(vmem, vmem),
     )(planes)
 
 
@@ -127,11 +133,12 @@
 
     columns = lax.all_gather(out_weight, "fy", axis=1, tiled=True)
 
-    chunks = head_chunks(jnp.transpose(projected, (1, 0, 2)), heads)
-    qkv = lax.all_to_all(chunks, ("fy", "fp"), split_axis=0, concat_axis=0, tiled=True)
-    halo = passed_along(qkv[per_frame:, 1:3], "tm", 1)
+    query_chunks, key_value_chunks = head_chunks(jnp.transpose(projected, (1, 0, 2)), heads)
+    kv = lax.all_to_all(key_value_chunks, ("fy", "fp"), split_axis=0, concat_axis=0, tiled=True)
+    halo = passed_along(kv[per_frame:], "tm", 1)
+    q = lax.all_to_all(query_chunks, ("fy", "fp"), split_axis=0, concat_axis=0, tiled=True)
     flag = (lax.axis_index("tm") > 0).astype(jnp.int32).reshape(1)
-    spread = attend(flag, qkv, halo, outer, inner)
+    spread = attend(flag, q, kv, halo, outer, inner)
 
     gathered = lax.all_to_all(spread, ("fy", "fp"), split_axis=0, concat_axis=0, tiled=True)
     total = project(gathered, jnp.transpose(columns))

time: 100 us -> 102 us (1.020)
  starting transfers between devices: 10.3 us -> 13.5 us
  blocking collectives: 23.2 us -> 20.2 us
  waiting for transfers between devices: 33.2 us -> 35.7 us
    all_to_all x0 -> x1, waiting for transfers between devices: none -> 9.11 us  [body(): lax.all_to_all(query_chunks, ('fy', 'fp'), split_axis=0, concat_axis=0, t...]
    ppermute x1, waiting for transfers between devices: 7.66 us -> 0.01 us  [passed_along(): lax.ppermute(value, axis, [(source, source + steps) for source in range(i...]
    all_to_all x0 -> x1, starting transfers between devices: none -> 4.5 us  [body(): lax.all_to_all(query_chunks, ('fy', 'fp'), split_axis=0, concat_axis=0, t...]
    all_to_all x1, blocking collectives: 23.2 us -> 20.2 us  [body(): lax.all_to_all(key_value_chunks, ('fy', 'fp'), split_axis=0, concat_axis=...]
    all_to_all x1, starting transfers between devices: 5.08 us -> 3.92 us  [body(): lax.all_to_all(spread, ('fy', 'fp'), split_axis=0, concat_axis=0, tiled=T...]
  transfers between devices with their start and end apart: 4 -> 5, of which waited for: 3 -> 4; matrix products, arithmetic and copies ran while one was open for 1% -> 1% of each run, Pallas kernels for 7% -> 7%
where the time goes in v7:
time: 102 us
  waiting for transfers between devices  35.7 us (35%)
  blocking collectives  20.2 us (20%)
  between operations  15.4 us (15%)
  starting transfers between devices  13.5 us (13%)
  Pallas kernels  11.8 us (12%)
  local copies, waits for them, and re-layouts  4.37 us (4%)
    all_to_all x1, blocking collectives, body(): lax.all_to_all(key_value_chunks, ('fy', 'fp'), split_axis=0, concat_axis=...  20.2 us
    all_to_all x1, waiting for transfers between devices, body(): lax.all_to_all(spread, ('fy', 'fp'), split_axis=0, concat_axis=0, tiled=T...  18.8 us
    all_to_all x1, waiting for transfers between devices, body(): lax.all_to_all(query_chunks, ('fy', 'fp'), split_axis=0, concat_axis=0, t...  9.11 us
    all_to_all x1, waiting for transfers between devices, body(): lax.all_to_all(total, 'fp', split_axis=0, concat_axis=0, tiled=True)  6.56 us
    pallas_call x1, Pallas kernels, attend(): pl.pallas_call(attention_kernel, out_shape=jax.ShapeDtypeStruct((outer *...  4.88 us
    pallas_call x1, Pallas kernels, project(): pl.pallas_call(projection_kernel, out_shape=jax.ShapeDtypeStruct((gathere...  4.75 us
    all_to_all x1, starting transfers between devices, body(): lax.all_to_all(query_chunks, ('fy', 'fp'), split_axis=0, concat_axis=0, t...  4.5 us
    all_to_all x1, starting transfers between devices, body(): lax.all_to_all(spread, ('fy', 'fp'), split_axis=0, concat_axis=0, tiled=T...  3.92 us
  transfers between devices with their start and end apart: 5, of which 4 were waited for; matrix products, arithmetic and copies ran while one was open for 1% of the time, Pallas kernels for 7%

profile of v7, /device:TPU:1, one launch (start us, length us, event | category | flops | bytes accessed | tf_op | source)
XLA Modules:
  0.0 101.8 jit_solution(11517847056152806688)
XLA Ops:
  6.5 0.0 copy-start
  6.5 0.0 all-gather.2.cloned.1.call-start
  6.5 0.7 all-gather.2.cloned.1.call-update
  7.3 2.1 %shard_map.55 = (bf16[16,1,64,128]{3,2,1,0:T(8,128)(2,1)}, bf16[16,2,64,128]{3,2,1,0:T(8,128)(2,1)}) custom-call(bf16[3,64,2048]{2,1,0:T(8,128)(2,1)} %bitcast.12), custom_call_target="tpu_custom_call" | custom-call | tf_op jit(solution)/shard_map/pallas_call | solution.py:91
  9.4 0.0 copy-start.6
  9.4 20.2 %all_to_all.20.kv_ref = bf16[16,2,64,128]{3,2,1,0:T(8,128)(2,1)S(1)} all-to-all(bf16[16,2,64,128]{3,2,1,0:T(8,128)(2,1)} %get-tuple-element.8), channel_id=1, replica_groups=mesh['tm'=32,'fy'=4,'fp'=4] {'fy','fp'}, dimensions={0} | all-to-all | bytes 1048576 | tf_op jit(solution)/shard_map/all_to_all | solution.py:137
  29.6 0.0 copy-start.2
  29.7 1.3 %collective-permute-start = (bf16[12,2,64,128]{3,2,1,0:T(8,128)(2,1)S(1)}, bf16[12,2,64,128]{3,2,1,0:T(8,128)(2,1)S(1)}, u32[]{:S(2)}, u32[]{:S(2)}) collective-permute-start(bf16[12,2,64,128]{3,2,1,0:T(8,128)(2,1)S(1)} %slice.4), channel_id=1, source_target_pairs={{0,16},{16,32},{32,48},{48,64},{64,80},{80,96},{96,112},{112,128},... | collective-permute-start | bytes 1179656 | tf_op jit(solution)/shard_map/ppermute | solution.py:16
  31.0 4.5 %all-to-all-start = ((bf16[16,1,64,128]{3,2,1,0:T(8,128)(2,1)}), bf16[16,1,64,128]{3,2,1,0:T(8,128)(2,1)S(1)}, u32[]{:S(2)}, u32[]{:S(2)}) async-start(bf16[16,1,64,128]{3,2,1,0:T(8,128)(2,1)} %get-tuple-element.7), calls=%async_computation | async-start | bytes 524288 | tf_op jit(solution)/shard_map/all_to_all | solution.py:139
  35.5 9.1 %all-to-all-done.q_ref = bf16[16,1,64,128]{3,2,1,0:T(8,128)(2,1)S(1)} async-done(((bf16[16,1,64,128]{3,2,1,0:T(8,128)(2,1)}), bf16[16,1,64,128]{3,2,1,0:T(8,128)(2,1)S(1)}, u32[]{:S(2)}, u32[]{:S(2)}) %all-to-all-start) | async-done | bytes 262176 | tf_op jit(solution)/shard_map/all_to_all | solution.py:139
  44.6 0.0 copy-start.3
  44.6 0.0 collective-permute-done.halo_ref
  44.6 0.0 copy-start.4
  44.6 0.0 copy-done.2
  44.6 0.7 copy-done.3
  45.3 0.1 copy-done.4
  45.4 4.9 %shard_map.56 = bf16[16,256,128]{2,1,0:T(8,128)(2,1)} custom-call(s32[1]{0:T(128)} %bitcast.2.flag_ref, bf16[16,1,64,128]{3,2,1,0:T(8,128)(2,1)} %copy-done.3, bf16[16,2,64,128]{3,2,1,0:T(8,128)(2,1)} %copy-done.2, bf16[12,2,64,128]{3,2,1,0:T(8,128)(2,1)} %copy-done.4), custom_call_target="tpu_custom_call" | custom-call | tf_op jit(solution)/shard_map/pallas_call | solution.py:72
  50.3 3.9 %all-to-all-start.2 = ((bf16[16,256,128]{2,1,0:T(8,128)(2,1)}), bf16[16,256,128]{2,1,0:T(8,128)(2,1)S(1)}, u32[]{:S(2)}, u32[]{:S(2)}) async-start(bf16[16,256,128]{2,1,0:T(8,128)(2,1)} %shard_map.56), calls=%async_computation.2 | async-start | bytes 2097152 | tf_op jit(solution)/shard_map/all_to_all | solution.py:143
  54.2 0.0 copy-done.6
  54.2 0.6 dynamic_slice.6
  56.8 18.8 %all-to-all-done.2.gathered_ref = bf16[16,256,128]{2,1,0:T(8,128)(2,1)S(1)} async-done(((bf16[16,256,128]{2,1,0:T(8,128)(2,1)}), bf16[16,256,128]{2,1,0:T(8,128)(2,1)S(1)}, u32[]{:S(2)}, u32[]{:S(2)}) %all-to-all-start.2) | async-done | bytes 1048608 | tf_op jit(solution)/shard_map/all_to_all | solution.py:143
  75.6 0.0 copy-start.1
  75.6 0.5 all-gather.2.cloned.1.call-done
  76.1 0.5 copy-done.1
  76.6 4.8 %shard_map.57 = bf16[256,768]{1,0:T(8,128)(2,1)} custom-call(bf16[16,256,128]{2,1,0:T(8,128)(2,1)} %copy-done.1, bf16[768,2048]{1,0:T(8,128)(2,1)} %bitcast.10), custom_call_target="tpu_custom_call" | custom-call | tf_op jit(solution)/shard_map/pallas_call | solution.py:118
  81.3 0.0 copy-start.5
  81.3 3.8 %all-to-all-start.3 = ((bf16[4,64,768]{2,1,0:T(8,128)(2,1)}), bf16[4,64,768]{2,1,0:T(8,128)(2,1)S(1)}, u32[]{:S(2)}, u32[]{:S(2)}) async-start(bf16[4,64,768]{2,1,0:T(8,128)(2,1)} %bitcast.11), calls=%async_computation.3 | async-start | bytes 786432 | tf_op jit(solution)/shard_map/all_to_all | solution.py:146
  85.1 0.0 copy-done
  85.1 6.6 %all-to-all-done.3 = bf16[4,64,768]{2,1,0:T(8,128)(2,1)S(1)} async-done(((bf16[4,64,768]{2,1,0:T(8,128)(2,1)}), bf16[4,64,768]{2,1,0:T(8,128)(2,1)S(1)}, u32[]{:S(2)}, u32[]{:S(2)}) %all-to-all-start.3) | async-done | bytes 393248 | tf_op jit(solution)/shard_map/all_to_all | solution.py:146
  91.7 0.8 reshape.20
  92.4 0.7 copy.8
  93.1 0.9 reshape.19
  94.1 0.0 copy-done.5
  94.1 0.8 add_convert_fusion
  (2 shorter events, 0.0 us)
Async XLA Ops:
  6.5 78.5 %copy-start = (f32[40,3072]{1,0:T(8,128)S(1)}, f32[40,3072]{1,0:T(8,128)}, u32[]{:S(2)}) copy-start(f32[40,3072]{1,0:T(8,128)} %param.8) | copy-start | bytes 1474564
  6.5 69.5 %all-gather.2.cloned.1.call-start = ((), (), s32[]{:S(2)}) async-start(), calls=%async_computation.4 | async-start | bytes 3932160 | tf_op jit(solution)/shard_map/all_gather | solution.py:134
  9.4 44.8 %copy-start.6 = (s32[4]{0:T(128)S(1)}, s32[4]{0:T(128)}, u32[]{:S(2)}) copy-start(s32[4]{0:T(128)} %param.9) | copy-start | bytes 52
  29.6 15.0 %copy-start.2 = (bf16[16,2,64,128]{3,2,1,0:T(8,128)(2,1)}, bf16[16,2,64,128]{3,2,1,0:T(8,128)(2,1)S(1)}, u32[]{:S(2)}) copy-start(bf16[16,2,64,128]{3,2,1,0:T(8,128)(2,1)S(1)} %all_to_all.20.kv_ref) | copy-start | bytes 1572868
  29.7 14.9 %collective-permute-start = (bf16[12,2,64,128]{3,2,1,0:T(8,128)(2,1)S(1)}, bf16[12,2,64,128]{3,2,1,0:T(8,128)(2,1)S(1)}, u32[]{:S(2)}, u32[]{:S(2)}) collective-permute-start(bf16[12,2,64,128]{3,2,1,0:T(8,128)(2,1)S(1)} %slice.4), channel_id=1, source_target_pairs={{0,16},{16,32},{32,48},{48,64},{64,80},{80,96},{96,112},{112,128},... | collective-permute-start | bytes 1179656 | tf_op jit(solution)/shard_map/ppermute | solution.py:16
  31.0 13.6 %all-to-all-start = ((bf16[16,1,64,128]{3,2,1,0:T(8,128)(2,1)}), bf16[16,1,64,128]{3,2,1,0:T(8,128)(2,1)S(1)}, u32[]{:S(2)}, u32[]{:S(2)}) async-start(bf16[16,1,64,128]{3,2,1,0:T(8,128)(2,1)} %get-tuple-element.7), calls=%async_computation | async-start | bytes 524288 | tf_op jit(solution)/shard_map/all_to_all | solution.py:139
  44.6 0.7 copy-start.3
  44.6 0.8 copy-start.4
  50.3 25.2 %all-to-all-start.2 = ((bf16[16,256,128]{2,1,0:T(8,128)(2,1)}), bf16[16,256,128]{2,1,0:T(8,128)(2,1)S(1)}, u32[]{:S(2)}, u32[]{:S(2)}) async-start(bf16[16,256,128]{2,1,0:T(8,128)(2,1)} %shard_map.56), calls=%async_computation.2 | async-start | bytes 2097152 | tf_op jit(solution)/shard_map/all_to_all | solution.py:143
  75.6 1.0 copy-start.1
  81.3 12.8 %copy-start.5 = (bf16[64,3072]{1,0:T(8,128)(2,1)S(1)}, bf16[64,3072]{1,0:T(8,128)(2,1)}, u32[]{:S(2)}) copy-start(bf16[64,3072]{1,0:T(8,128)(2,1)} %param.5) | copy-start | bytes 1179652
  81.3 10.3 %all-to-all-start.3 = ((bf16[4,64,768]{2,1,0:T(8,128)(2,1)}), bf16[4,64,768]{2,1,0:T(8,128)(2,1)S(1)}, u32[]{:S(2)}, u32[]{:S(2)}) async-start(bf16[4,64,768]{2,1,0:T(8,128)(2,1)} %bitcast.11), calls=%async_computation.3 | async-start | bytes 786432 | tf_op jit(solution)/shard_map/all_to_all | solution.py:146
Sparse Core Ops, SparseCore 0:
  9.5 66.5 all-gather.1

commit v8 on v4

--- a/solution.py
+++ b/solution.py
@@ -93,28 +93,63 @@
     )(planes)
 
 
-def projection_kernel(gathered_ref, weight_ref, out_ref):
-    heads, head_dim = gathered_ref.shape[0], gathered_ref.shape[2]
-    total = None
-    for head in range(heads):
-        part = lax.dot_general(
-            gathered_ref[head],
-            weight_ref[:, head * head_dim : (head + 1) * head_dim],
-            (((1,), (1,)), ((), ())),
-            preferred_element_type=jnp.float32,
-        )
-        total = part if total is None else total + part
-    out_ref[...] = total.astype(out_ref.dtype)
+def projection_kernel(gathered_ref, weight_ref, out_ref, total_ref):
+    head = pl.program_id(0)
+    part = lax.dot_general(
+        gathered_ref[0], weight_ref[...], (((1,), (1,)), ((), ())), preferred_element_type=jnp.float32
+    )
+
+    @pl.when(head == 0)
+    def _():
+        total_ref[...] = part
+
+    @pl.when(head > 0)
+    def _():
+        total_ref[...] += part
+
+    @pl.when(head == pl.num_programs(0) - 1)
+    def _():
+        out_ref[...] = total_ref[...].astype(out_ref.dtype)
 
 
 def project(gathered, weight_t):
+    heads, rows, head_dim = gathered.shape
+    width = weight_t.shape[0]
+    return pl.pallas_call(
+        projection_kernel,
+        out_shape=jax.ShapeDtypeStruct((rows, width), jnp.bfloat16),
+        grid=(heads,),
+        in_specs=[
+            pl.BlockSpec((1, rows, head_dim), lambda h: (h, 0, 0)),
+            pl.BlockSpec((width, head_dim), lambda h: (0, h)),
+        ],
+        out_specs=pl.BlockSpec((rows, width), lambda h: (0, 0)),
+        scratch_shapes=[pltpu.VMEM((rows, width), jnp.float32)],
+    )(gathered, weight_t)
+
+
+def finish_kernel(returned_ref, latents_ref, gate_ref, out_ref):
+    senders, _, width = returned_ref.shape
+    blocks = gate_ref.shape[1] // (senders * senders)
+    for sender in range(senders):
+        for block in range(width // blocks):
+            column = blocks * (senders * block + sender)
+            branch = returned_ref[sender, :, block * blocks : (block + 1) * blocks]
+            residual = latents_ref[:, column : column + blocks].astype(jnp.float32)
+            gate = gate_ref[:, column : column + blocks]
+            out_ref[:, column : column + blocks] = (
+                residual + gate * branch.astype(jnp.float32)
+            ).astype(out_ref.dtype)
+
+
+def finish(returned, latents, gate_row):
     vmem = pl.BlockSpec(memory_space=pltpu.VMEM)
     return pl.pallas_call(
-        projection_kernel,
-        out_shape=jax.ShapeDtypeStruct((gathered.shape[1], weight_t.shape[0]), jnp.bfloat16),
-        in_specs=[vmem, vmem],
+        finish_kernel,
+        out_shape=jax.ShapeDtypeStruct(latents.shape, jnp.bfloat16),
+        in_specs=[vmem, vmem, vmem],
         out_specs=vmem,
-    )(gathered, weight_t)
+    )(returned, latents, gate_row)
 
 
 def body(latents, projected, out_weight, gate_table, timesteps):
@@ -137,14 +172,10 @@
     total = project(gathered, jnp.transpose(columns))
     total = total.reshape(inner, row_count, total.shape[1])
     returned = lax.all_to_all(total, "fp", split_axis=0, concat_axis=0, tiled=True)
-    width = out_weight.shape[1]
-    branch = returned.reshape(inner, row_count, outer, width)
-    branch = jnp.transpose(branch, (1, 2, 0, 3)).reshape(row_count, -1)
 
     frame_index = (shard * row_count) // FRAME_TOK
-    gate_row = gate_table[timesteps[frame_index]]
-    updated = latents.astype(jnp.float32) + gate_row[None, :] * branch.astype(jnp.float32)
-    return updated.astype(jnp.bfloat16)
+    gate_row = lax.dynamic_index_in_dim(gate_table, timesteps[frame_index], 0, keepdims=True)
+    return finish(returned, latents, gate_row)
 
 
 def solution(mesh):

time: 100 us -> 107 us (1.070)
  Pallas kernels: 11.8 us -> 20.9 us
  local copies, waits for them, and re-layouts: 4.78 us -> 3.71 us
    pallas_call x1 -> x2, Pallas kernels: 4.75 us -> 13.8 us  [the longest x1 11.8 us: project(): pl.pallas_call(projection_kernel, out_shape=jax.ShapeDtypeStruct((rows, w...]
    convert_element_type x3 -> x0, local copies, waits for them, and re-layouts: 2.4 us -> none  [body(): branch.astype(jnp.float32)]
where the time goes in v8:
time: 107 us; the launch traced here: 106 us
  waiting for transfers between devices  32.6 us (30%)
  blocking collectives  23.2 us (22%)
  Pallas kernels  20.9 us (20%)
  between operations  15.4 us (14%)
  starting transfers between devices  10.2 us (10%)
  local copies, waits for them, and re-layouts  3.71 us (3%)
    all_to_all x1, blocking collectives, body(): lax.all_to_all(chunks, ('fy', 'fp'), split_axis=0, concat_axis=0, tiled=T...  23.2 us
    all_to_all x1, waiting for transfers between devices, body(): lax.all_to_all(spread, ('fy', 'fp'), split_axis=0, concat_axis=0, tiled=T...  18.3 us
    pallas_call x1, Pallas kernels, project(): pl.pallas_call(projection_kernel, out_shape=jax.ShapeDtypeStruct((rows, w...  11.8 us
    ppermute x1, waiting for transfers between devices, passed_along(): lax.ppermute(value, axis, [(source, source + steps) for source in range(i...  7.66 us
    all_to_all x1, waiting for transfers between devices, body(): lax.all_to_all(total, 'fp', split_axis=0, concat_axis=0, tiled=True)  5.96 us
    all_to_all x1, starting transfers between devices, body(): lax.all_to_all(spread, ('fy', 'fp'), split_axis=0, concat_axis=0, tiled=T...  5.08 us
    pallas_call x1, Pallas kernels, attend(): pl.pallas_call(attention_kernel, out_shape=jax.ShapeDtypeStruct((outer *...  4.87 us
    all_to_all x1, starting transfers between devices, body(): lax.all_to_all(total, 'fp', split_axis=0, concat_axis=0, tiled=True)  3.82 us
  transfers between devices with their start and end apart: 4, of which 3 were waited for; matrix products, arithmetic and copies ran while one was open for 1% of the time, Pallas kernels for 7%

profile of v8, /device:TPU:1, one launch (start us, length us, event | category | flops | bytes accessed | tf_op | source)
XLA Modules:
  0.0 106.0 jit_solution(10690998985047779966)
XLA Ops:
  6.5 0.0 copy-start
  6.5 0.0 all-gather.2.cloned.1.call-start
  6.5 0.7 all-gather.2.cloned.1.call-update
  7.3 2.2 %shard_map.55 = bf16[16,3,64,128]{3,2,1,0:T(8,128)(2,1)} custom-call(bf16[3,64,2048]{2,1,0:T(8,128)(2,1)} %bitcast.7), custom_call_target="tpu_custom_call" | custom-call | tf_op jit(solution)/shard_map/pallas_call | solution.py:88
  9.4 0.0 copy-start.5
  9.4 23.2 %all_to_all.15.qkv_ref = bf16[16,3,64,128]{3,2,1,0:T(8,128)(2,1)S(1)} all-to-all(bf16[16,3,64,128]{3,2,1,0:T(8,128)(2,1)} %shard_map.55), channel_id=1, replica_groups=mesh['tm'=32,'fy'=4,'fp'=4] {'fy','fp'}, dimensions={0} | all-to-all | bytes 1572864 | tf_op jit(solution)/shard_map/all_to_all | solution.py:166
  32.7 0.0 copy-start.1
  32.7 1.3 %collective-permute-start = (bf16[12,2,64,128]{3,2,1,0:T(8,128)(2,1)S(1)}, bf16[12,2,64,128]{3,2,1,0:T(8,128)(2,1)S(1)}, u32[]{:S(2)}, u32[]{:S(2)}) collective-permute-start(bf16[12,2,64,128]{3,2,1,0:T(8,128)(2,1)S(1)} %slice.4), channel_id=1, source_target_pairs={{0,16},{16,32},{32,48},{48,64},{64,80},{80,96},{96,112},{112,128},... | collective-permute-start | bytes 1179656 | tf_op jit(solution)/shard_map/ppermute | solution.py:16
  34.0 7.7 %collective-permute-done.halo_ref = bf16[12,2,64,128]{3,2,1,0:T(8,128)(2,1)S(1)} collective-permute-done((bf16[12,2,64,128]{3,2,1,0:T(8,128)(2,1)S(1)}, bf16[12,2,64,128]{3,2,1,0:T(8,128)(2,1)S(1)}, u32[]{:S(2)}, u32[]{:S(2)}) %collective-permute-start) | collective-permute-done | bytes 393248 | tf_op jit(solution)/shard_map/ppermute | solution.py:16
  41.7 0.0 copy-start.4
  41.7 0.0 copy-done.1
  41.7 0.7 copy-done.4
  42.4 4.9 %shard_map.56 = bf16[16,256,128]{2,1,0:T(8,128)(2,1)} custom-call(s32[1]{0:T(128)} %bitcast.flag_ref, bf16[16,3,64,128]{3,2,1,0:T(8,128)(2,1)} %copy-done.1, bf16[12,2,64,128]{3,2,1,0:T(8,128)(2,1)} %copy-done.4), custom_call_target="tpu_custom_call" | custom-call | tf_op jit(solution)/shard_map/pallas_call | solution.py:71
  47.3 5.1 %all-to-all-start.1 = ((bf16[16,256,128]{2,1,0:T(8,128)(2,1)}), bf16[16,256,128]{2,1,0:T(8,128)(2,1)S(1)}, u32[]{:S(2)}, u32[]{:S(2)}) async-start(bf16[16,256,128]{2,1,0:T(8,128)(2,1)} %shard_map.56), calls=%async_computation.1 | async-start | bytes 2097152 | tf_op jit(solution)/shard_map/all_to_all | solution.py:171
  52.4 0.0 copy-done.5
  52.4 0.6 dynamic_slice.7
  54.9 18.3 %all-to-all-done.1.gathered_ref = bf16[16,256,128]{2,1,0:T(8,128)(2,1)S(1)} async-done(((bf16[16,256,128]{2,1,0:T(8,128)(2,1)}), bf16[16,256,128]{2,1,0:T(8,128)(2,1)S(1)}, u32[]{:S(2)}, u32[]{:S(2)}) %all-to-all-start.1) | async-done | bytes 1048608 | tf_op jit(solution)/shard_map/all_to_all | solution.py:171
  73.2 0.0 copy-start.2
  73.2 0.0 all-gather.2.cloned.1.call-done
  73.2 1.0 copy-done.2
  74.2 11.8 %shard_map.57 = bf16[256,768]{1,0:T(8,128)(2,1)} custom-call(bf16[16,256,128]{2,1,0:T(8,128)(2,1)} %copy-done.2, bf16[768,2048]{1,0:T(8,128)(2,1)} %bitcast.5), custom_call_target="tpu_custom_call" | custom-call | tf_op jit(solution)/shard_map/pallas_call | solution.py:118
  86.0 3.8 %all-to-all-start.2 = ((bf16[4,64,768]{2,1,0:T(8,128)(2,1)}), bf16[4,64,768]{2,1,0:T(8,128)(2,1)S(1)}, u32[]{:S(2)}, u32[]{:S(2)}) async-start(bf16[4,64,768]{2,1,0:T(8,128)(2,1)} %bitcast.6), calls=%async_computation.2 | async-start | bytes 786432 | tf_op jit(solution)/shard_map/all_to_all | solution.py:174
  89.8 0.0 copy-done
  89.8 0.6 constant_dynamic-slice_fusion.gate_ref
  90.4 6.0 %all-to-all-done.2.returned_ref = bf16[4,64,768]{2,1,0:T(8,128)(2,1)S(1)} async-done(((bf16[4,64,768]{2,1,0:T(8,128)(2,1)}), bf16[4,64,768]{2,1,0:T(8,128)(2,1)S(1)}, u32[]{:S(2)}, u32[]{:S(2)}) %all-to-all-start.2) | async-done | bytes 393248 | tf_op jit(solution)/shard_map/all_to_all | solution.py:174
  96.4 0.0 copy-start.3
  96.4 0.7 copy-done.3
  97.1 2.1 %shard_map.58 = bf16[64,3072]{1,0:T(8,128)(2,1)} custom-call(bf16[4,64,768]{2,1,0:T(8,128)(2,1)} %copy-done.3, bf16[64,3072]{1,0:T(8,128)(2,1)} %latents_ref.1, f32[1,3072]{1,0:T(1,128)} %constant_dynamic-slice_fusion.gate_ref), custom_call_target="tpu_custom_call" | custom-call | tf_op jit(solution)/shard_map/pallas_call | solution.py:147
  (1 shorter events, 0.0 us)
Async XLA Ops:
  6.5 83.3 %copy-start = (f32[40,3072]{1,0:T(8,128)S(1)}, f32[40,3072]{1,0:T(8,128)}, u32[]{:S(2)}) copy-start(f32[40,3072]{1,0:T(8,128)} %param.8) | copy-start | bytes 1474564
  6.5 66.7 %all-gather.2.cloned.1.call-start = ((), (), s32[]{:S(2)}) async-start(), calls=%async_computation.3 | async-start | bytes 3932160 | tf_op jit(solution)/shard_map/all_gather | solution.py:163
  9.4 43.0 %copy-start.5 = (s32[4]{0:T(128)S(1)}, s32[4]{0:T(128)}, u32[]{:S(2)}) copy-start(s32[4]{0:T(128)} %param.9) | copy-start | bytes 52
  32.7 9.0 %copy-start.1 = (bf16[16,3,64,128]{3,2,1,0:T(8,128)(2,1)}, bf16[16,3,64,128]{3,2,1,0:T(8,128)(2,1)S(1)}, u32[]{:S(2)}) copy-start(bf16[16,3,64,128]{3,2,1,0:T(8,128)(2,1)S(1)} %all_to_all.15.qkv_ref) | copy-start | bytes 2359300
  32.7 9.0 %collective-permute-start = (bf16[12,2,64,128]{3,2,1,0:T(8,128)(2,1)S(1)}, bf16[12,2,64,128]{3,2,1,0:T(8,128)(2,1)S(1)}, u32[]{:S(2)}, u32[]{:S(2)}) collective-permute-start(bf16[12,2,64,128]{3,2,1,0:T(8,128)(2,1)S(1)} %slice.4), channel_id=1, source_target_pairs={{0,16},{16,32},{32,48},{48,64},{64,80},{80,96},{96,112},{112,128},... | collective-permute-start | bytes 1179656 | tf_op jit(solution)/shard_map/ppermute | solution.py:16
  41.7 0.7 copy-start.4
  47.3 25.9 %all-to-all-start.1 = ((bf16[16,256,128]{2,1,0:T(8,128)(2,1)}), bf16[16,256,128]{2,1,0:T(8,128)(2,1)S(1)}, u32[]{:S(2)}, u32[]{:S(2)}) async-start(bf16[16,256,128]{2,1,0:T(8,128)(2,1)} %shard_map.56), calls=%async_computation.1 | async-start | bytes 2097152 | tf_op jit(solution)/shard_map/all_to_all | solution.py:171
  73.2 1.0 copy-start.2
  86.0 10.4 %all-to-all-start.2 = ((bf16[4,64,768]{2,1,0:T(8,128)(2,1)}), bf16[4,64,768]{2,1,0:T(8,128)(2,1)S(1)}, u32[]{:S(2)}, u32[]{:S(2)}) async-start(bf16[4,64,768]{2,1,0:T(8,128)(2,1)} %bitcast.6), calls=%async_computation.2 | async-start | bytes 786432 | tf_op jit(solution)/shard_map/all_to_all | solution.py:174
  96.4 0.7 copy-start.3
Sparse Core Ops, SparseCore 0:
  9.5 62.9 all-gather.1

commit v9 on v8

--- a/solution.py
+++ b/solution.py
@@ -93,38 +93,33 @@
     )(planes)
 
 
-def projection_kernel(gathered_ref, weight_ref, out_ref, total_ref):
-    head = pl.program_id(0)
-    part = lax.dot_general(
-        gathered_ref[0], weight_ref[...], (((1,), (1,)), ((), ())), preferred_element_type=jnp.float32
-    )
-
-    @pl.when(head == 0)
-    def _():
-        total_ref[...] = part
-
-    @pl.when(head > 0)
-    def _():
-        total_ref[...] += part
-
-    @pl.when(head == pl.num_programs(0) - 1)
-    def _():
-        out_ref[...] = total_ref[...].astype(out_ref.dtype)
+def projection_kernel(gathered_ref, weight_ref, out_ref):
+    heads, head_dim = gathered_ref.shape[0], gathered_ref.shape[2]
+    total = None
+    for head in range(heads):
+        part = lax.dot_general(
+            gathered_ref[head],
+            weight_ref[:, head * head_dim : (head + 1) * head_dim],
+            (((1,), (1,)), ((), ())),
+            preferred_element_type=jnp.float32,
+        )
+        total = part if total is None else total + part
+    out_ref[...] = total.astype(out_ref.dtype)
 
 
 def project(gathered, weight_t):
     heads, rows, head_dim = gathered.shape
-    width = weight_t.shape[0]
+    width, depth = weight_t.shape
+    step = 128
     return pl.pallas_call(
         projection_kernel,
         out_shape=jax.ShapeDtypeStruct((rows, width), jnp.bfloat16),
-        grid=(heads,),
+        grid=(width // step,),
         in_specs=[
-            pl.BlockSpec((1, rows, head_dim), lambda h: (h, 0, 0)),
-            pl.BlockSpec((width, head_dim), lambda h: (0, h)),
+            pl.BlockSpec((heads, rows, head_dim), lambda n: (0, 0, 0)),
+            pl.BlockSpec((step, depth), lambda n: (n, 0)),
         ],
-        out_specs=pl.BlockSpec((rows, width), lambda h: (0, 0)),
-        scratch_shapes=[pltpu.VMEM((rows, width), jnp.float32)],
+        out_specs=pl.BlockSpec((rows, step), lambda n: (0, n)),
     )(gathered, weight_t)
 
 

time: 107 us -> 101 us (0.944)
  Pallas kernels: 20.9 us -> 15.2 us
    pallas_call x1, Pallas kernels: 11.8 us -> 6.14 us  [project(): pl.pallas_call(projection_kernel, out_shape=jax.ShapeDtypeStruct((rows, w...]
where the time goes in v9:
time: 101 us; the launch traced here: 100 us
  waiting for transfers between devices  32.6 us (32%)
  blocking collectives  23.2 us (23%)
  between operations  15.4 us (15%)
  Pallas kernels  15.2 us (15%)
  starting transfers between devices  10.2 us (10%)
  local copies, waits for them, and re-layouts  3.71 us (4%)
    all_to_all x1, blocking collectives, body(): lax.all_to_all(chunks, ('fy', 'fp'), split_axis=0, concat_axis=0, tiled=T...  23.2 us
    all_to_all x1, waiting for transfers between devices, body(): lax.all_to_all(spread, ('fy', 'fp'), split_axis=0, concat_axis=0, tiled=T...  18.3 us
    ppermute x1, waiting for transfers between devices, passed_along(): lax.ppermute(value, axis, [(source, source + steps) for source in range(i...  7.66 us
    pallas_call x1, Pallas kernels, project(): pl.pallas_call(projection_kernel, out_shape=jax.ShapeDtypeStruct((rows, w...  6.14 us
    all_to_all x1, waiting for transfers between devices, body(): lax.all_to_all(total, 'fp', split_axis=0, concat_axis=0, tiled=True)  5.96 us
    all_to_all x1, starting transfers between devices, body(): lax.all_to_all(spread, ('fy', 'fp'), split_axis=0, concat_axis=0, tiled=T...  5.08 us
    pallas_call x1, Pallas kernels, attend(): pl.pallas_call(attention_kernel, out_shape=jax.ShapeDtypeStruct((outer *...  4.87 us
    all_to_all x1, starting transfers between devices, body(): lax.all_to_all(total, 'fp', split_axis=0, concat_axis=0, tiled=True)  3.83 us
  transfers between devices with their start and end apart: 4, of which 3 were waited for; matrix products, arithmetic and copies ran while one was open for 1% of the time, Pallas kernels for 7%

profile of v9, /device:TPU:1, one launch (start us, length us, event | category | flops | bytes accessed | tf_op | source)
XLA Modules:
  0.0 100.4 jit_solution(13868086520863063469)
XLA Ops:
  6.5 0.0 copy-start
  6.5 0.0 all-gather.2.cloned.1.call-start
  6.5 0.7 all-gather.2.cloned.1.call-update
  7.3 2.2 %shard_map.55 = bf16[16,3,64,128]{3,2,1,0:T(8,128)(2,1)} custom-call(bf16[3,64,2048]{2,1,0:T(8,128)(2,1)} %bitcast.7), custom_call_target="tpu_custom_call" | custom-call | tf_op jit(solution)/shard_map/pallas_call | solution.py:88
  9.4 0.0 copy-start.5
  9.4 23.2 %all_to_all.15.qkv_ref = bf16[16,3,64,128]{3,2,1,0:T(8,128)(2,1)S(1)} all-to-all(bf16[16,3,64,128]{3,2,1,0:T(8,128)(2,1)} %shard_map.55), channel_id=1, replica_groups=mesh['tm'=32,'fy'=4,'fp'=4] {'fy','fp'}, dimensions={0} | all-to-all | bytes 1572864 | tf_op jit(solution)/shard_map/all_to_all | solution.py:161
  32.7 0.0 copy-start.1
  32.7 1.3 %collective-permute-start = (bf16[12,2,64,128]{3,2,1,0:T(8,128)(2,1)S(1)}, bf16[12,2,64,128]{3,2,1,0:T(8,128)(2,1)S(1)}, u32[]{:S(2)}, u32[]{:S(2)}) collective-permute-start(bf16[12,2,64,128]{3,2,1,0:T(8,128)(2,1)S(1)} %slice.4), channel_id=1, source_target_pairs={{0,16},{16,32},{32,48},{48,64},{64,80},{80,96},{96,112},{112,128},... | collective-permute-start | bytes 1179656 | tf_op jit(solution)/shard_map/ppermute | solution.py:16
  34.0 7.7 %collective-permute-done.halo_ref = bf16[12,2,64,128]{3,2,1,0:T(8,128)(2,1)S(1)} collective-permute-done((bf16[12,2,64,128]{3,2,1,0:T(8,128)(2,1)S(1)}, bf16[12,2,64,128]{3,2,1,0:T(8,128)(2,1)S(1)}, u32[]{:S(2)}, u32[]{:S(2)}) %collective-permute-start) | collective-permute-done | bytes 393248 | tf_op jit(solution)/shard_map/ppermute | solution.py:16
  41.7 0.0 copy-start.4
  41.7 0.0 copy-done.1
  41.7 0.7 copy-done.4
  42.4 4.9 %shard_map.56 = bf16[16,256,128]{2,1,0:T(8,128)(2,1)} custom-call(s32[1]{0:T(128)} %bitcast.flag_ref, bf16[16,3,64,128]{3,2,1,0:T(8,128)(2,1)} %copy-done.1, bf16[12,2,64,128]{3,2,1,0:T(8,128)(2,1)} %copy-done.4), custom_call_target="tpu_custom_call" | custom-call | tf_op jit(solution)/shard_map/pallas_call | solution.py:71
  47.3 5.1 %all-to-all-start.1 = ((bf16[16,256,128]{2,1,0:T(8,128)(2,1)}), bf16[16,256,128]{2,1,0:T(8,128)(2,1)S(1)}, u32[]{:S(2)}, u32[]{:S(2)}) async-start(bf16[16,256,128]{2,1,0:T(8,128)(2,1)} %shard_map.56), calls=%async_computation.1 | async-start | bytes 2097152 | tf_op jit(solution)/shard_map/all_to_all | solution.py:166
  52.4 0.0 copy-done.5
  52.4 0.6 dynamic_slice.7
  54.9 18.3 %all-to-all-done.1.gathered_ref = bf16[16,256,128]{2,1,0:T(8,128)(2,1)S(1)} async-done(((bf16[16,256,128]{2,1,0:T(8,128)(2,1)}), bf16[16,256,128]{2,1,0:T(8,128)(2,1)S(1)}, u32[]{:S(2)}, u32[]{:S(2)}) %all-to-all-start.1) | async-done | bytes 1048608 | tf_op jit(solution)/shard_map/all_to_all | solution.py:166
  73.2 0.0 copy-start.2
  73.2 0.0 all-gather.2.cloned.1.call-done
  73.2 1.0 copy-done.2
  74.2 6.1 %shard_map.57 = bf16[256,768]{1,0:T(8,128)(2,1)} custom-call(bf16[16,256,128]{2,1,0:T(8,128)(2,1)} %copy-done.2, bf16[768,2048]{1,0:T(8,128)(2,1)} %bitcast.5), custom_call_target="tpu_custom_call" | custom-call | tf_op jit(solution)/shard_map/pallas_call | solution.py:114
  80.4 3.8 %all-to-all-start.2 = ((bf16[4,64,768]{2,1,0:T(8,128)(2,1)}), bf16[4,64,768]{2,1,0:T(8,128)(2,1)S(1)}, u32[]{:S(2)}, u32[]{:S(2)}) async-start(bf16[4,64,768]{2,1,0:T(8,128)(2,1)} %bitcast.6), calls=%async_computation.2 | async-start | bytes 786432 | tf_op jit(solution)/shard_map/all_to_all | solution.py:169
  84.2 0.0 copy-done
  84.2 0.6 constant_dynamic-slice_fusion.gate_ref
  84.8 6.0 %all-to-all-done.2.returned_ref = bf16[4,64,768]{2,1,0:T(8,128)(2,1)S(1)} async-done(((bf16[4,64,768]{2,1,0:T(8,128)(2,1)}), bf16[4,64,768]{2,1,0:T(8,128)(2,1)S(1)}, u32[]{:S(2)}, u32[]{:S(2)}) %all-to-all-start.2) | async-done | bytes 393248 | tf_op jit(solution)/shard_map/all_to_all | solution.py:169
  90.8 0.0 copy-start.3
  90.8 0.7 copy-done.3
  91.5 2.1 %shard_map.58 = bf16[64,3072]{1,0:T(8,128)(2,1)} custom-call(bf16[4,64,768]{2,1,0:T(8,128)(2,1)} %copy-done.3, bf16[64,3072]{1,0:T(8,128)(2,1)} %latents_ref.1, f32[1,3072]{1,0:T(1,128)} %constant_dynamic-slice_fusion.gate_ref), custom_call_target="tpu_custom_call" | custom-call | tf_op jit(solution)/shard_map/pallas_call | solution.py:142
  (1 shorter events, 0.0 us)
Async XLA Ops:
  6.5 77.7 %copy-start = (f32[40,3072]{1,0:T(8,128)S(1)}, f32[40,3072]{1,0:T(8,128)}, u32[]{:S(2)}) copy-start(f32[40,3072]{1,0:T(8,128)} %param.8) | copy-start | bytes 1474564
  6.5 66.7 %all-gather.2.cloned.1.call-start = ((), (), s32[]{:S(2)}) async-start(), calls=%async_computation.3 | async-start | bytes 3932160 | tf_op jit(solution)/shard_map/all_gather | solution.py:158
  9.4 43.0 %copy-start.5 = (s32[4]{0:T(128)S(1)}, s32[4]{0:T(128)}, u32[]{:S(2)}) copy-start(s32[4]{0:T(128)} %param.9) | copy-start | bytes 52
  32.7 9.0 %copy-start.1 = (bf16[16,3,64,128]{3,2,1,0:T(8,128)(2,1)}, bf16[16,3,64,128]{3,2,1,0:T(8,128)(2,1)S(1)}, u32[]{:S(2)}) copy-start(bf16[16,3,64,128]{3,2,1,0:T(8,128)(2,1)S(1)} %all_to_all.15.qkv_ref) | copy-start | bytes 2359300
  32.7 9.0 %collective-permute-start = (bf16[12,2,64,128]{3,2,1,0:T(8,128)(2,1)S(1)}, bf16[12,2,64,128]{3,2,1,0:T(8,128)(2,1)S(1)}, u32[]{:S(2)}, u32[]{:S(2)}) collective-permute-start(bf16[12,2,64,128]{3,2,1,0:T(8,128)(2,1)S(1)} %slice.4), channel_id=1, source_target_pairs={{0,16},{16,32},{32,48},{48,64},{64,80},{80,96},{96,112},{112,128},... | collective-permute-start | bytes 1179656 | tf_op jit(solution)/shard_map/ppermute | solution.py:16
  41.7 0.7 copy-start.4
  47.3 25.9 %all-to-all-start.1 = ((bf16[16,256,128]{2,1,0:T(8,128)(2,1)}), bf16[16,256,128]{2,1,0:T(8,128)(2,1)S(1)}, u32[]{:S(2)}, u32[]{:S(2)}) async-start(bf16[16,256,128]{2,1,0:T(8,128)(2,1)} %shard_map.56), calls=%async_computation.1 | async-start | bytes 2097152 | tf_op jit(solution)/shard_map/all_to_all | solution.py:166
  73.2 1.0 copy-start.2
  80.4 10.4 %all-to-all-start.2 = ((bf16[4,64,768]{2,1,0:T(8,128)(2,1)}), bf16[4,64,768]{2,1,0:T(8,128)(2,1)S(1)}, u32[]{:S(2)}, u32[]{:S(2)}) async-start(bf16[4,64,768]{2,1,0:T(8,128)(2,1)} %bitcast.6), calls=%async_computation.2 | async-start | bytes 786432 | tf_op jit(solution)/shard_map/all_to_all | solution.py:169
  90.8 0.7 copy-start.3
Sparse Core Ops, SparseCore 0:
  9.5 62.9 all-gather.1

commit v10 on v9

--- a/solution.py
+++ b/solution.py
@@ -108,18 +108,12 @@
 
 
 def project(gathered, weight_t):
-    heads, rows, head_dim = gathered.shape
-    width, depth = weight_t.shape
-    step = 128
+    vmem = pl.BlockSpec(memory_space=pltpu.VMEM)
     return pl.pallas_call(
         projection_kernel,
-        out_shape=jax.ShapeDtypeStruct((rows, width), jnp.bfloat16),
-        grid=(width // step,),
-        in_specs=[
-            pl.BlockSpec((heads, rows, head_dim), lambda n: (0, 0, 0)),
-            pl.BlockSpec((step, depth), lambda n: (n, 0)),
-        ],
-        out_specs=pl.BlockSpec((rows, step), lambda n: (0, n)),
+        out_shape=jax.ShapeDtypeStruct((gathered.shape[1], weight_t.shape[0]), jnp.bfloat16),
+        in_specs=[vmem, vmem],
+        out_specs=vmem,
     )(gathered, weight_t)
 
 
@@ -155,10 +149,17 @@
     per_frame = FRAME_TOK // row_count
     shard = lax.axis_index("fy") * inner + lax.axis_index("fp")
 
-    columns = lax.all_gather(out_weight, "fy", axis=1, tiled=True)
-
     chunks = head_chunks(jnp.transpose(projected, (1, 0, 2)), heads)
     qkv = lax.all_to_all(chunks, ("fy", "fp"), split_axis=0, concat_axis=0, tiled=True)
+    qkv, own_weight = lax.optimization_barrier((qkv, out_weight))
+    shards = [own_weight]
+    for shift in range(1, outer):
+        pairs = [(source, (source + shift) % outer) for source in range(outer)]
+        shards.append(lax.ppermute(own_weight, "fy", pairs))
+    me_outer = lax.axis_index("fy")
+    order = (me_outer - jnp.arange(outer, dtype=jnp.int32)) % outer
+    columns = jnp.stack(shards)[order]
+    columns = jnp.transpose(columns, (1, 0, 2)).reshape(out_weight.shape[0], -1)
     halo = passed_along(qkv[per_frame:, 1:3], "tm", 1)
     flag = (lax.axis_index("tm") > 0).astype(jnp.int32).reshape(1)
     spread = attend(flag, qkv, halo, outer, inner)

time: 101 us -> 104 us (1.030)
  between operations: 15.4 us -> 2.05 us
  starting transfers between devices: 10.2 us -> 22 us
  local copies, waits for them, and re-layouts: 3.71 us -> 8.78 us
  other arithmetic: 0 us -> 3.01 us
  waiting for transfers between devices: 32.6 us -> 30.4 us
  Pallas kernels: 15.2 us -> 14 us
    ppermute x0 -> x3, waiting for transfers between devices: none -> 24.4 us  [body(): shards.append(lax.ppermute(own_weight, 'fy', pairs))]
    all_to_all x1, waiting for transfers between devices: 18.3 us -> 0.01 us  [body(): lax.all_to_all(spread, ('fy', 'fp'), split_axis=0, concat_axis=0, tiled=T...]
    ppermute x0 -> x3, starting transfers between devices: none -> 8.95 us  [body(): shards.append(lax.ppermute(own_weight, 'fy', pairs))]
    ppermute x1, waiting for transfers between devices: 7.66 us -> 0.01 us  [passed_along(): lax.ppermute(value, axis, [(source, source + steps) for source in range(i...]
    gather x0 -> x1, local copies, waits for them, and re-layouts: none -> 4.3 us  [body(): columns = jnp.stack(shards)[order]]
    another operation x0 -> x1, other arithmetic: none -> 2.99 us  [body(): columns = jnp.stack(shards)[order]]
    all_to_all x1, starting transfers between devices: 3.83 us -> 6.34 us  [body(): lax.all_to_all(total, 'fp', split_axis=0, concat_axis=0, tiled=True)]
    pallas_call x1, Pallas kernels: 6.14 us -> 4.75 us  [project(): pl.pallas_call(projection_kernel, out_shape=jax.ShapeDtypeStruct((gathere...]
  transfers between devices with their start and end apart: 4 -> 6, of which waited for: 3 -> 3; matrix products, arithmetic and copies ran while one was open for 1% -> 8% of each run, Pallas kernels for 7% -> 5%
where the time goes in v10:
time: 104 us; the launch traced here: 103 us
  waiting for transfers between devices  30.4 us (29%)
  blocking collectives  23.2 us (22%)
  starting transfers between devices  22 us (21%)
  Pallas kernels  14 us (13%)
  local copies, waits for them, and re-layouts  8.78 us (8%)
  other arithmetic  3.01 us (3%)
  between operations  2.05 us (2%)
    ppermute x3, waiting for transfers between devices, body(): shards.append(lax.ppermute(own_weight, 'fy', pairs))  24.4 us
    all_to_all x1, blocking collectives, body(): lax.all_to_all(chunks, ('fy', 'fp'), split_axis=0, concat_axis=0, tiled=T...  23.2 us
    ppermute x3, starting transfers between devices, body(): shards.append(lax.ppermute(own_weight, 'fy', pairs))  8.95 us
    all_to_all x1, starting transfers between devices, body(): lax.all_to_all(total, 'fp', split_axis=0, concat_axis=0, tiled=True)  6.34 us
    all_to_all x1, waiting for transfers between devices, body(): lax.all_to_all(total, 'fp', split_axis=0, concat_axis=0, tiled=True)  5.97 us
    all_to_all x1, starting transfers between devices, body(): lax.all_to_all(spread, ('fy', 'fp'), split_axis=0, concat_axis=0, tiled=T...  5.43 us
    pallas_call x1, Pallas kernels, attend(): pl.pallas_call(attention_kernel, out_shape=jax.ShapeDtypeStruct((outer *...  4.87 us
    pallas_call x1, Pallas kernels, project(): pl.pallas_call(projection_kernel, out_shape=jax.ShapeDtypeStruct((gathere...  4.75 us
  transfers between devices with their start and end apart: 6, of which 3 were waited for; matrix products, arithmetic and copies ran while one was open for 8% of the time, Pallas kernels for 5%

profile of v10, /device:TPU:1, one launch (start us, length us, event | category | flops | bytes accessed | tf_op | source)
XLA Modules:
  0.0 103.5 jit_solution(3249383661710823190)
XLA Ops:
  0.0 0.0 copy-start
  0.0 0.0 copy-start.4
  0.0 2.3 %shard_map.55 = bf16[16,3,64,128]{3,2,1,0:T(8,128)(2,1)} custom-call(bf16[3,64,2048]{2,1,0:T(8,128)(2,1)} %bitcast.19), custom_call_target="tpu_custom_call" | custom-call | tf_op jit(solution)/shard_map/pallas_call | solution.py:88
  2.3 0.0 copy-start.6
  2.3 23.2 %all_to_all.15.qkv_ref = bf16[16,3,64,128]{3,2,1,0:T(8,128)(2,1)S(1)} all-to-all(bf16[16,3,64,128]{3,2,1,0:T(8,128)(2,1)} %shard_map.55), channel_id=1, replica_groups=mesh['tm'=32,'fy'=4,'fp'=4] {'fy','fp'}, dimensions={0} | all-to-all | bytes 1572864 | tf_op jit(solution)/shard_map/all_to_all | solution.py:153
  25.5 0.0 copy-start.1
  25.5 0.8 slice.3
  26.3 1.3 %collective-permute-start = (bf16[12,2,64,128]{3,2,1,0:T(8,128)(2,1)}, bf16[12,2,64,128]{3,2,1,0:T(8,128)(2,1)S(1)}, u32[]{:S(2)}, u32[]{:S(2)}) collective-permute-start(bf16[12,2,64,128]{3,2,1,0:T(8,128)(2,1)} %slice.3), channel_id=1, source_target_pairs={{0,16},{16,32},{32,48},{48,64},{64,80},{80,96},{96,112},{112,128},... | collective-permute-start | bytes 1179656 | tf_op jit(solution)/shard_map/ppermute | solution.py:16
  27.7 0.0 copy-done.4
  27.7 2.2 %collective-permute-start.1 = (bf16[2048,192]{0,1:T(8,128)(2,1)S(1)}, bf16[2048,192]{0,1:T(8,128)(2,1)S(1)}, u32[]{:S(2)}, u32[]{:S(2)}) collective-permute-start(bf16[2048,192]{0,1:T(8,128)(2,1)S(1)} %copy-done.4), channel_id=1, source_target_pairs={{0,4},{4,8},{8,12},{12,0},{1,5},{5,9},{9,13},{13,1},{2,6},{6,10},{... | collective-permute-start | bytes 2359304 | tf_op jit(solution)/shard_map/ppermute | solution.py:158
  29.9 3.6 %collective-permute-start.2 = (bf16[2048,192]{0,1:T(8,128)(2,1)S(1)}, bf16[2048,192]{0,1:T(8,128)(2,1)}, u32[]{:S(2)}, u32[]{:S(2)}) collective-permute-start(bf16[2048,192]{0,1:T(8,128)(2,1)S(1)} %copy-done.4), channel_id=1, source_target_pairs={{0,8},{4,12},{8,0},{12,4},{1,9},{5,13},{9,1},{13,5},{2,10},{6,14},... | collective-permute-start | bytes 2359304 | tf_op jit(solution)/shard_map/ppermute | solution.py:158
  33.6 3.1 %collective-permute-start.3 = (bf16[2048,192]{0,1:T(8,128)(2,1)S(1)}, bf16[2048,192]{0,1:T(8,128)(2,1)}, u32[]{:S(2)}, u32[]{:S(2)}) collective-permute-start(bf16[2048,192]{0,1:T(8,128)(2,1)S(1)} %copy-done.4), channel_id=1, source_target_pairs={{0,12},{4,0},{8,4},{12,8},{1,13},{5,1},{9,5},{13,9},{2,14},{6,2},{... | collective-permute-start | bytes 2359304 | tf_op jit(solution)/shard_map/ppermute | solution.py:158
  36.7 0.0 collective-permute-done.halo_ref
  36.7 0.0 copy-start.5
  36.7 0.0 copy-done.1
  36.7 0.7 copy-done.5
  37.4 4.9 %shard_map.56 = bf16[16,256,128]{2,1,0:T(8,128)(2,1)} custom-call(s32[1]{0:T(128)} %bitcast.flag_ref, bf16[16,3,64,128]{3,2,1,0:T(8,128)(2,1)} %copy-done.1, bf16[12,2,64,128]{3,2,1,0:T(8,128)(2,1)} %copy-done.5), custom_call_target="tpu_custom_call" | custom-call | tf_op jit(solution)/shard_map/pallas_call | solution.py:71
  42.3 5.4 %all-to-all-start.1 = ((bf16[16,256,128]{2,1,0:T(8,128)(2,1)}), bf16[16,256,128]{2,1,0:T(8,128)(2,1)S(1)}, u32[]{:S(2)}, u32[]{:S(2)}) async-start(bf16[16,256,128]{2,1,0:T(8,128)(2,1)} %shard_map.56), calls=%async_computation.1 | async-start | bytes 2097152 | tf_op jit(solution)/shard_map/all_to_all | solution.py:167
  47.7 0.0 copy-done.6
  47.7 0.6 dynamic_slice.7
  50.3 0.0 collective-permute-done.1
  50.3 20.9 %collective-permute-done.2 = bf16[2048,192]{0,1:T(8,128)(2,1)} collective-permute-done((bf16[2048,192]{0,1:T(8,128)(2,1)S(1)}, bf16[2048,192]{0,1:T(8,128)(2,1)}, u32[]{:S(2)}, u32[]{:S(2)}) %collective-permute-start.2) | collective-permute-done | bytes 786464 | tf_op jit(solution)/shard_map/ppermute | solution.py:158
  71.2 3.6 %collective-permute-done.3 = bf16[2048,192]{0,1:T(8,128)(2,1)} collective-permute-done((bf16[2048,192]{0,1:T(8,128)(2,1)S(1)}, bf16[2048,192]{0,1:T(8,128)(2,1)}, u32[]{:S(2)}, u32[]{:S(2)}) %collective-permute-start.3) | collective-permute-done | bytes 786464 | tf_op jit(solution)/shard_map/ppermute | solution.py:158
  74.7 3.0 %pad_maximum_fusion = bf16[4,2048,192]{1,2,0:T(8,128)(2,1)} fusion(bf16[1,2048,192]{1,2,0:T(8,128)(2,1)} %bitcast.5, bf16[1,2048,192]{1,2,0:T(8,128)(2,1)} %bitcast.4, bf16[1,2048,192]{1,2,0:T(8,128)(2,1)S(1)} %bitcast.18, bf16[1,2048,192]{1,2,0:T(8,128)(2,1)S(1)} %bitcast.17), kind=kLoop, calls=%fused_computation.1 | loop fusion | flops 4718592 | bytes 6291456 | tf_op jit(solution)/shard_map/stack | solution.py:161
  77.7 4.3 %gather_fusion = bf16[4,2048,192]{1,2,0:T(8,128)(2,1)} fusion(bf16[4,2048,192]{1,2,0:T(8,128)(2,1)} %pad_maximum_fusion, s32[1024]{0:T(1024)S(1)} %pad_clamp_fusion), kind=kCustom, calls=%fused_computation | custom fusion | bytes 6291472 | tf_op jit(solution)/shard_map/gather | solution.py:161
  82.0 0.0 all-to-all-done.1.gathered_ref
  82.0 0.0 copy-start.2
  82.0 1.0 copy-done.2
  83.0 4.8 %shard_map.57 = bf16[256,768]{1,0:T(8,128)(2,1)} custom-call(bf16[16,256,128]{2,1,0:T(8,128)(2,1)} %copy-done.2, bf16[768,2048]{1,0:T(8,128)(2,1)} %bitcast.15), custom_call_target="tpu_custom_call" | custom-call | tf_op jit(solution)/shard_map/pallas_call | solution.py:112
  87.8 6.3 %all-to-all-start.2 = ((bf16[4,64,768]{2,1,0:T(8,128)(2,1)}), bf16[4,64,768]{2,1,0:T(8,128)(2,1)S(1)}, u32[]{:S(2)}, u32[]{:S(2)}) async-start(bf16[4,64,768]{2,1,0:T(8,128)(2,1)} %bitcast.16), calls=%async_computation.2 | async-start | bytes 786432 | tf_op jit(solution)/shard_map/all_to_all | solution.py:170
  94.1 0.0 copy-done
  94.1 0.6 constant_dynamic-slice_fusion.gate_ref
  94.7 6.0 %all-to-all-done.2.returned_ref = bf16[4,64,768]{2,1,0:T(8,128)(2,1)S(1)} async-done(((bf16[4,64,768]{2,1,0:T(8,128)(2,1)}), bf16[4,64,768]{2,1,0:T(8,128)(2,1)S(1)}, u32[]{:S(2)}, u32[]{:S(2)}) %all-to-all-start.2) | async-done | bytes 393248 | tf_op jit(solution)/shard_map/all_to_all | solution.py:170
  100.7 0.0 copy-start.3
  100.7 0.7 copy-done.3
  101.4 2.1 %shard_map.58 = bf16[64,3072]{1,0:T(8,128)(2,1)} custom-call(bf16[4,64,768]{2,1,0:T(8,128)(2,1)} %copy-done.3, bf16[64,3072]{1,0:T(8,128)(2,1)} %latents_ref.1, f32[1,3072]{1,0:T(1,128)} %constant_dynamic-slice_fusion.gate_ref), custom_call_target="tpu_custom_call" | custom-call | tf_op jit(solution)/shard_map/pallas_call | solution.py:136
  (2 shorter events, 0.0 us)
Async XLA Ops:
  0.0 94.1 %copy-start = (f32[40,3072]{1,0:T(8,128)S(1)}, f32[40,3072]{1,0:T(8,128)}, u32[]{:S(2)}) copy-start(f32[40,3072]{1,0:T(8,128)} %param.8) | copy-start | bytes 1474564
  0.0 27.7 %copy-start.4 = (bf16[2048,192]{0,1:T(8,128)(2,1)S(1)}, bf16[2048,192]{0,1:T(8,128)(2,1)}, u32[]{:S(2)}) copy-start(bf16[2048,192]{0,1:T(8,128)(2,1)} %param.7) | copy-start | bytes 2359300
  2.3 45.4 %copy-start.6 = (s32[4]{0:T(128)S(1)}, s32[4]{0:T(128)}, u32[]{:S(2)}) copy-start(s32[4]{0:T(128)} %param.9) | copy-start | bytes 52
  25.5 11.1 %copy-start.1 = (bf16[16,3,64,128]{3,2,1,0:T(8,128)(2,1)}, bf16[16,3,64,128]{3,2,1,0:T(8,128)(2,1)S(1)}, u32[]{:S(2)}) copy-start(bf16[16,3,64,128]{3,2,1,0:T(8,128)(2,1)S(1)} %all_to_all.15.qkv_ref) | copy-start | bytes 2359300
  26.3 10.3 %collective-permute-start = (bf16[12,2,64,128]{3,2,1,0:T(8,128)(2,1)}, bf16[12,2,64,128]{3,2,1,0:T(8,128)(2,1)S(1)}, u32[]{:S(2)}, u32[]{:S(2)}) collective-permute-start(bf16[12,2,64,128]{3,2,1,0:T(8,128)(2,1)} %slice.3), channel_id=1, source_target_pairs={{0,16},{16,32},{32,48},{48,64},{64,80},{80,96},{96,112},{112,128},... | collective-permute-start | bytes 1179656 | tf_op jit(solution)/shard_map/ppermute | solution.py:16
  27.7 22.6 %collective-permute-start.1 = (bf16[2048,192]{0,1:T(8,128)(2,1)S(1)}, bf16[2048,192]{0,1:T(8,128)(2,1)S(1)}, u32[]{:S(2)}, u32[]{:S(2)}) collective-permute-start(bf16[2048,192]{0,1:T(8,128)(2,1)S(1)} %copy-done.4), channel_id=1, source_target_pairs={{0,4},{4,8},{8,12},{12,0},{1,5},{5,9},{9,13},{13,1},{2,6},{6,10},{... | collective-permute-start | bytes 2359304 | tf_op jit(solution)/shard_map/ppermute | solution.py:158
  29.9 41.3 %collective-permute-start.2 = (bf16[2048,192]{0,1:T(8,128)(2,1)S(1)}, bf16[2048,192]{0,1:T(8,128)(2,1)}, u32[]{:S(2)}, u32[]{:S(2)}) collective-permute-start(bf16[2048,192]{0,1:T(8,128)(2,1)S(1)} %copy-done.4), channel_id=1, source_target_pairs={{0,8},{4,12},{8,0},{12,4},{1,9},{5,13},{9,1},{13,5},{2,10},{6,14},... | collective-permute-start | bytes 2359304 | tf_op jit(solution)/shard_map/ppermute | solution.py:158
  33.6 41.2 %collective-permute-start.3 = (bf16[2048,192]{0,1:T(8,128)(2,1)S(1)}, bf16[2048,192]{0,1:T(8,128)(2,1)}, u32[]{:S(2)}, u32[]{:S(2)}) collective-permute-start(bf16[2048,192]{0,1:T(8,128)(2,1)S(1)} %copy-done.4), channel_id=1, source_target_pairs={{0,12},{4,0},{8,4},{12,8},{1,13},{5,1},{9,5},{13,9},{2,14},{6,2},{... | collective-permute-start | bytes 2359304 | tf_op jit(solution)/shard_map/ppermute | solution.py:158
  36.7 0.7 copy-start.5
  42.3 39.8 %all-to-all-start.1 = ((bf16[16,256,128]{2,1,0:T(8,128)(2,1)}), bf16[16,256,128]{2,1,0:T(8,128)(2,1)S(1)}, u32[]{:S(2)}, u32[]{:S(2)}) async-start(bf16[16,256,128]{2,1,0:T(8,128)(2,1)} %shard_map.56), calls=%async_computation.1 | async-start | bytes 2097152 | tf_op jit(solution)/shard_map/all_to_all | solution.py:167
  82.0 1.0 copy-start.2
  87.8 12.9 %all-to-all-start.2 = ((bf16[4,64,768]{2,1,0:T(8,128)(2,1)}), bf16[4,64,768]{2,1,0:T(8,128)(2,1)S(1)}, u32[]{:S(2)}, u32[]{:S(2)}) async-start(bf16[4,64,768]{2,1,0:T(8,128)(2,1)} %bitcast.16), calls=%async_computation.2 | async-start | bytes 786432 | tf_op jit(solution)/shard_map/all_to_all | solution.py:170
  100.7 0.7 copy-start.3

commit v11 on v10

--- a/solution.py
+++ b/solution.py
@@ -93,40 +93,46 @@
     )(planes)
 
 
-def projection_kernel(gathered_ref, weight_ref, out_ref):
+def projection_kernel(place_ref, gathered_ref, *refs):
+    weight_refs, out_ref = refs[:-1], refs[-1]
     heads, head_dim = gathered_ref.shape[0], gathered_ref.shape[2]
-    total = None
-    for head in range(heads):
-        part = lax.dot_general(
-            gathered_ref[head],
-            weight_ref[:, head * head_dim : (head + 1) * head_dim],
-            (((1,), (1,)), ((), ())),
-            preferred_element_type=jnp.float32,
-        )
-        total = part if total is None else total + part
-    out_ref[...] = total.astype(out_ref.dtype)
+    for shift, weight_ref in enumerate(weight_refs):
+        total = None
+        for head in range(heads):
+            part = lax.dot_general(
+                gathered_ref[head],
+                weight_ref[:, head * head_dim : (head + 1) * head_dim],
+                (((1,), (1,)), ((), ())),
+                preferred_element_type=jnp.float32,
+            )
+            total = part if total is None else total + part
+        total = total.astype(out_ref.dtype)
+        rows = out_ref.shape[2]
+        for group in range(out_ref.shape[0]):
+            out_ref[group, place_ref[shift]] = total[group * rows : (group + 1) * rows]
 
 
-def project(gathered, weight_t):
+def project(place, gathered, weights_t, groups):
     vmem = pl.BlockSpec(memory_space=pltpu.VMEM)
+    count, width = len(weights_t), weights_t[0].shape[0]
+    rows = gathered.shape[1] // groups
     return pl.pallas_call(
         projection_kernel,
-        out_shape=jax.ShapeDtypeStruct((gathered.shape[1], weight_t.shape[0]), jnp.bfloat16),
-        in_specs=[vmem, vmem],
+        out_shape=jax.ShapeDtypeStruct((groups, count, rows, width), jnp.bfloat16),
+        in_specs=[pl.BlockSpec(memory_space=pltpu.SMEM)] + [vmem] * (count + 1),
         out_specs=vmem,
-    )(gathered, weight_t)
+    )(place, gathered, *weights_t)
 
 
 def finish_kernel(returned_ref, latents_ref, gate_ref, out_ref):
-    senders, _, width = returned_ref.shape
-    blocks = gate_ref.shape[1] // (senders * senders)
-    for sender in range(senders):
-        for block in range(width // blocks):
-            column = blocks * (senders * block + sender)
-            branch = returned_ref[sender, :, block * blocks : (block + 1) * blocks]
-            residual = latents_ref[:, column : column + blocks].astype(jnp.float32)
-            gate = gate_ref[:, column : column + blocks]
-            out_ref[:, column : column + blocks] = (
+    senders, blocks, _, width = returned_ref.shape
+    for block in range(blocks):
+        for sender in range(senders):
+            column = width * (senders * block + sender)
+            branch = returned_ref[sender, block]
+            residual = latents_ref[:, column : column + width].astype(jnp.float32)
+            gate = gate_ref[:, column : column + width]
+            out_ref[:, column : column + width] = (
                 residual + gate * branch.astype(jnp.float32)
             ).astype(out_ref.dtype)
 
@@ -157,16 +163,13 @@
         pairs = [(source, (source + shift) % outer) for source in range(outer)]
         shards.append(lax.ppermute(own_weight, "fy", pairs))
     me_outer = lax.axis_index("fy")
-    order = (me_outer - jnp.arange(outer, dtype=jnp.int32)) % outer
-    columns = jnp.stack(shards)[order]
-    columns = jnp.transpose(columns, (1, 0, 2)).reshape(out_weight.shape[0], -1)
+    place = ((me_outer - jnp.arange(outer, dtype=jnp.int32)) % outer).astype(jnp.int32)
     halo = passed_along(qkv[per_frame:, 1:3], "tm", 1)
     flag = (lax.axis_index("tm") > 0).astype(jnp.int32).reshape(1)
     spread = attend(flag, qkv, halo, outer, inner)
 
     gathered = lax.all_to_all(spread, ("fy", "fp"), split_axis=0, concat_axis=0, tiled=True)
-    total = project(gathered, jnp.transpose(columns))
-    total = total.reshape(inner, row_count, total.shape[1])
+    total = project(place, gathered, [jnp.transpose(shard_w) for shard_w in shards], inner)
     returned = lax.all_to_all(total, "fp", split_axis=0, concat_axis=0, tiled=True)
 
     frame_index = (shard * row_count) // FRAME_TOK

time: 104 us -> 119 us (1.14)
  the two profiles are of different devices: /device:TPU:1 before, /device:TPU:256 now
where the time goes in v11:
time: 119 us; the launch traced here: 118 us
  waiting for transfers between devices  53.7 us (45%)
  starting transfers between devices  23.6 us (20%)
  blocking collectives  19.2 us (16%)
  Pallas kernels  14.5 us (12%)
  local copies, waits for them, and re-layouts  4.39 us (4%)
  between operations  2.07 us (2%)
    ppermute x3, waiting for transfers between devices, body(): shards.append(lax.ppermute(own_weight, 'fy', pairs))  34.1 us
    all_to_all x1, blocking collectives, body(): lax.all_to_all(chunks, ('fy', 'fp'), split_axis=0, concat_axis=0, tiled=T...  19.2 us
    ppermute x3, starting transfers between devices, body(): shards.append(lax.ppermute(own_weight, 'fy', pairs))  11.7 us
    ppermute x1, waiting for transfers between devices, passed_along(): lax.ppermute(value, axis, [(source, source + steps) for source in range(i...  11.4 us
    all_to_all x1, waiting for transfers between devices, body(): lax.all_to_all(total, 'fp', split_axis=0, concat_axis=0, tiled=True)  8.18 us
    pallas_call x1, Pallas kernels, project(): pl.pallas_call(projection_kernel, out_shape=jax.ShapeDtypeStruct((groups,...  5.33 us
    pallas_call x1, Pallas kernels, attend(): pl.pallas_call(attention_kernel, out_shape=jax.ShapeDtypeStruct((outer *...  4.86 us
    ppermute x1, starting transfers between devices, passed_along(): lax.ppermute(value, axis, [(source, source + steps) for source in range(i...  4.64 us
  transfers between devices with their start and end apart: 6, of which 4 were waited for; matrix products, arithmetic and copies ran while one was open for 1% of the time, Pallas kernels for 0%

profile of v11, /device:TPU:256, one launch (start us, length us, event | category | flops | bytes accessed | tf_op | source)
XLA Modules:
  0.0 118.0 jit_solution(8476033161890620822)
XLA Ops:
  0.0 0.0 copy-start
  0.0 2.2 %shard_map.55 = bf16[16,3,64,128]{3,2,1,0:T(8,128)(2,1)} custom-call(bf16[3,64,2048]{2,1,0:T(8,128)(2,1)} %bitcast.9), custom_call_target="tpu_custom_call" | custom-call | tf_op jit(solution)/shard_map/pallas_call | solution.py:88
  2.2 19.2 %all_to_all.15.qkv_ref = bf16[16,3,64,128]{3,2,1,0:T(8,128)(2,1)S(1)} all-to-all(bf16[16,3,64,128]{3,2,1,0:T(8,128)(2,1)} %shard_map.55), channel_id=1, replica_groups=mesh['tm'=32,'fy'=4,'fp'=4] {'fy','fp'}, dimensions={0} | all-to-all | bytes 1572864 | tf_op jit(solution)/shard_map/all_to_all | solution.py:159
  21.4 0.0 copy-start.1
  21.4 4.6 %collective-permute-start = (bf16[12,2,64,128]{3,2,1,0:T(8,128)(2,1)S(1)}, bf16[12,2,64,128]{3,2,1,0:T(8,128)(2,1)S(1)}, u32[]{:S(2)}, u32[]{:S(2)}) collective-permute-start(bf16[12,2,64,128]{3,2,1,0:T(8,128)(2,1)S(1)} %slice.3), channel_id=1, source_target_pairs={{0,16},{16,32},{32,48},{48,64},{64,80},{80,96},{96,112},{112,128},... | collective-permute-start | bytes 1179656 | tf_op jit(solution)/shard_map/ppermute | solution.py:16
  26.1 11.4 %collective-permute-done.halo_ref = bf16[12,2,64,128]{3,2,1,0:T(8,128)(2,1)S(1)} collective-permute-done((bf16[12,2,64,128]{3,2,1,0:T(8,128)(2,1)S(1)}, bf16[12,2,64,128]{3,2,1,0:T(8,128)(2,1)S(1)}, u32[]{:S(2)}, u32[]{:S(2)}) %collective-permute-start) | collective-permute-done | bytes 393248 | tf_op jit(solution)/shard_map/ppermute | solution.py:16
  37.5 0.0 copy-start.6
  37.5 0.0 copy-done.1
  37.5 0.7 copy-done.6
  38.2 4.9 %shard_map.56 = bf16[16,256,128]{2,1,0:T(8,128)(2,1)} custom-call(s32[1]{0:T(128)} %bitcast.flag_ref, bf16[16,3,64,128]{3,2,1,0:T(8,128)(2,1)} %copy-done.1, bf16[12,2,64,128]{3,2,1,0:T(8,128)(2,1)} %copy-done.6), custom_call_target="tpu_custom_call" | custom-call | tf_op jit(solution)/shard_map/pallas_call | solution.py:71
  43.1 0.0 copy-start.4
  43.1 3.8 %all-to-all-start.1 = ((bf16[16,256,128]{2,1,0:T(8,128)(2,1)}), bf16[16,256,128]{2,1,0:T(8,128)(2,1)S(1)}, u32[]{:S(2)}, u32[]{:S(2)}) async-start(bf16[16,256,128]{2,1,0:T(8,128)(2,1)} %shard_map.56), calls=%async_computation.1 | async-start | bytes 2097152 | tf_op jit(solution)/shard_map/all_to_all | solution.py:171
  46.9 0.0 copy-done.4
  46.9 3.7 %collective-permute-start.1 = (bf16[2048,192]{0,1:T(8,128)(2,1)S(1)}, bf16[2048,192]{0,1:T(8,128)(2,1)S(1)}, u32[]{:S(2)}, u32[]{:S(2)}) collective-permute-start(bf16[2048,192]{0,1:T(8,128)(2,1)S(1)} %copy-done.4), channel_id=1, source_target_pairs={{0,4},{4,8},{8,12},{12,0},{1,5},{5,9},{9,13},{13,1},{2,6},{6,10},{... | collective-permute-start | bytes 2359304 | tf_op jit(solution)/shard_map/ppermute | solution.py:164
  50.6 4.6 %collective-permute-start.2 = (bf16[2048,192]{0,1:T(8,128)(2,1)S(1)}, bf16[2048,192]{0,1:T(8,128)(2,1)}, u32[]{:S(2)}, u32[]{:S(2)}) collective-permute-start(bf16[2048,192]{0,1:T(8,128)(2,1)S(1)} %copy-done.4), channel_id=1, source_target_pairs={{0,8},{4,12},{8,0},{12,4},{1,9},{5,13},{9,1},{13,5},{2,10},{6,14},... | collective-permute-start | bytes 2359304 | tf_op jit(solution)/shard_map/ppermute | solution.py:164
  55.3 3.3 %collective-permute-start.3 = (bf16[2048,192]{0,1:T(8,128)(2,1)S(1)}, bf16[2048,192]{0,1:T(8,128)(2,1)}, u32[]{:S(2)}, u32[]{:S(2)}) collective-permute-start(bf16[2048,192]{0,1:T(8,128)(2,1)S(1)} %copy-done.4), channel_id=1, source_target_pairs={{0,12},{4,0},{8,4},{12,8},{1,13},{5,1},{9,5},{13,9},{2,14},{6,2},{... | collective-permute-start | bytes 2359304 | tf_op jit(solution)/shard_map/ppermute | solution.py:164
  58.7 0.0 copy-start.7
  58.7 0.6 copy-done.7
  59.3 0.6 dynamic_slice.7
  61.8 0.5 and_select_fusion.place_ref
  62.4 17.1 %collective-permute-done.1 = bf16[2048,192]{0,1:T(8,128)(2,1)S(1)} collective-permute-done((bf16[2048,192]{0,1:T(8,128)(2,1)S(1)}, bf16[2048,192]{0,1:T(8,128)(2,1)S(1)}, u32[]{:S(2)}, u32[]{:S(2)}) %collective-permute-start.1) | collective-permute-done | bytes 786464 | tf_op jit(solution)/shard_map/ppermute | solution.py:164
  79.5 0.0 copy-start.5
  79.5 17.0 %collective-permute-done.2 = bf16[2048,192]{0,1:T(8,128)(2,1)} collective-permute-done((bf16[2048,192]{0,1:T(8,128)(2,1)S(1)}, bf16[2048,192]{0,1:T(8,128)(2,1)}, u32[]{:S(2)}, u32[]{:S(2)}) %collective-permute-start.2) | collective-permute-done | bytes 786464 | tf_op jit(solution)/shard_map/ppermute | solution.py:164
  96.5 0.0 collective-permute-done.3
  96.5 0.0 all-to-all-done.1.gathered_ref
  96.5 0.0 copy-start.2
  96.5 0.0 copy-done.5
  96.5 1.0 copy-done.2
  97.5 5.3 %shard_map.57 = bf16[4,4,64,192]{3,2,1,0:T(8,128)(2,1)} custom-call(s32[4]{0:T(128)} %and_select_fusion.place_ref, bf16[16,256,128]{2,1,0:T(8,128)(2,1)} %copy-done.2, bf16[192,2048]{1,0:T(8,128)(2,1)} %bitcast.7, bf16[192,2048]{1,0:T(8,128)(2,1)} %bitcast.8, bf16[192,2048]{1,0:T(8,128)(2,1)} %bitcast.4.refs_2_, bf16[192,2048]{1,0:T(8,128)(2,1)} %bitcast.5.refs_3_), custom_call_target="tpu_custom_call" | custom-call | tf_op jit(solution)/shard_map/pallas_call | solution.py:119
  102.8 3.5 %all-to-all-start.2 = ((bf16[4,4,64,192]{3,2,1,0:T(8,128)(2,1)}), bf16[4,4,64,192]{3,2,1,0:T(8,128)(2,1)S(1)}, u32[]{:S(2)}, u32[]{:S(2)}) async-start(bf16[4,4,64,192]{3,2,1,0:T(8,128)(2,1)} %shard_map.57), calls=%async_computation.2 | async-start | bytes 1048576 | tf_op jit(solution)/shard_map/all_to_all | solution.py:173
  106.3 0.0 copy-done
  106.3 0.6 constant_dynamic-slice_fusion.gate_ref
  106.9 8.2 %all-to-all-done.2.returned_ref = bf16[4,4,64,192]{3,2,1,0:T(8,128)(2,1)S(1)} async-done(((bf16[4,4,64,192]{3,2,1,0:T(8,128)(2,1)}), bf16[4,4,64,192]{3,2,1,0:T(8,128)(2,1)S(1)}, u32[]{:S(2)}, u32[]{:S(2)}) %all-to-all-start.2) | async-done | bytes 393248 | tf_op jit(solution)/shard_map/all_to_all | solution.py:173
  115.1 0.0 copy-start.3
  115.1 0.8 copy-done.3
  115.9 2.1 %shard_map.58 = bf16[64,3072]{1,0:T(8,128)(2,1)} custom-call(bf16[4,4,64,192]{3,2,1,0:T(8,128)(2,1)} %copy-done.3, bf16[64,3072]{1,0:T(8,128)(2,1)} %latents_ref.1, f32[1,3072]{1,0:T(1,128)} %constant_dynamic-slice_fusion.gate_ref), custom_call_target="tpu_custom_call" | custom-call | tf_op jit(solution)/shard_map/pallas_call | solution.py:142
  (1 shorter events, 0.0 us)
Async XLA Ops:
  0.0 106.3 %copy-start = (f32[40,3072]{1,0:T(8,128)S(1)}, f32[40,3072]{1,0:T(8,128)}, u32[]{:S(2)}) copy-start(f32[40,3072]{1,0:T(8,128)} %param.8) | copy-start | bytes 1474564
  21.4 16.1 %copy-start.1 = (bf16[16,3,64,128]{3,2,1,0:T(8,128)(2,1)}, bf16[16,3,64,128]{3,2,1,0:T(8,128)(2,1)S(1)}, u32[]{:S(2)}) copy-start(bf16[16,3,64,128]{3,2,1,0:T(8,128)(2,1)S(1)} %all_to_all.15.qkv_ref) | copy-start | bytes 2359300
  21.4 16.1 %collective-permute-start = (bf16[12,2,64,128]{3,2,1,0:T(8,128)(2,1)S(1)}, bf16[12,2,64,128]{3,2,1,0:T(8,128)(2,1)S(1)}, u32[]{:S(2)}, u32[]{:S(2)}) collective-permute-start(bf16[12,2,64,128]{3,2,1,0:T(8,128)(2,1)S(1)} %slice.3), channel_id=1, source_target_pairs={{0,16},{16,32},{32,48},{48,64},{64,80},{80,96},{96,112},{112,128},... | collective-permute-start | bytes 1179656 | tf_op jit(solution)/shard_map/ppermute | solution.py:16
  37.5 0.7 copy-start.6
  43.1 3.8 %copy-start.4 = (bf16[2048,192]{0,1:T(8,128)(2,1)S(1)}, bf16[2048,192]{0,1:T(8,128)(2,1)}, u32[]{:S(2)}) copy-start(bf16[2048,192]{0,1:T(8,128)(2,1)} %param.7) | copy-start | bytes 2359300
  43.1 53.4 %all-to-all-start.1 = ((bf16[16,256,128]{2,1,0:T(8,128)(2,1)}), bf16[16,256,128]{2,1,0:T(8,128)(2,1)S(1)}, u32[]{:S(2)}, u32[]{:S(2)}) async-start(bf16[16,256,128]{2,1,0:T(8,128)(2,1)} %shard_map.56), calls=%async_computation.1 | async-start | bytes 2097152 | tf_op jit(solution)/shard_map/all_to_all | solution.py:171
  46.9 32.6 %collective-permute-start.1 = (bf16[2048,192]{0,1:T(8,128)(2,1)S(1)}, bf16[2048,192]{0,1:T(8,128)(2,1)S(1)}, u32[]{:S(2)}, u32[]{:S(2)}) collective-permute-start(bf16[2048,192]{0,1:T(8,128)(2,1)S(1)} %copy-done.4), channel_id=1, source_target_pairs={{0,4},{4,8},{8,12},{12,0},{1,5},{5,9},{9,13},{13,1},{2,6},{6,10},{... | collective-permute-start | bytes 2359304 | tf_op jit(solution)/shard_map/ppermute | solution.py:164
  50.6 45.9 %collective-permute-start.2 = (bf16[2048,192]{0,1:T(8,128)(2,1)S(1)}, bf16[2048,192]{0,1:T(8,128)(2,1)}, u32[]{:S(2)}, u32[]{:S(2)}) collective-permute-start(bf16[2048,192]{0,1:T(8,128)(2,1)S(1)} %copy-done.4), channel_id=1, source_target_pairs={{0,8},{4,12},{8,0},{12,4},{1,9},{5,13},{9,1},{13,5},{2,10},{6,14},... | collective-permute-start | bytes 2359304 | tf_op jit(solution)/shard_map/ppermute | solution.py:164
  55.3 41.2 %collective-permute-start.3 = (bf16[2048,192]{0,1:T(8,128)(2,1)S(1)}, bf16[2048,192]{0,1:T(8,128)(2,1)}, u32[]{:S(2)}, u32[]{:S(2)}) collective-permute-start(bf16[2048,192]{0,1:T(8,128)(2,1)S(1)} %copy-done.4), channel_id=1, source_target_pairs={{0,12},{4,0},{8,4},{12,8},{1,13},{5,1},{9,5},{13,9},{2,14},{6,2},{... | collective-permute-start | bytes 2359304 | tf_op jit(solution)/shard_map/ppermute | solution.py:164
  58.7 0.7 copy-start.7
  79.5 17.0 %copy-start.5 = (bf16[2048,192]{0,1:T(8,128)(2,1)}, bf16[2048,192]{0,1:T(8,128)(2,1)S(1)}, u32[]{:S(2)}) copy-start(bf16[2048,192]{0,1:T(8,128)(2,1)S(1)} %collective-permute-done.1) | copy-start | bytes 2359300
  96.5 1.0 copy-start.2
  102.8 12.3 %all-to-all-start.2 = ((bf16[4,4,64,192]{3,2,1,0:T(8,128)(2,1)}), bf16[4,4,64,192]{3,2,1,0:T(8,128)(2,1)S(1)}, u32[]{:S(2)}, u32[]{:S(2)}) async-start(bf16[4,4,64,192]{3,2,1,0:T(8,128)(2,1)} %shard_map.57), calls=%async_computation.2 | async-start | bytes 1048576 | tf_op jit(solution)/shard_map/all_to_all | solution.py:173
  115.1 0.8 copy-start.3

commit v12 on v11

--- a/solution.py
+++ b/solution.py
@@ -167,6 +167,7 @@
     halo = passed_along(qkv[per_frame:, 1:3], "tm", 1)
     flag = (lax.axis_index("tm") > 0).astype(jnp.int32).reshape(1)
     spread = attend(flag, qkv, halo, outer, inner)
+    spread, *shards = lax.optimization_barrier((spread, *shards))
 
     gathered = lax.all_to_all(spread, ("fy", "fp"), split_axis=0, concat_axis=0, tiled=True)
     total = project(place, gathered, [jnp.transpose(shard_w) for shard_w in shards], inner)

time: 119 us -> 111 us (0.933)
  the two profiles are of different devices: /device:TPU:256 before, /device:TPU:1 now
where the time goes in v12:
time: 111 us; the launch traced here: 110 us
  waiting for transfers between devices  43.7 us (39%)
  blocking collectives  23.2 us (21%)
  starting transfers between devices  20.9 us (19%)
  Pallas kernels  14.5 us (13%)
  local copies, waits for them, and re-layouts  5.14 us (5%)
  between operations  2.01 us (2%)
    all_to_all x1, blocking collectives, body(): lax.all_to_all(chunks, ('fy', 'fp'), split_axis=0, concat_axis=0, tiled=T...  23.2 us
    ppermute x3, waiting for transfers between devices, body(): shards.append(lax.ppermute(own_weight, 'fy', pairs))  16.5 us
    all_to_all x1, waiting for transfers between devices, body(): lax.all_to_all(spread, ('fy', 'fp'), split_axis=0, concat_axis=0, tiled=T...  12.1 us
    ppermute x3, starting transfers between devices, body(): shards.append(lax.ppermute(own_weight, 'fy', pairs))  8.94 us
    ppermute x1, waiting for transfers between devices, passed_along(): lax.ppermute(value, axis, [(source, source + steps) for source in range(i...  7.74 us
    all_to_all x1, waiting for transfers between devices, body(): lax.all_to_all(total, 'fp', split_axis=0, concat_axis=0, tiled=True)  7.37 us
    all_to_all x1, starting transfers between devices, body(): lax.all_to_all(spread, ('fy', 'fp'), split_axis=0, concat_axis=0, tiled=T...  6.39 us
    pallas_call x1, Pallas kernels, project(): pl.pallas_call(projection_kernel, out_shape=jax.ShapeDtypeStruct((groups,...  5.33 us
  transfers between devices with their start and end apart: 6, of which 5 were waited for; matrix products, arithmetic and copies ran while one was open for 2% of the time, Pallas kernels for 4%

profile of v12, /device:TPU:1, one launch (start us, length us, event | category | flops | bytes accessed | tf_op | source)
XLA Modules:
  0.0 110.1 jit_solution(13020946420538568821)
XLA Ops:
  0.0 0.0 copy-start
  0.0 2.2 %shard_map.55 = bf16[16,3,64,128]{3,2,1,0:T(8,128)(2,1)} custom-call(bf16[3,64,2048]{2,1,0:T(8,128)(2,1)} %bitcast.9), custom_call_target="tpu_custom_call" | custom-call | tf_op jit(solution)/shard_map/pallas_call | solution.py:88
  2.2 0.0 copy-start.4
  2.2 23.2 %all_to_all.15.qkv_ref = bf16[16,3,64,128]{3,2,1,0:T(8,128)(2,1)S(1)} all-to-all(bf16[16,3,64,128]{3,2,1,0:T(8,128)(2,1)} %shard_map.55), channel_id=1, replica_groups=mesh['tm'=32,'fy'=4,'fp'=4] {'fy','fp'}, dimensions={0} | all-to-all | bytes 1572864 | tf_op jit(solution)/shard_map/all_to_all | solution.py:159
  25.5 0.0 copy-done.4
  25.5 0.0 copy-start.1
  25.5 2.2 %collective-permute-start.1 = (bf16[2048,192]{0,1:T(8,128)(2,1)S(1)}, bf16[2048,192]{0,1:T(8,128)(2,1)S(1)}, u32[]{:S(2)}, u32[]{:S(2)}) collective-permute-start(bf16[2048,192]{0,1:T(8,128)(2,1)S(1)} %copy-done.4), channel_id=1, source_target_pairs={{0,4},{4,8},{8,12},{12,0},{1,5},{5,9},{9,13},{13,1},{2,6},{6,10},{... | collective-permute-start | bytes 2359304 | tf_op jit(solution)/shard_map/ppermute | solution.py:164
  27.7 3.6 %collective-permute-start.2 = (bf16[2048,192]{0,1:T(8,128)(2,1)S(1)}, bf16[2048,192]{0,1:T(8,128)(2,1)}, u32[]{:S(2)}, u32[]{:S(2)}) collective-permute-start(bf16[2048,192]{0,1:T(8,128)(2,1)S(1)} %copy-done.4), channel_id=1, source_target_pairs={{0,8},{4,12},{8,0},{12,4},{1,9},{5,13},{9,1},{13,5},{2,10},{6,14},... | collective-permute-start | bytes 2359304 | tf_op jit(solution)/shard_map/ppermute | solution.py:164
  31.4 3.1 %collective-permute-start.3 = (bf16[2048,192]{0,1:T(8,128)(2,1)S(1)}, bf16[2048,192]{0,1:T(8,128)(2,1)}, u32[]{:S(2)}, u32[]{:S(2)}) collective-permute-start(bf16[2048,192]{0,1:T(8,128)(2,1)S(1)} %copy-done.4), channel_id=1, source_target_pairs={{0,12},{4,0},{8,4},{12,8},{1,13},{5,1},{9,5},{13,9},{2,14},{6,2},{... | collective-permute-start | bytes 2359304 | tf_op jit(solution)/shard_map/ppermute | solution.py:164
  34.5 0.8 slice.3
  35.2 1.3 %collective-permute-start = (bf16[12,2,64,128]{3,2,1,0:T(8,128)(2,1)}, bf16[12,2,64,128]{3,2,1,0:T(8,128)(2,1)S(1)}, u32[]{:S(2)}, u32[]{:S(2)}) collective-permute-start(bf16[12,2,64,128]{3,2,1,0:T(8,128)(2,1)} %slice.3), channel_id=1, source_target_pairs={{0,16},{16,32},{32,48},{48,64},{64,80},{80,96},{96,112},{112,128},... | collective-permute-start | bytes 1179656 | tf_op jit(solution)/shard_map/ppermute | solution.py:16
  36.5 7.7 %collective-permute-done.halo_ref = bf16[12,2,64,128]{3,2,1,0:T(8,128)(2,1)S(1)} collective-permute-done((bf16[12,2,64,128]{3,2,1,0:T(8,128)(2,1)}, bf16[12,2,64,128]{3,2,1,0:T(8,128)(2,1)S(1)}, u32[]{:S(2)}, u32[]{:S(2)}) %collective-permute-start) | collective-permute-done | bytes 393248 | tf_op jit(solution)/shard_map/ppermute | solution.py:16
  44.3 0.0 copy-start.6
  44.3 0.0 copy-done.1
  44.3 0.7 copy-done.6
  45.0 4.8 %shard_map.56 = bf16[16,256,128]{2,1,0:T(8,128)(2,1)} custom-call(s32[1]{0:T(128)} %bitcast.flag_ref, bf16[16,3,64,128]{3,2,1,0:T(8,128)(2,1)} %copy-done.1, bf16[12,2,64,128]{3,2,1,0:T(8,128)(2,1)} %copy-done.6), custom_call_target="tpu_custom_call" | custom-call | tf_op jit(solution)/shard_map/pallas_call | solution.py:71
  49.9 0.0 collective-permute-done.1
  49.9 0.0 copy-start.5
  49.9 13.5 %collective-permute-done.2 = bf16[2048,192]{0,1:T(8,128)(2,1)} collective-permute-done((bf16[2048,192]{0,1:T(8,128)(2,1)S(1)}, bf16[2048,192]{0,1:T(8,128)(2,1)}, u32[]{:S(2)}, u32[]{:S(2)}) %collective-permute-start.2) | collective-permute-done | bytes 786464 | tf_op jit(solution)/shard_map/ppermute | solution.py:164
  63.4 3.0 %collective-permute-done.3 = bf16[2048,192]{0,1:T(8,128)(2,1)} collective-permute-done((bf16[2048,192]{0,1:T(8,128)(2,1)S(1)}, bf16[2048,192]{0,1:T(8,128)(2,1)}, u32[]{:S(2)}, u32[]{:S(2)}) %collective-permute-start.3) | collective-permute-done | bytes 786464 | tf_op jit(solution)/shard_map/ppermute | solution.py:164
  66.4 0.0 copy-done.5
  66.4 6.4 %all-to-all-start.1 = ((bf16[16,256,128]{2,1,0:T(8,128)(2,1)}), bf16[16,256,128]{2,1,0:T(8,128)(2,1)S(1)}, u32[]{:S(2)}, u32[]{:S(2)}) async-start(bf16[16,256,128]{2,1,0:T(8,128)(2,1)} %shard_map.56), calls=%async_computation.1 | async-start | bytes 2097152 | tf_op jit(solution)/shard_map/all_to_all | solution.py:172
  72.8 0.0 copy-start.7
  72.8 0.6 copy-done.7
  73.4 0.6 dynamic_slice.7
  75.9 0.5 and_select_fusion.place_ref
  76.5 12.1 %all-to-all-done.1.gathered_ref = bf16[16,256,128]{2,1,0:T(8,128)(2,1)S(1)} async-done(((bf16[16,256,128]{2,1,0:T(8,128)(2,1)}), bf16[16,256,128]{2,1,0:T(8,128)(2,1)S(1)}, u32[]{:S(2)}, u32[]{:S(2)}) %all-to-all-start.1) | async-done | bytes 1048608 | tf_op jit(solution)/shard_map/all_to_all | solution.py:172
  88.6 0.0 copy-start.2
  88.6 1.0 copy-done.2
  89.6 5.3 %shard_map.57 = bf16[4,4,64,192]{3,2,1,0:T(8,128)(2,1)} custom-call(s32[4]{0:T(128)} %and_select_fusion.place_ref, bf16[16,256,128]{2,1,0:T(8,128)(2,1)} %copy-done.2, bf16[192,2048]{1,0:T(8,128)(2,1)} %bitcast.7, bf16[192,2048]{1,0:T(8,128)(2,1)} %bitcast.8, bf16[192,2048]{1,0:T(8,128)(2,1)} %bitcast.4.refs_2_, bf16[192,2048]{1,0:T(8,128)(2,1)} %bitcast.5.refs_3_), custom_call_target="tpu_custom_call" | custom-call | tf_op jit(solution)/shard_map/pallas_call | solution.py:119
  94.9 4.3 %all-to-all-start.2 = ((bf16[4,4,64,192]{3,2,1,0:T(8,128)(2,1)}), bf16[4,4,64,192]{3,2,1,0:T(8,128)(2,1)S(1)}, u32[]{:S(2)}, u32[]{:S(2)}) async-start(bf16[4,4,64,192]{3,2,1,0:T(8,128)(2,1)} %shard_map.57), calls=%async_computation.2 | async-start | bytes 1048576 | tf_op jit(solution)/shard_map/all_to_all | solution.py:174
  99.2 0.0 copy-done
  99.2 0.6 constant_dynamic-slice_fusion.gate_ref
  99.8 7.4 %all-to-all-done.2.returned_ref = bf16[4,4,64,192]{3,2,1,0:T(8,128)(2,1)S(1)} async-done(((bf16[4,4,64,192]{3,2,1,0:T(8,128)(2,1)}), bf16[4,4,64,192]{3,2,1,0:T(8,128)(2,1)S(1)}, u32[]{:S(2)}, u32[]{:S(2)}) %all-to-all-start.2) | async-done | bytes 393248 | tf_op jit(solution)/shard_map/all_to_all | solution.py:174
  107.2 0.0 copy-start.3
  107.2 0.8 copy-done.3
  108.0 2.1 %shard_map.58 = bf16[64,3072]{1,0:T(8,128)(2,1)} custom-call(bf16[4,4,64,192]{3,2,1,0:T(8,128)(2,1)} %copy-done.3, bf16[64,3072]{1,0:T(8,128)(2,1)} %latents_ref.1, f32[1,3072]{1,0:T(1,128)} %constant_dynamic-slice_fusion.gate_ref), custom_call_target="tpu_custom_call" | custom-call | tf_op jit(solution)/shard_map/pallas_call | solution.py:142
Async XLA Ops:
  0.0 99.2 %copy-start = (f32[40,3072]{1,0:T(8,128)S(1)}, f32[40,3072]{1,0:T(8,128)}, u32[]{:S(2)}) copy-start(f32[40,3072]{1,0:T(8,128)} %param.8) | copy-start | bytes 1474564
  2.2 23.2 %copy-start.4 = (bf16[2048,192]{0,1:T(8,128)(2,1)S(1)}, bf16[2048,192]{0,1:T(8,128)(2,1)}, u32[]{:S(2)}) copy-start(bf16[2048,192]{0,1:T(8,128)(2,1)} %param.7) | copy-start | bytes 2359300
  25.5 18.8 %copy-start.1 = (bf16[16,3,64,128]{3,2,1,0:T(8,128)(2,1)}, bf16[16,3,64,128]{3,2,1,0:T(8,128)(2,1)S(1)}, u32[]{:S(2)}) copy-start(bf16[16,3,64,128]{3,2,1,0:T(8,128)(2,1)S(1)} %all_to_all.15.qkv_ref) | copy-start | bytes 2359300
  25.5 24.4 %collective-permute-start.1 = (bf16[2048,192]{0,1:T(8,128)(2,1)S(1)}, bf16[2048,192]{0,1:T(8,128)(2,1)S(1)}, u32[]{:S(2)}, u32[]{:S(2)}) collective-permute-start(bf16[2048,192]{0,1:T(8,128)(2,1)S(1)} %copy-done.4), channel_id=1, source_target_pairs={{0,4},{4,8},{8,12},{12,0},{1,5},{5,9},{9,13},{13,1},{2,6},{6,10},{... | collective-permute-start | bytes 2359304 | tf_op jit(solution)/shard_map/ppermute | solution.py:164
  27.7 35.6 %collective-permute-start.2 = (bf16[2048,192]{0,1:T(8,128)(2,1)S(1)}, bf16[2048,192]{0,1:T(8,128)(2,1)}, u32[]{:S(2)}, u32[]{:S(2)}) collective-permute-start(bf16[2048,192]{0,1:T(8,128)(2,1)S(1)} %copy-done.4), channel_id=1, source_target_pairs={{0,8},{4,12},{8,0},{12,4},{1,9},{5,13},{9,1},{13,5},{2,10},{6,14},... | collective-permute-start | bytes 2359304 | tf_op jit(solution)/shard_map/ppermute | solution.py:164
  31.4 35.0 %collective-permute-start.3 = (bf16[2048,192]{0,1:T(8,128)(2,1)S(1)}, bf16[2048,192]{0,1:T(8,128)(2,1)}, u32[]{:S(2)}, u32[]{:S(2)}) collective-permute-start(bf16[2048,192]{0,1:T(8,128)(2,1)S(1)} %copy-done.4), channel_id=1, source_target_pairs={{0,12},{4,0},{8,4},{12,8},{1,13},{5,1},{9,5},{13,9},{2,14},{6,2},{... | collective-permute-start | bytes 2359304 | tf_op jit(solution)/shard_map/ppermute | solution.py:164
  35.2 9.1 %collective-permute-start = (bf16[12,2,64,128]{3,2,1,0:T(8,128)(2,1)}, bf16[12,2,64,128]{3,2,1,0:T(8,128)(2,1)S(1)}, u32[]{:S(2)}, u32[]{:S(2)}) collective-permute-start(bf16[12,2,64,128]{3,2,1,0:T(8,128)(2,1)} %slice.3), channel_id=1, source_target_pairs={{0,16},{16,32},{32,48},{48,64},{64,80},{80,96},{96,112},{112,128},... | collective-permute-start | bytes 1179656 | tf_op jit(solution)/shard_map/ppermute | solution.py:16
  44.3 0.7 copy-start.6
  49.9 16.5 %copy-start.5 = (bf16[2048,192]{0,1:T(8,128)(2,1)}, bf16[2048,192]{0,1:T(8,128)(2,1)S(1)}, u32[]{:S(2)}) copy-start(bf16[2048,192]{0,1:T(8,128)(2,1)S(1)} %collective-permute-done.1) | copy-start | bytes 2359300
  66.4 22.2 %all-to-all-start.1 = ((bf16[16,256,128]{2,1,0:T(8,128)(2,1)}), bf16[16,256,128]{2,1,0:T(8,128)(2,1)S(1)}, u32[]{:S(2)}, u32[]{:S(2)}) async-start(bf16[16,256,128]{2,1,0:T(8,128)(2,1)} %shard_map.56), calls=%async_computation.1 | async-start | bytes 2097152 | tf_op jit(solution)/shard_map/all_to_all | solution.py:172
  72.8 0.7 copy-start.7
  88.6 1.0 copy-start.2
  94.9 12.3 %all-to-all-start.2 = ((bf16[4,4,64,192]{3,2,1,0:T(8,128)(2,1)}), bf16[4,4,64,192]{3,2,1,0:T(8,128)(2,1)S(1)}, u32[]{:S(2)}, u32[]{:S(2)}) async-start(bf16[4,4,64,192]{3,2,1,0:T(8,128)(2,1)} %shard_map.57), calls=%async_computation.2 | async-start | bytes 1048576 | tf_op jit(solution)/shard_map/all_to_all | solution.py:174
  107.2 0.8 copy-start.3

commit v13 on v12

--- a/solution.py
+++ b/solution.py
@@ -157,7 +157,7 @@
 
     chunks = head_chunks(jnp.transpose(projected, (1, 0, 2)), heads)
     qkv = lax.all_to_all(chunks, ("fy", "fp"), split_axis=0, concat_axis=0, tiled=True)
-    qkv, own_weight = lax.optimization_barrier((qkv, out_weight))
+    own_weight = out_weight
     shards = [own_weight]
     for shift in range(1, outer):
         pairs = [(source, (source + shift) % outer) for source in range(outer)]

time: 111 us -> 101 us (0.910)
  blocking collectives: 23.2 us -> 0 us
  starting transfers between devices: 20.9 us -> 31.1 us
  waiting for transfers between devices: 43.7 us -> 47.2 us
    all_to_all x1 -> x0, blocking collectives: 23.2 us -> none  [body(): lax.all_to_all(chunks, ('fy', 'fp'), split_axis=0, concat_axis=0, tiled=T...]
    all_to_all x0 -> x1, starting transfers between devices: none -> 10.4 us  [body(): lax.all_to_all(chunks, ('fy', 'fp'), split_axis=0, concat_axis=0, tiled=T...]
    all_to_all x0 -> x1, waiting for transfers between devices: none -> 2.31 us  [body(): lax.all_to_all(chunks, ('fy', 'fp'), split_axis=0, concat_axis=0, tiled=T...]
    all_to_all x1, starting transfers between devices: 6.39 us -> 4.36 us  [body(): lax.all_to_all(spread, ('fy', 'fp'), split_axis=0, concat_axis=0, tiled=T...]
    ppermute x3, starting transfers between devices: 8.94 us -> 10.7 us  [body(): shards.append(lax.ppermute(own_weight, 'fy', pairs))]
  transfers between devices with their start and end apart: 6 -> 7, of which waited for: 5 -> 5; matrix products, arithmetic and copies ran while one was open for 2% -> 3% of each run, Pallas kernels for 4% -> 5%
where the time goes in v13:
time: 101 us
  waiting for transfers between devices  47.2 us (47%)
  starting transfers between devices  31.1 us (31%)
  Pallas kernels  14.5 us (14%)
  local copies, waits for them, and re-layouts  5.2 us (5%)
  between operations  2.01 us (2%)
    ppermute x3, waiting for transfers between devices, body(): shards.append(lax.ppermute(own_weight, 'fy', pairs))  17.2 us
    all_to_all x1, waiting for transfers between devices, body(): lax.all_to_all(spread, ('fy', 'fp'), split_axis=0, concat_axis=0, tiled=T...  12.2 us
    ppermute x3, starting transfers between devices, body(): shards.append(lax.ppermute(own_weight, 'fy', pairs))  10.7 us
    all_to_all x1, starting transfers between devices, body(): lax.all_to_all(chunks, ('fy', 'fp'), split_axis=0, concat_axis=0, tiled=T...  10.4 us
    ppermute x1, waiting for transfers between devices, passed_along(): lax.ppermute(value, axis, [(source, source + steps) for source in range(i...  8.08 us
    all_to_all x1, waiting for transfers between devices, body(): lax.all_to_all(total, 'fp', split_axis=0, concat_axis=0, tiled=True)  7.37 us
    pallas_call x1, Pallas kernels, project(): pl.pallas_call(projection_kernel, out_shape=jax.ShapeDtypeStruct((groups,...  5.32 us
    pallas_call x1, Pallas kernels, attend(): pl.pallas_call(attention_kernel, out_shape=jax.ShapeDtypeStruct((outer *...  4.85 us
  transfers between devices with their start and end apart: 7, of which 5 were waited for; matrix products, arithmetic and copies ran while one was open for 3% of the time, Pallas kernels for 5%

profile of v13, /device:TPU:1, one launch (start us, length us, event | category | flops | bytes accessed | tf_op | source)
XLA Modules:
  0.0 100.5 jit_solution(3973661902070179518)
XLA Ops:
  0.0 0.0 copy-start
  0.0 2.2 %shard_map.55 = bf16[16,3,64,128]{3,2,1,0:T(8,128)(2,1)} custom-call(bf16[3,64,2048]{2,1,0:T(8,128)(2,1)} %bitcast.9), custom_call_target="tpu_custom_call" | custom-call | tf_op jit(solution)/shard_map/pallas_call | solution.py:88
  2.2 0.0 copy-start.4
  2.2 10.4 %all-to-all-start = ((bf16[16,3,64,128]{3,2,1,0:T(8,128)(2,1)}), bf16[16,3,64,128]{3,2,1,0:T(8,128)(2,1)S(1)}, u32[]{:S(2)}, u32[]{:S(2)}) async-start(bf16[16,3,64,128]{3,2,1,0:T(8,128)(2,1)} %shard_map.55), calls=%async_computation | async-start | bytes 1572864 | tf_op jit(solution)/shard_map/all_to_all | solution.py:159
  12.6 0.0 copy-done.4
  12.6 3.3 %collective-permute-start.1 = (bf16[2048,192]{0,1:T(8,128)(2,1)S(1)}, bf16[2048,192]{0,1:T(8,128)(2,1)S(1)}, u32[]{:S(2)}, u32[]{:S(2)}) collective-permute-start(bf16[2048,192]{0,1:T(8,128)(2,1)S(1)} %copy-done.4), channel_id=1, source_target_pairs={{0,4},{4,8},{8,12},{12,0},{1,5},{5,9},{9,13},{13,1},{2,6},{6,10},{... | collective-permute-start | bytes 2359304 | tf_op jit(solution)/shard_map/ppermute | solution.py:164
  16.0 4.4 %collective-permute-start.2 = (bf16[2048,192]{0,1:T(8,128)(2,1)S(1)}, bf16[2048,192]{0,1:T(8,128)(2,1)}, u32[]{:S(2)}, u32[]{:S(2)}) collective-permute-start(bf16[2048,192]{0,1:T(8,128)(2,1)S(1)} %copy-done.4), channel_id=1, source_target_pairs={{0,8},{4,12},{8,0},{12,4},{1,9},{5,13},{9,1},{13,5},{2,10},{6,14},... | collective-permute-start | bytes 2359304 | tf_op jit(solution)/shard_map/ppermute | solution.py:164
  20.3 3.1 %collective-permute-start.3 = (bf16[2048,192]{0,1:T(8,128)(2,1)S(1)}, bf16[2048,192]{0,1:T(8,128)(2,1)}, u32[]{:S(2)}, u32[]{:S(2)}) collective-permute-start(bf16[2048,192]{0,1:T(8,128)(2,1)S(1)} %copy-done.4), channel_id=1, source_target_pairs={{0,12},{4,0},{8,4},{12,8},{1,13},{5,1},{9,5},{13,9},{2,14},{6,2},{... | collective-permute-start | bytes 2359304 | tf_op jit(solution)/shard_map/ppermute | solution.py:164
  23.4 2.3 %all-to-all-done.qkv_ref = bf16[16,3,64,128]{3,2,1,0:T(8,128)(2,1)S(1)} async-done(((bf16[16,3,64,128]{3,2,1,0:T(8,128)(2,1)}), bf16[16,3,64,128]{3,2,1,0:T(8,128)(2,1)S(1)}, u32[]{:S(2)}, u32[]{:S(2)}) %all-to-all-start) | async-done | bytes 786464 | tf_op jit(solution)/shard_map/all_to_all | solution.py:159
  25.7 0.0 copy-start.1
  25.7 0.8 slice.4
  26.5 1.3 %collective-permute-start = (bf16[12,2,64,128]{3,2,1,0:T(8,128)(2,1)}, bf16[12,2,64,128]{3,2,1,0:T(8,128)(2,1)S(1)}, u32[]{:S(2)}, u32[]{:S(2)}) collective-permute-start(bf16[12,2,64,128]{3,2,1,0:T(8,128)(2,1)} %slice.4), channel_id=1, source_target_pairs={{0,16},{16,32},{32,48},{48,64},{64,80},{80,96},{96,112},{112,128},... | collective-permute-start | bytes 1179656 | tf_op jit(solution)/shard_map/ppermute | solution.py:16
  27.9 8.1 %collective-permute-done.halo_ref = bf16[12,2,64,128]{3,2,1,0:T(8,128)(2,1)S(1)} collective-permute-done((bf16[12,2,64,128]{3,2,1,0:T(8,128)(2,1)}, bf16[12,2,64,128]{3,2,1,0:T(8,128)(2,1)S(1)}, u32[]{:S(2)}, u32[]{:S(2)}) %collective-permute-start) | collective-permute-done | bytes 393248 | tf_op jit(solution)/shard_map/ppermute | solution.py:16
  35.9 0.0 copy-start.6
  35.9 0.0 copy-done.1
  35.9 0.7 copy-done.6
  36.7 4.9 %shard_map.56 = bf16[16,256,128]{2,1,0:T(8,128)(2,1)} custom-call(s32[1]{0:T(128)} %bitcast.flag_ref, bf16[16,3,64,128]{3,2,1,0:T(8,128)(2,1)} %copy-done.1, bf16[12,2,64,128]{3,2,1,0:T(8,128)(2,1)} %copy-done.6), custom_call_target="tpu_custom_call" | custom-call | tf_op jit(solution)/shard_map/pallas_call | solution.py:71
  41.5 0.0 collective-permute-done.1
  41.6 0.0 copy-start.5
  41.6 17.2 %collective-permute-done.2 = bf16[2048,192]{0,1:T(8,128)(2,1)} collective-permute-done((bf16[2048,192]{0,1:T(8,128)(2,1)S(1)}, bf16[2048,192]{0,1:T(8,128)(2,1)}, u32[]{:S(2)}, u32[]{:S(2)}) %collective-permute-start.2) | collective-permute-done | bytes 786464 | tf_op jit(solution)/shard_map/ppermute | solution.py:164
  58.8 0.0 collective-permute-done.3
  58.8 0.0 copy-done.5
  58.8 4.4 %all-to-all-start.1 = ((bf16[16,256,128]{2,1,0:T(8,128)(2,1)}), bf16[16,256,128]{2,1,0:T(8,128)(2,1)S(1)}, u32[]{:S(2)}, u32[]{:S(2)}) async-start(bf16[16,256,128]{2,1,0:T(8,128)(2,1)} %shard_map.56), calls=%async_computation.1 | async-start | bytes 2097152 | tf_op jit(solution)/shard_map/all_to_all | solution.py:172
  63.2 0.0 copy-start.7
  63.2 0.6 copy-done.7
  63.8 0.6 dynamic_slice.7
  66.3 0.5 and_select_fusion.place_ref
  66.9 12.2 %all-to-all-done.1.gathered_ref = bf16[16,256,128]{2,1,0:T(8,128)(2,1)S(1)} async-done(((bf16[16,256,128]{2,1,0:T(8,128)(2,1)}), bf16[16,256,128]{2,1,0:T(8,128)(2,1)S(1)}, u32[]{:S(2)}, u32[]{:S(2)}) %all-to-all-start.1) | async-done | bytes 1048608 | tf_op jit(solution)/shard_map/all_to_all | solution.py:172
  79.0 0.0 copy-start.2
  79.0 1.0 copy-done.2
  80.0 5.3 %shard_map.57 = bf16[4,4,64,192]{3,2,1,0:T(8,128)(2,1)} custom-call(s32[4]{0:T(128)} %and_select_fusion.place_ref, bf16[16,256,128]{2,1,0:T(8,128)(2,1)} %copy-done.2, bf16[192,2048]{1,0:T(8,128)(2,1)} %bitcast.7, bf16[192,2048]{1,0:T(8,128)(2,1)} %bitcast.8, bf16[192,2048]{1,0:T(8,128)(2,1)} %bitcast.4.refs_2_, bf16[192,2048]{1,0:T(8,128)(2,1)} %bitcast.5.refs_3_), custom_call_target="tpu_custom_call" | custom-call | tf_op jit(solution)/shard_map/pallas_call | solution.py:119
  85.3 4.3 %all-to-all-start.2 = ((bf16[4,4,64,192]{3,2,1,0:T(8,128)(2,1)}), bf16[4,4,64,192]{3,2,1,0:T(8,128)(2,1)S(1)}, u32[]{:S(2)}, u32[]{:S(2)}) async-start(bf16[4,4,64,192]{3,2,1,0:T(8,128)(2,1)} %shard_map.57), calls=%async_computation.2 | async-start | bytes 1048576 | tf_op jit(solution)/shard_map/all_to_all | solution.py:174
  89.6 0.0 copy-done
  89.6 0.6 constant_dynamic-slice_fusion.gate_ref
  90.2 7.4 %all-to-all-done.2.returned_ref = bf16[4,4,64,192]{3,2,1,0:T(8,128)(2,1)S(1)} async-done(((bf16[4,4,64,192]{3,2,1,0:T(8,128)(2,1)}), bf16[4,4,64,192]{3,2,1,0:T(8,128)(2,1)S(1)}, u32[]{:S(2)}, u32[]{:S(2)}) %all-to-all-start.2) | async-done | bytes 393248 | tf_op jit(solution)/shard_map/all_to_all | solution.py:174
  97.6 0.0 copy-start.3
  97.6 0.8 copy-done.3
  98.4 2.1 %shard_map.58 = bf16[64,3072]{1,0:T(8,128)(2,1)} custom-call(bf16[4,4,64,192]{3,2,1,0:T(8,128)(2,1)} %copy-done.3, bf16[64,3072]{1,0:T(8,128)(2,1)} %latents_ref.1, f32[1,3072]{1,0:T(1,128)} %constant_dynamic-slice_fusion.gate_ref), custom_call_target="tpu_custom_call" | custom-call | tf_op jit(solution)/shard_map/pallas_call | solution.py:142
Async XLA Ops:
  0.0 89.6 %copy-start = (f32[40,3072]{1,0:T(8,128)S(1)}, f32[40,3072]{1,0:T(8,128)}, u32[]{:S(2)}) copy-start(f32[40,3072]{1,0:T(8,128)} %param.8) | copy-start | bytes 1474564
  2.2 10.4 %copy-start.4 = (bf16[2048,192]{0,1:T(8,128)(2,1)S(1)}, bf16[2048,192]{0,1:T(8,128)(2,1)}, u32[]{:S(2)}) copy-start(bf16[2048,192]{0,1:T(8,128)(2,1)} %param.7) | copy-start | bytes 2359300
  2.2 23.5 %all-to-all-start = ((bf16[16,3,64,128]{3,2,1,0:T(8,128)(2,1)}), bf16[16,3,64,128]{3,2,1,0:T(8,128)(2,1)S(1)}, u32[]{:S(2)}, u32[]{:S(2)}) async-start(bf16[16,3,64,128]{3,2,1,0:T(8,128)(2,1)} %shard_map.55), calls=%async_computation | async-start | bytes 1572864 | tf_op jit(solution)/shard_map/all_to_all | solution.py:159
  12.6 28.9 %collective-permute-start.1 = (bf16[2048,192]{0,1:T(8,128)(2,1)S(1)}, bf16[2048,192]{0,1:T(8,128)(2,1)S(1)}, u32[]{:S(2)}, u32[]{:S(2)}) collective-permute-start(bf16[2048,192]{0,1:T(8,128)(2,1)S(1)} %copy-done.4), channel_id=1, source_target_pairs={{0,4},{4,8},{8,12},{12,0},{1,5},{5,9},{9,13},{13,1},{2,6},{6,10},{... | collective-permute-start | bytes 2359304 | tf_op jit(solution)/shard_map/ppermute | solution.py:164
  16.0 42.8 %collective-permute-start.2 = (bf16[2048,192]{0,1:T(8,128)(2,1)S(1)}, bf16[2048,192]{0,1:T(8,128)(2,1)}, u32[]{:S(2)}, u32[]{:S(2)}) collective-permute-start(bf16[2048,192]{0,1:T(8,128)(2,1)S(1)} %copy-done.4), channel_id=1, source_target_pairs={{0,8},{4,12},{8,0},{12,4},{1,9},{5,13},{9,1},{13,5},{2,10},{6,14},... | collective-permute-start | bytes 2359304 | tf_op jit(solution)/shard_map/ppermute | solution.py:164
  20.3 38.5 %collective-permute-start.3 = (bf16[2048,192]{0,1:T(8,128)(2,1)S(1)}, bf16[2048,192]{0,1:T(8,128)(2,1)}, u32[]{:S(2)}, u32[]{:S(2)}) collective-permute-start(bf16[2048,192]{0,1:T(8,128)(2,1)S(1)} %copy-done.4), channel_id=1, source_target_pairs={{0,12},{4,0},{8,4},{12,8},{1,13},{5,1},{9,5},{13,9},{2,14},{6,2},{... | collective-permute-start | bytes 2359304 | tf_op jit(solution)/shard_map/ppermute | solution.py:164
  25.7 10.2 %copy-start.1 = (bf16[16,3,64,128]{3,2,1,0:T(8,128)(2,1)}, bf16[16,3,64,128]{3,2,1,0:T(8,128)(2,1)S(1)}, u32[]{:S(2)}) copy-start(bf16[16,3,64,128]{3,2,1,0:T(8,128)(2,1)S(1)} %all-to-all-done.qkv_ref) | copy-start | bytes 2359300
  26.5 9.4 %collective-permute-start = (bf16[12,2,64,128]{3,2,1,0:T(8,128)(2,1)}, bf16[12,2,64,128]{3,2,1,0:T(8,128)(2,1)S(1)}, u32[]{:S(2)}, u32[]{:S(2)}) collective-permute-start(bf16[12,2,64,128]{3,2,1,0:T(8,128)(2,1)} %slice.4), channel_id=1, source_target_pairs={{0,16},{16,32},{32,48},{48,64},{64,80},{80,96},{96,112},{112,128},... | collective-permute-start | bytes 1179656 | tf_op jit(solution)/shard_map/ppermute | solution.py:16
  35.9 0.7 copy-start.6
  41.6 17.2 %copy-start.5 = (bf16[2048,192]{0,1:T(8,128)(2,1)}, bf16[2048,192]{0,1:T(8,128)(2,1)S(1)}, u32[]{:S(2)}) copy-start(bf16[2048,192]{0,1:T(8,128)(2,1)S(1)} %collective-permute-done.1) | copy-start | bytes 2359300
  58.8 20.2 %all-to-all-start.1 = ((bf16[16,256,128]{2,1,0:T(8,128)(2,1)}), bf16[16,256,128]{2,1,0:T(8,128)(2,1)S(1)}, u32[]{:S(2)}, u32[]{:S(2)}) async-start(bf16[16,256,128]{2,1,0:T(8,128)(2,1)} %shard_map.56), calls=%async_computation.1 | async-start | bytes 2097152 | tf_op jit(solution)/shard_map/all_to_all | solution.py:172
  63.2 0.7 copy-start.7
  79.0 1.0 copy-start.2
  85.3 12.3 %all-to-all-start.2 = ((bf16[4,4,64,192]{3,2,1,0:T(8,128)(2,1)}), bf16[4,4,64,192]{3,2,1,0:T(8,128)(2,1)S(1)}, u32[]{:S(2)}, u32[]{:S(2)}) async-start(bf16[4,4,64,192]{3,2,1,0:T(8,128)(2,1)} %shard_map.57), calls=%async_computation.2 | async-start | bytes 1048576 | tf_op jit(solution)/shard_map/all_to_all | solution.py:174
  97.6 0.8 copy-start.3

commit v14 on v11

--- a/solution.py
+++ b/solution.py
@@ -96,30 +96,36 @@
 def projection_kernel(place_ref, gathered_ref, *refs):
     weight_refs, out_ref = refs[:-1], refs[-1]
     heads, head_dim = gathered_ref.shape[0], gathered_ref.shape[2]
-    for shift, weight_ref in enumerate(weight_refs):
+    rows = out_ref.shape[2]
+    slots = out_ref.shape[1]
+    pieces = [[ref] for ref in weight_refs[:2]] + [list(weight_refs[2:4])] + [[weight_refs[4]]]
+    for shift in range(slots):
+        parts = pieces[shift]
+        per_part = heads // len(parts)
         total = None
         for head in range(heads):
+            weight_ref = parts[head // per_part]
+            column = (head % per_part) * head_dim
             part = lax.dot_general(
                 gathered_ref[head],
-                weight_ref[:, head * head_dim : (head + 1) * head_dim],
+                weight_ref[:, column : column + head_dim],
                 (((1,), (1,)), ((), ())),
                 preferred_element_type=jnp.float32,
             )
             total = part if total is None else total + part
         total = total.astype(out_ref.dtype)
-        rows = out_ref.shape[2]
         for group in range(out_ref.shape[0]):
             out_ref[group, place_ref[shift]] = total[group * rows : (group + 1) * rows]
 
 
 def project(place, gathered, weights_t, groups):
     vmem = pl.BlockSpec(memory_space=pltpu.VMEM)
-    count, width = len(weights_t), weights_t[0].shape[0]
+    count, width = 4, weights_t[0].shape[0]
     rows = gathered.shape[1] // groups
     return pl.pallas_call(
         projection_kernel,
         out_shape=jax.ShapeDtypeStruct((groups, count, rows, width), jnp.bfloat16),
-        in_specs=[pl.BlockSpec(memory_space=pltpu.SMEM)] + [vmem] * (count + 1),
+        in_specs=[pl.BlockSpec(memory_space=pltpu.SMEM)] + [vmem] * (len(weights_t) + 1),
         out_specs=vmem,
     )(place, gathered, *weights_t)
 
@@ -157,19 +163,26 @@
 
     chunks = head_chunks(jnp.transpose(projected, (1, 0, 2)), heads)
     qkv = lax.all_to_all(chunks, ("fy", "fp"), split_axis=0, concat_axis=0, tiled=True)
-    qkv, own_weight = lax.optimization_barrier((qkv, out_weight))
-    shards = [own_weight]
-    for shift in range(1, outer):
+    def shifted(value, shift):
         pairs = [(source, (source + shift) % outer) for source in range(outer)]
-        shards.append(lax.ppermute(own_weight, "fy", pairs))
+        return lax.ppermute(value, "fy", pairs)
+
+    half = out_weight.shape[0] // 2
+    from_below = shifted(out_weight, 1)
+    from_above = shifted(out_weight, -1)
+    far_low = shifted(from_below[:half], 1)
+    far_high = shifted(from_above[half:], -1)
+    shards = [out_weight, from_below, (far_low, far_high), from_above]
     me_outer = lax.axis_index("fy")
     place = ((me_outer - jnp.arange(outer, dtype=jnp.int32)) % outer).astype(jnp.int32)
     halo = passed_along(qkv[per_frame:, 1:3], "tm", 1)
     flag = (lax.axis_index("tm") > 0).astype(jnp.int32).reshape(1)
     spread = attend(flag, qkv, halo, outer, inner)
+    spread, shards = lax.optimization_barrier((spread, shards))
 
     gathered = lax.all_to_all(spread, ("fy", "fp"), split_axis=0, concat_axis=0, tiled=True)
-    total = project(place, gathered, [jnp.transpose(shard_w) for shard_w in shards], inner)
+    flat = [shards[0], shards[1], shards[2][0], shards[2][1], shards[3]]
+    total = project(place, gathered, [jnp.transpose(shard_w) for shard_w in flat], inner)
     returned = lax.all_to_all(total, "fp", split_axis=0, concat_axis=0, tiled=True)
 
     frame_index = (shard * row_count) // FRAME_TOK

time: 119 us -> 102 us (0.86)
  the two profiles are of different devices: /device:TPU:256 before, /device:TPU:1 now
where the time goes in v14:
time: 102 us; the launch traced here: 100 us
  starting transfers between devices  28.6 us (28%)
  blocking collectives  24.3 us (24%)
  waiting for transfers between devices  22.9 us (22%)
  Pallas kernels  14.4 us (14%)
  local copies, waits for them, and re-layouts  7.7 us (8%)
  between operations  2.01 us (2%)
    all_to_all x1, blocking collectives, body(): lax.all_to_all(chunks, ('fy', 'fp'), split_axis=0, concat_axis=0, tiled=T...  24.3 us
    ppermute x4, starting transfers between devices, shifted(): return lax.ppermute(value, 'fy', pairs)  14.1 us
    all_to_all x1, waiting for transfers between devices, body(): lax.all_to_all(spread, ('fy', 'fp'), split_axis=0, concat_axis=0, tiled=T...  12.1 us
    all_to_all x1, waiting for transfers between devices, body(): lax.all_to_all(total, 'fp', split_axis=0, concat_axis=0, tiled=True)  7.37 us
    all_to_all x1, starting transfers between devices, body(): lax.all_to_all(spread, ('fy', 'fp'), split_axis=0, concat_axis=0, tiled=T...  5.56 us
    pallas_call x1, Pallas kernels, project(): pl.pallas_call(projection_kernel, out_shape=jax.ShapeDtypeStruct((groups,...  5.31 us
    pallas_call x1, Pallas kernels, attend(): pl.pallas_call(attention_kernel, out_shape=jax.ShapeDtypeStruct((outer *...  4.85 us
    ppermute x1, starting transfers between devices, passed_along(): lax.ppermute(value, axis, [(source, source + steps) for source in range(i...  4.66 us
  transfers between devices with their start and end apart: 7, of which 5 were waited for; matrix products, arithmetic and copies ran while one was open for 4% of the time, Pallas kernels for 7%

profile of v14, /device:TPU:1, one launch (start us, length us, event | category | flops | bytes accessed | tf_op | source)
XLA Modules:
  0.0 100.4 jit_solution(14403788835311273623)
XLA Ops:
  0.0 0.0 copy-start
  0.0 4.2 %collective-permute-start.1 = (bf16[2048,192]{0,1:T(8,128)(2,1)}, bf16[2048,192]{0,1:T(8,128)(2,1)S(1)}, u32[]{:S(2)}, u32[]{:S(2)}) collective-permute-start(bf16[2048,192]{0,1:T(8,128)(2,1)} %param.7), channel_id=1, source_target_pairs={{0,4},{4,8},{8,12},{12,0},{1,5},{5,9},{9,13},{13,1},{2,6},{6,10},{... | collective-permute-start | bytes 2359304 | tf_op jit(solution)/shard_map/ppermute | solution.py:168
  4.2 3.4 %collective-permute-start.3 = (bf16[2048,192]{0,1:T(8,128)(2,1)}, bf16[2048,192]{0,1:T(8,128)(2,1)S(1)}, u32[]{:S(2)}, u32[]{:S(2)}) collective-permute-start(bf16[2048,192]{0,1:T(8,128)(2,1)} %param.7), channel_id=1, source_target_pairs={{0,12},{4,0},{8,4},{12,8},{1,13},{5,1},{9,5},{13,9},{2,14},{6,2},{... | collective-permute-start | bytes 2359304 | tf_op jit(solution)/shard_map/ppermute | solution.py:168
  7.5 2.2 %shard_map.55 = bf16[16,3,64,128]{3,2,1,0:T(8,128)(2,1)} custom-call(bf16[3,64,2048]{2,1,0:T(8,128)(2,1)} %bitcast.11), custom_call_target="tpu_custom_call" | custom-call | tf_op jit(solution)/shard_map/pallas_call | solution.py:88
  9.7 24.3 %all_to_all.15.qkv_ref = bf16[16,3,64,128]{3,2,1,0:T(8,128)(2,1)S(1)} all-to-all(bf16[16,3,64,128]{3,2,1,0:T(8,128)(2,1)} %shard_map.55), channel_id=1, replica_groups=mesh['tm'=32,'fy'=4,'fp'=4] {'fy','fp'}, dimensions={0} | all-to-all | bytes 1572864 | tf_op jit(solution)/shard_map/all_to_all | solution.py:165
  34.0 0.0 copy-start.1
  34.0 0.8 slice.12
  34.8 4.7 %collective-permute-start = (bf16[12,2,64,128]{3,2,1,0:T(8,128)(2,1)}, bf16[12,2,64,128]{3,2,1,0:T(8,128)(2,1)S(1)}, u32[]{:S(2)}, u32[]{:S(2)}) collective-permute-start(bf16[12,2,64,128]{3,2,1,0:T(8,128)(2,1)} %slice.12), channel_id=1, source_target_pairs={{0,16},{16,32},{32,48},{48,64},{64,80},{80,96},{96,112},{112,128},... | collective-permute-start | bytes 1179656 | tf_op jit(solution)/shard_map/ppermute | solution.py:16
  39.5 0.0 collective-permute-done.1
  39.5 0.0 copy-start.4
  39.5 0.8 slice.13
  40.3 0.0 copy-done.1
  40.3 3.7 %collective-permute-start.2 = (bf16[1024,192]{0,1:T(8,128)(2,1)}, bf16[1024,192]{0,1:T(8,128)(2,1)S(1)}, u32[]{:S(2)}, u32[]{:S(2)}) collective-permute-start(bf16[1024,192]{0,1:T(8,128)(2,1)} %slice.13), channel_id=1, source_target_pairs={{0,4},{4,8},{8,12},{12,0},{1,5},{5,9},{9,13},{13,1},{2,6},{6,10},{... | collective-permute-start | bytes 1179656 | tf_op jit(solution)/shard_map/ppermute | solution.py:168
  44.1 0.0 collective-permute-done.3
  44.1 0.0 copy-start.5
  44.1 0.8 slice.14
  44.9 0.0 copy-done.4
  44.9 2.8 %collective-permute-start.4 = (bf16[1024,192]{0,1:T(8,128)(2,1)}, bf16[1024,192]{0,1:T(8,128)(2,1)S(1)}, u32[]{:S(2)}, u32[]{:S(2)}) collective-permute-start(bf16[1024,192]{0,1:T(8,128)(2,1)} %slice.14), channel_id=1, source_target_pairs={{0,12},{4,0},{8,4},{12,8},{1,13},{5,1},{9,5},{13,9},{2,14},{6,2},{... | collective-permute-start | bytes 1179656 | tf_op jit(solution)/shard_map/ppermute | solution.py:168
  47.8 0.1 collective-permute-done.halo_ref
  47.9 0.0 copy-start.8
  47.9 0.7 copy-done.8
  48.7 4.8 %shard_map.56 = bf16[16,256,128]{2,1,0:T(8,128)(2,1)} custom-call(s32[1]{0:T(128)} %bitcast.flag_ref, bf16[16,3,64,128]{3,2,1,0:T(8,128)(2,1)} %copy-done.1, bf16[12,2,64,128]{3,2,1,0:T(8,128)(2,1)} %copy-done.8), custom_call_target="tpu_custom_call" | custom-call | tf_op jit(solution)/shard_map/pallas_call | solution.py:71
  53.5 0.0 copy-done.5
  53.5 0.4 collective-permute-done.2
  53.9 0.0 copy-start.6
  53.9 2.8 %collective-permute-done.4 = bf16[1024,192]{0,1:T(8,128)(2,1)S(1)} collective-permute-done((bf16[1024,192]{0,1:T(8,128)(2,1)}, bf16[1024,192]{0,1:T(8,128)(2,1)S(1)}, u32[]{:S(2)}, u32[]{:S(2)}) %collective-permute-start.4) | collective-permute-done | bytes 393248 | tf_op jit(solution)/shard_map/ppermute | solution.py:168
  56.8 0.0 copy-start.7
  56.8 0.8 copy-done.7
  57.5 0.0 copy-done.6
  57.5 5.6 %all-to-all-start.1 = ((bf16[16,256,128]{2,1,0:T(8,128)(2,1)}), bf16[16,256,128]{2,1,0:T(8,128)(2,1)S(1)}, u32[]{:S(2)}, u32[]{:S(2)}) async-start(bf16[16,256,128]{2,1,0:T(8,128)(2,1)} %shard_map.56), calls=%async_computation.1 | async-start | bytes 2097152 | tf_op jit(solution)/shard_map/all_to_all | solution.py:183
  63.1 0.0 copy-start.9
  63.1 0.6 copy-done.9
  63.8 0.6 dynamic_slice.7
  66.3 0.5 and_select_fusion.place_ref
  66.8 12.1 %all-to-all-done.1.gathered_ref = bf16[16,256,128]{2,1,0:T(8,128)(2,1)S(1)} async-done(((bf16[16,256,128]{2,1,0:T(8,128)(2,1)}), bf16[16,256,128]{2,1,0:T(8,128)(2,1)S(1)}, u32[]{:S(2)}, u32[]{:S(2)}) %all-to-all-start.1) | async-done | bytes 1048608 | tf_op jit(solution)/shard_map/all_to_all | solution.py:183
  78.9 0.0 copy-start.2
  78.9 1.0 copy-done.2
  79.9 5.3 %shard_map.57 = bf16[4,4,64,192]{3,2,1,0:T(8,128)(2,1)} custom-call(s32[4]{0:T(128)} %and_select_fusion.place_ref, bf16[16,256,128]{2,1,0:T(8,128)(2,1)} %copy-done.2, bf16[192,2048]{1,0:T(8,128)(2,1)} %bitcast.10, bf16[192,2048]{1,0:T(8,128)(2,1)} %bitcast.8, bf16[192,1024]{1,0:T(8,128)(2,1)} %bitcast.12, bf16[192,1024]{1,0:T(8,128)(2,1)} %bitcast.13, ...), custom_call_target="tpu_custom_call" | custom-call | tf_op jit(solution)/shard_map/pallas_call | solution.py:125
  85.2 4.3 %all-to-all-start.2 = ((bf16[4,4,64,192]{3,2,1,0:T(8,128)(2,1)}), bf16[4,4,64,192]{3,2,1,0:T(8,128)(2,1)S(1)}, u32[]{:S(2)}, u32[]{:S(2)}) async-start(bf16[4,4,64,192]{3,2,1,0:T(8,128)(2,1)} %shard_map.57), calls=%async_computation.2 | async-start | bytes 1048576 | tf_op jit(solution)/shard_map/all_to_all | solution.py:186
  89.5 0.0 copy-done
  89.5 0.6 constant_dynamic-slice_fusion.gate_ref
  90.2 7.4 %all-to-all-done.2.returned_ref = bf16[4,4,64,192]{3,2,1,0:T(8,128)(2,1)S(1)} async-done(((bf16[4,4,64,192]{3,2,1,0:T(8,128)(2,1)}), bf16[4,4,64,192]{3,2,1,0:T(8,128)(2,1)S(1)}, u32[]{:S(2)}, u32[]{:S(2)}) %all-to-all-start.2) | async-done | bytes 393248 | tf_op jit(solution)/shard_map/all_to_all | solution.py:186
  97.5 0.0 copy-start.3
  97.5 0.8 copy-done.3
  98.3 2.1 %shard_map.58 = bf16[64,3072]{1,0:T(8,128)(2,1)} custom-call(bf16[4,4,64,192]{3,2,1,0:T(8,128)(2,1)} %copy-done.3, bf16[64,3072]{1,0:T(8,128)(2,1)} %latents_ref.1, f32[1,3072]{1,0:T(1,128)} %constant_dynamic-slice_fusion.gate_ref), custom_call_target="tpu_custom_call" | custom-call | tf_op jit(solution)/shard_map/pallas_call | solution.py:148
Async XLA Ops:
  0.0 89.5 %copy-start = (f32[40,3072]{1,0:T(8,128)S(1)}, f32[40,3072]{1,0:T(8,128)}, u32[]{:S(2)}) copy-start(f32[40,3072]{1,0:T(8,128)} %param.8) | copy-start | bytes 1474564
  0.0 39.5 %collective-permute-start.1 = (bf16[2048,192]{0,1:T(8,128)(2,1)}, bf16[2048,192]{0,1:T(8,128)(2,1)S(1)}, u32[]{:S(2)}, u32[]{:S(2)}) collective-permute-start(bf16[2048,192]{0,1:T(8,128)(2,1)} %param.7), channel_id=1, source_target_pairs={{0,4},{4,8},{8,12},{12,0},{1,5},{5,9},{9,13},{13,1},{2,6},{6,10},{... | collective-permute-start | bytes 2359304 | tf_op jit(solution)/shard_map/ppermute | solution.py:168
  4.2 39.9 %collective-permute-start.3 = (bf16[2048,192]{0,1:T(8,128)(2,1)}, bf16[2048,192]{0,1:T(8,128)(2,1)S(1)}, u32[]{:S(2)}, u32[]{:S(2)}) collective-permute-start(bf16[2048,192]{0,1:T(8,128)(2,1)} %param.7), channel_id=1, source_target_pairs={{0,12},{4,0},{8,4},{12,8},{1,13},{5,1},{9,5},{13,9},{2,14},{6,2},{... | collective-permute-start | bytes 2359304 | tf_op jit(solution)/shard_map/ppermute | solution.py:168
  34.0 6.4 %copy-start.1 = (bf16[16,3,64,128]{3,2,1,0:T(8,128)(2,1)}, bf16[16,3,64,128]{3,2,1,0:T(8,128)(2,1)S(1)}, u32[]{:S(2)}) copy-start(bf16[16,3,64,128]{3,2,1,0:T(8,128)(2,1)S(1)} %all_to_all.15.qkv_ref) | copy-start | bytes 2359300
  34.8 13.1 %collective-permute-start = (bf16[12,2,64,128]{3,2,1,0:T(8,128)(2,1)}, bf16[12,2,64,128]{3,2,1,0:T(8,128)(2,1)S(1)}, u32[]{:S(2)}, u32[]{:S(2)}) collective-permute-start(bf16[12,2,64,128]{3,2,1,0:T(8,128)(2,1)} %slice.12), channel_id=1, source_target_pairs={{0,16},{16,32},{32,48},{48,64},{64,80},{80,96},{96,112},{112,128},... | collective-permute-start | bytes 1179656 | tf_op jit(solution)/shard_map/ppermute | solution.py:16
  39.5 5.5 %copy-start.4 = (bf16[2048,192]{0,1:T(8,128)(2,1)}, bf16[2048,192]{0,1:T(8,128)(2,1)S(1)}, u32[]{:S(2)}) copy-start(bf16[2048,192]{0,1:T(8,128)(2,1)S(1)} %collective-permute-done.1) | copy-start | bytes 2359300
  40.3 13.6 %collective-permute-start.2 = (bf16[1024,192]{0,1:T(8,128)(2,1)}, bf16[1024,192]{0,1:T(8,128)(2,1)S(1)}, u32[]{:S(2)}, u32[]{:S(2)}) collective-permute-start(bf16[1024,192]{0,1:T(8,128)(2,1)} %slice.13), channel_id=1, source_target_pairs={{0,4},{4,8},{8,12},{12,0},{1,5},{5,9},{9,13},{13,1},{2,6},{6,10},{... | collective-permute-start | bytes 1179656 | tf_op jit(solution)/shard_map/ppermute | solution.py:168
  44.1 9.4 %copy-start.5 = (bf16[2048,192]{0,1:T(8,128)(2,1)}, bf16[2048,192]{0,1:T(8,128)(2,1)S(1)}, u32[]{:S(2)}) copy-start(bf16[2048,192]{0,1:T(8,128)(2,1)S(1)} %collective-permute-done.3) | copy-start | bytes 2359300
  44.9 11.8 %collective-permute-start.4 = (bf16[1024,192]{0,1:T(8,128)(2,1)}, bf16[1024,192]{0,1:T(8,128)(2,1)S(1)}, u32[]{:S(2)}, u32[]{:S(2)}) collective-permute-start(bf16[1024,192]{0,1:T(8,128)(2,1)} %slice.14), channel_id=1, source_target_pairs={{0,12},{4,0},{8,4},{12,8},{1,13},{5,1},{9,5},{13,9},{2,14},{6,2},{... | collective-permute-start | bytes 1179656 | tf_op jit(solution)/shard_map/ppermute | solution.py:168
  47.9 0.7 copy-start.8
  53.9 3.6 %copy-start.6 = (bf16[1024,192]{0,1:T(8,128)(2,1)}, bf16[1024,192]{0,1:T(8,128)(2,1)S(1)}, u32[]{:S(2)}) copy-start(bf16[1024,192]{0,1:T(8,128)(2,1)S(1)} %collective-permute-done.2) | copy-start | bytes 1179652
  56.8 0.8 copy-start.7
  57.5 21.4 %all-to-all-start.1 = ((bf16[16,256,128]{2,1,0:T(8,128)(2,1)}), bf16[16,256,128]{2,1,0:T(8,128)(2,1)S(1)}, u32[]{:S(2)}, u32[]{:S(2)}) async-start(bf16[16,256,128]{2,1,0:T(8,128)(2,1)} %shard_map.56), calls=%async_computation.1 | async-start | bytes 2097152 | tf_op jit(solution)/shard_map/all_to_all | solution.py:183
  63.1 0.7 copy-start.9
  78.9 1.0 copy-start.2
  85.2 12.3 %all-to-all-start.2 = ((bf16[4,4,64,192]{3,2,1,0:T(8,128)(2,1)}), bf16[4,4,64,192]{3,2,1,0:T(8,128)(2,1)S(1)}, u32[]{:S(2)}, u32[]{:S(2)}) async-start(bf16[4,4,64,192]{3,2,1,0:T(8,128)(2,1)} %shard_map.57), calls=%async_computation.2 | async-start | bytes 1048576 | tf_op jit(solution)/shard_map/all_to_all | solution.py:186
  97.5 0.8 copy-start.3

commit v15 on v14

--- a/solution.py
+++ b/solution.py
@@ -178,7 +178,8 @@
     halo = passed_along(qkv[per_frame:, 1:3], "tm", 1)
     flag = (lax.axis_index("tm") > 0).astype(jnp.int32).reshape(1)
     spread = attend(flag, qkv, halo, outer, inner)
-    spread, shards = lax.optimization_barrier((spread, shards))
+    spread, near = lax.optimization_barrier((spread, (shards[1], shards[3])))
+    shards = [shards[0], near[0], shards[2], near[1]]
 
     gathered = lax.all_to_all(spread, ("fy", "fp"), split_axis=0, concat_axis=0, tiled=True)
     flat = [shards[0], shards[1], shards[2][0], shards[2][1], shards[3]]

time: 102 us -> 94.2 us (0.924)
  the two profiles are of different devices: /device:TPU:1 before, /device:TPU:256 now
where the time goes in v15:
time: 94.2 us; the launch traced here: 93.7 us
  waiting for transfers between devices  38.9 us (41%)
  starting transfers between devices  31.4 us (33%)
  Pallas kernels  14.5 us (15%)
  local copies, waits for them, and re-layouts  6.28 us (7%)
  between operations  2.11 us (2%)
    ppermute x4, starting transfers between devices, shifted(): return lax.ppermute(value, 'fy', pairs)  14.1 us
    ppermute x4, waiting for transfers between devices, shifted(): return lax.ppermute(value, 'fy', pairs)  12.3 us
    ppermute x1, waiting for transfers between devices, passed_along(): lax.ppermute(value, axis, [(source, source + steps) for source in range(i...  11.7 us
    all_to_all x1, waiting for transfers between devices, body(): lax.all_to_all(total, 'fp', split_axis=0, concat_axis=0, tiled=True)  8.19 us
    all_to_all x1, waiting for transfers between devices, body(): lax.all_to_all(chunks, ('fy', 'fp'), split_axis=0, concat_axis=0, tiled=T...  6.74 us
    all_to_all x1, starting transfers between devices, body(): lax.all_to_all(chunks, ('fy', 'fp'), split_axis=0, concat_axis=0, tiled=T...  5.5 us
    pallas_call x1, Pallas kernels, project(): pl.pallas_call(projection_kernel, out_shape=jax.ShapeDtypeStruct((groups,...  5.31 us
    pallas_call x1, Pallas kernels, attend(): pl.pallas_call(attention_kernel, out_shape=jax.ShapeDtypeStruct((outer *...  4.86 us
  transfers between devices with their start and end apart: 8, of which 4 were waited for; matrix products, arithmetic and copies ran while one was open for 4% of the time, Pallas kernels for 5%

profile of v15, /device:TPU:256, one launch (start us, length us, event | category | flops | bytes accessed | tf_op | source)
XLA Modules:
  0.0 93.7 jit_solution(17691581449549079602)
XLA Ops:
  0.0 0.0 copy-start
  0.0 2.2 %shard_map.55 = bf16[16,3,64,128]{3,2,1,0:T(8,128)(2,1)} custom-call(bf16[3,64,2048]{2,1,0:T(8,128)(2,1)} %bitcast.10), custom_call_target="tpu_custom_call" | custom-call | tf_op jit(solution)/shard_map/pallas_call | solution.py:88
  2.2 5.5 %all-to-all-start = ((bf16[16,3,64,128]{3,2,1,0:T(8,128)(2,1)}), bf16[16,3,64,128]{3,2,1,0:T(8,128)(2,1)S(1)}, u32[]{:S(2)}, u32[]{:S(2)}) async-start(bf16[16,3,64,128]{3,2,1,0:T(8,128)(2,1)} %shard_map.55), calls=%async_computation | async-start | bytes 1572864 | tf_op jit(solution)/shard_map/all_to_all | solution.py:165
  7.7 3.8 %collective-permute-start.1 = (bf16[2048,192]{0,1:T(8,128)(2,1)}, bf16[2048,192]{0,1:T(8,128)(2,1)S(1)}, u32[]{:S(2)}, u32[]{:S(2)}) collective-permute-start(bf16[2048,192]{0,1:T(8,128)(2,1)} %param.7), channel_id=1, source_target_pairs={{0,4},{4,8},{8,12},{12,0},{1,5},{5,9},{9,13},{13,1},{2,6},{6,10},{... | collective-permute-start | bytes 2359304 | tf_op jit(solution)/shard_map/ppermute | solution.py:168
  11.6 3.2 %collective-permute-start.2 = (bf16[2048,192]{0,1:T(8,128)(2,1)}, bf16[2048,192]{0,1:T(8,128)(2,1)S(1)}, u32[]{:S(2)}, u32[]{:S(2)}) collective-permute-start(bf16[2048,192]{0,1:T(8,128)(2,1)} %param.7), channel_id=1, source_target_pairs={{0,12},{4,0},{8,4},{12,8},{1,13},{5,1},{9,5},{13,9},{2,14},{6,2},{... | collective-permute-start | bytes 2359304 | tf_op jit(solution)/shard_map/ppermute | solution.py:168
  14.8 6.7 %all-to-all-done.qkv_ref = bf16[16,3,64,128]{3,2,1,0:T(8,128)(2,1)S(1)} async-done(((bf16[16,3,64,128]{3,2,1,0:T(8,128)(2,1)}), bf16[16,3,64,128]{3,2,1,0:T(8,128)(2,1)S(1)}, u32[]{:S(2)}, u32[]{:S(2)}) %all-to-all-start) | async-done | bytes 786464 | tf_op jit(solution)/shard_map/all_to_all | solution.py:165
  21.5 0.0 copy-start.1
  21.5 0.8 slice.12
  22.4 4.6 %collective-permute-start = (bf16[12,2,64,128]{3,2,1,0:T(8,128)(2,1)}, bf16[12,2,64,128]{3,2,1,0:T(8,128)(2,1)S(1)}, u32[]{:S(2)}, u32[]{:S(2)}) collective-permute-start(bf16[12,2,64,128]{3,2,1,0:T(8,128)(2,1)} %slice.12), channel_id=1, source_target_pairs={{0,16},{16,32},{32,48},{48,64},{64,80},{80,96},{96,112},{112,128},... | collective-permute-start | bytes 1179656 | tf_op jit(solution)/shard_map/ppermute | solution.py:16
  27.0 11.7 %collective-permute-done.halo_ref = bf16[12,2,64,128]{3,2,1,0:T(8,128)(2,1)S(1)} collective-permute-done((bf16[12,2,64,128]{3,2,1,0:T(8,128)(2,1)}, bf16[12,2,64,128]{3,2,1,0:T(8,128)(2,1)S(1)}, u32[]{:S(2)}, u32[]{:S(2)}) %collective-permute-start) | collective-permute-done | bytes 393248 | tf_op jit(solution)/shard_map/ppermute | solution.py:16
  38.7 0.0 copy-start.8
  38.7 0.0 copy-done.1
  38.7 0.7 copy-done.8
  39.4 4.9 %shard_map.56 = bf16[16,256,128]{2,1,0:T(8,128)(2,1)} custom-call(s32[1]{0:T(128)} %bitcast.flag_ref, bf16[16,3,64,128]{3,2,1,0:T(8,128)(2,1)} %copy-done.1, bf16[12,2,64,128]{3,2,1,0:T(8,128)(2,1)} %copy-done.8), custom_call_target="tpu_custom_call" | custom-call | tf_op jit(solution)/shard_map/pallas_call | solution.py:71
  44.3 0.0 collective-permute-done.1
  44.3 0.0 copy-start.4
  44.3 0.0 collective-permute-done.2
  44.3 0.0 copy-start.5
  44.3 3.7 %all-to-all-start.1 = ((bf16[16,256,128]{2,1,0:T(8,128)(2,1)}), bf16[16,256,128]{2,1,0:T(8,128)(2,1)S(1)}, u32[]{:S(2)}, u32[]{:S(2)}) async-start(bf16[16,256,128]{2,1,0:T(8,128)(2,1)} %shard_map.56), calls=%async_computation.1 | async-start | bytes 2097152 | tf_op jit(solution)/shard_map/all_to_all | solution.py:184
  48.0 0.0 copy-done.4
  48.0 3.7 %collective-permute-start.3 = (bf16[1024,192]{0,1:T(8,128)(2,1)S(1)}, bf16[1024,192]{0,1:T(8,128)(2,1)S(1)}, u32[]{:S(2)}, u32[]{:S(2)}) collective-permute-start(bf16[1024,192]{0,1:T(8,128)(2,1)S(1)} %slice.13), channel_id=1, source_target_pairs={{0,4},{4,8},{8,12},{12,0},{1,5},{5,9},{9,13},{13,1},{2,6},{6,10},{... | collective-permute-start | bytes 1179656 | tf_op jit(solution)/shard_map/ppermute | solution.py:168
  51.8 0.0 copy-done.5
  51.8 0.8 slice.14
  52.6 3.3 %collective-permute-start.4 = (bf16[1024,192]{0,1:T(8,128)(2,1)}, bf16[1024,192]{0,1:T(8,128)(2,1)S(1)}, u32[]{:S(2)}, u32[]{:S(2)}) collective-permute-start(bf16[1024,192]{0,1:T(8,128)(2,1)} %slice.14), channel_id=1, source_target_pairs={{0,12},{4,0},{8,4},{12,8},{1,13},{5,1},{9,5},{13,9},{2,14},{6,2},{... | collective-permute-start | bytes 1179656 | tf_op jit(solution)/shard_map/ppermute | solution.py:168
  55.9 0.0 copy-start.9
  55.9 0.6 copy-done.9
  56.6 0.6 dynamic_slice.7
  59.1 0.5 and_select_fusion.place_ref
  59.6 12.3 %collective-permute-done.3 = bf16[1024,192]{0,1:T(8,128)(2,1)S(1)} collective-permute-done((bf16[1024,192]{0,1:T(8,128)(2,1)S(1)}, bf16[1024,192]{0,1:T(8,128)(2,1)S(1)}, u32[]{:S(2)}, u32[]{:S(2)}) %collective-permute-start.3) | collective-permute-done | bytes 393248 | tf_op jit(solution)/shard_map/ppermute | solution.py:168
  71.9 0.0 copy-start.6
  71.9 0.0 collective-permute-done.4
  71.9 0.0 copy-start.7
  71.9 0.0 all-to-all-done.1.gathered_ref
  71.9 0.0 copy-start.2
  71.9 0.7 copy-done.6
  72.7 0.2 copy-done.7
  72.8 0.3 copy-done.2
  73.2 5.3 %shard_map.57 = bf16[4,4,64,192]{3,2,1,0:T(8,128)(2,1)} custom-call(s32[4]{0:T(128)} %and_select_fusion.place_ref, bf16[16,256,128]{2,1,0:T(8,128)(2,1)} %copy-done.2, bf16[192,2048]{1,0:T(8,128)(2,1)} %bitcast.2.refs_0_, bf16[192,2048]{1,0:T(8,128)(2,1)} %bitcast.8, bf16[192,1024]{1,0:T(8,128)(2,1)} %bitcast.11, bf16[192,1024]{1,0:T(8,128)(2,1)} %bitcast.12, ...), custom_call_target="tpu_custom_call" | custom-call | tf_op jit(solution)/shard_map/pallas_call | solution.py:125
  78.5 3.5 %all-to-all-start.2 = ((bf16[4,4,64,192]{3,2,1,0:T(8,128)(2,1)}), bf16[4,4,64,192]{3,2,1,0:T(8,128)(2,1)S(1)}, u32[]{:S(2)}, u32[]{:S(2)}) async-start(bf16[4,4,64,192]{3,2,1,0:T(8,128)(2,1)} %shard_map.57), calls=%async_computation.2 | async-start | bytes 1048576 | tf_op jit(solution)/shard_map/all_to_all | solution.py:187
  82.0 0.0 copy-done
  82.0 0.6 constant_dynamic-slice_fusion.gate_ref
  82.6 8.2 %all-to-all-done.2.returned_ref = bf16[4,4,64,192]{3,2,1,0:T(8,128)(2,1)S(1)} async-done(((bf16[4,4,64,192]{3,2,1,0:T(8,128)(2,1)}), bf16[4,4,64,192]{3,2,1,0:T(8,128)(2,1)S(1)}, u32[]{:S(2)}, u32[]{:S(2)}) %all-to-all-start.2) | async-done | bytes 393248 | tf_op jit(solution)/shard_map/all_to_all | solution.py:187
  90.8 0.0 copy-start.3
  90.8 0.8 copy-done.3
  91.6 2.1 %shard_map.58 = bf16[64,3072]{1,0:T(8,128)(2,1)} custom-call(bf16[4,4,64,192]{3,2,1,0:T(8,128)(2,1)} %copy-done.3, bf16[64,3072]{1,0:T(8,128)(2,1)} %latents_ref.1, f32[1,3072]{1,0:T(1,128)} %constant_dynamic-slice_fusion.gate_ref), custom_call_target="tpu_custom_call" | custom-call | tf_op jit(solution)/shard_map/pallas_call | solution.py:148
  (1 shorter events, 0.0 us)
Async XLA Ops:
  0.0 82.0 %copy-start = (f32[40,3072]{1,0:T(8,128)S(1)}, f32[40,3072]{1,0:T(8,128)}, u32[]{:S(2)}) copy-start(f32[40,3072]{1,0:T(8,128)} %param.8) | copy-start | bytes 1474564
  2.2 19.3 %all-to-all-start = ((bf16[16,3,64,128]{3,2,1,0:T(8,128)(2,1)}), bf16[16,3,64,128]{3,2,1,0:T(8,128)(2,1)S(1)}, u32[]{:S(2)}, u32[]{:S(2)}) async-start(bf16[16,3,64,128]{3,2,1,0:T(8,128)(2,1)} %shard_map.55), calls=%async_computation | async-start | bytes 1572864 | tf_op jit(solution)/shard_map/all_to_all | solution.py:165
  7.7 36.6 %collective-permute-start.1 = (bf16[2048,192]{0,1:T(8,128)(2,1)}, bf16[2048,192]{0,1:T(8,128)(2,1)S(1)}, u32[]{:S(2)}, u32[]{:S(2)}) collective-permute-start(bf16[2048,192]{0,1:T(8,128)(2,1)} %param.7), channel_id=1, source_target_pairs={{0,4},{4,8},{8,12},{12,0},{1,5},{5,9},{9,13},{13,1},{2,6},{6,10},{... | collective-permute-start | bytes 2359304 | tf_op jit(solution)/shard_map/ppermute | solution.py:168
  11.6 32.7 %collective-permute-start.2 = (bf16[2048,192]{0,1:T(8,128)(2,1)}, bf16[2048,192]{0,1:T(8,128)(2,1)S(1)}, u32[]{:S(2)}, u32[]{:S(2)}) collective-permute-start(bf16[2048,192]{0,1:T(8,128)(2,1)} %param.7), channel_id=1, source_target_pairs={{0,12},{4,0},{8,4},{12,8},{1,13},{5,1},{9,5},{13,9},{2,14},{6,2},{... | collective-permute-start | bytes 2359304 | tf_op jit(solution)/shard_map/ppermute | solution.py:168
  21.5 17.1 %copy-start.1 = (bf16[16,3,64,128]{3,2,1,0:T(8,128)(2,1)}, bf16[16,3,64,128]{3,2,1,0:T(8,128)(2,1)S(1)}, u32[]{:S(2)}) copy-start(bf16[16,3,64,128]{3,2,1,0:T(8,128)(2,1)S(1)} %all-to-all-done.qkv_ref) | copy-start | bytes 2359300
  22.4 16.3 %collective-permute-start = (bf16[12,2,64,128]{3,2,1,0:T(8,128)(2,1)}, bf16[12,2,64,128]{3,2,1,0:T(8,128)(2,1)S(1)}, u32[]{:S(2)}, u32[]{:S(2)}) collective-permute-start(bf16[12,2,64,128]{3,2,1,0:T(8,128)(2,1)} %slice.12), channel_id=1, source_target_pairs={{0,16},{16,32},{32,48},{48,64},{64,80},{80,96},{96,112},{112,128},... | collective-permute-start | bytes 1179656 | tf_op jit(solution)/shard_map/ppermute | solution.py:16
  38.7 0.7 copy-start.8
  44.3 3.7 %copy-start.4 = (bf16[2048,192]{0,1:T(8,128)(2,1)}, bf16[2048,192]{0,1:T(8,128)(2,1)S(1)}, u32[]{:S(2)}) copy-start(bf16[2048,192]{0,1:T(8,128)(2,1)S(1)} %collective-permute-done.1) | copy-start | bytes 2359300
  44.3 7.5 %copy-start.5 = (bf16[2048,192]{0,1:T(8,128)(2,1)}, bf16[2048,192]{0,1:T(8,128)(2,1)S(1)}, u32[]{:S(2)}) copy-start(bf16[2048,192]{0,1:T(8,128)(2,1)S(1)} %collective-permute-done.2) | copy-start | bytes 2359300
  44.3 27.6 %all-to-all-start.1 = ((bf16[16,256,128]{2,1,0:T(8,128)(2,1)}), bf16[16,256,128]{2,1,0:T(8,128)(2,1)S(1)}, u32[]{:S(2)}, u32[]{:S(2)}) async-start(bf16[16,256,128]{2,1,0:T(8,128)(2,1)} %shard_map.56), calls=%async_computation.1 | async-start | bytes 2097152 | tf_op jit(solution)/shard_map/all_to_all | solution.py:184
  48.0 23.9 %collective-permute-start.3 = (bf16[1024,192]{0,1:T(8,128)(2,1)S(1)}, bf16[1024,192]{0,1:T(8,128)(2,1)S(1)}, u32[]{:S(2)}, u32[]{:S(2)}) collective-permute-start(bf16[1024,192]{0,1:T(8,128)(2,1)S(1)} %slice.13), channel_id=1, source_target_pairs={{0,4},{4,8},{8,12},{12,0},{1,5},{5,9},{9,13},{13,1},{2,6},{6,10},{... | collective-permute-start | bytes 1179656 | tf_op jit(solution)/shard_map/ppermute | solution.py:168
  52.6 19.4 %collective-permute-start.4 = (bf16[1024,192]{0,1:T(8,128)(2,1)}, bf16[1024,192]{0,1:T(8,128)(2,1)S(1)}, u32[]{:S(2)}, u32[]{:S(2)}) collective-permute-start(bf16[1024,192]{0,1:T(8,128)(2,1)} %slice.14), channel_id=1, source_target_pairs={{0,12},{4,0},{8,4},{12,8},{1,13},{5,1},{9,5},{13,9},{2,14},{6,2},{... | collective-permute-start | bytes 1179656 | tf_op jit(solution)/shard_map/ppermute | solution.py:168
  55.9 0.7 copy-start.9
  71.9 0.7 copy-start.6
  71.9 0.9 copy-start.7
  71.9 1.2 %copy-start.2 = (bf16[16,256,128]{2,1,0:T(8,128)(2,1)}, bf16[16,256,128]{2,1,0:T(8,128)(2,1)S(1)}, u32[]{:S(2)}) copy-start(bf16[16,256,128]{2,1,0:T(8,128)(2,1)S(1)} %all-to-all-done.1.gathered_ref) | copy-start | bytes 3145732
  78.5 12.3 %all-to-all-start.2 = ((bf16[4,4,64,192]{3,2,1,0:T(8,128)(2,1)}), bf16[4,4,64,192]{3,2,1,0:T(8,128)(2,1)S(1)}, u32[]{:S(2)}, u32[]{:S(2)}) async-start(bf16[4,4,64,192]{3,2,1,0:T(8,128)(2,1)} %shard_map.57), calls=%async_computation.2 | async-start | bytes 1048576 | tf_op jit(solution)/shard_map/all_to_all | solution.py:187
  90.8 0.8 copy-start.3

commit v16 on v14

--- a/solution.py
+++ b/solution.py
@@ -176,9 +176,10 @@
     me_outer = lax.axis_index("fy")
     place = ((me_outer - jnp.arange(outer, dtype=jnp.int32)) % outer).astype(jnp.int32)
     halo = passed_along(qkv[per_frame:, 1:3], "tm", 1)
+    halo, near = lax.optimization_barrier((halo, (shards[1], shards[3])))
+    shards = [shards[0], near[0], shards[2], near[1]]
     flag = (lax.axis_index("tm") > 0).astype(jnp.int32).reshape(1)
     spread = attend(flag, qkv, halo, outer, inner)
-    spread, shards = lax.optimization_barrier((spread, shards))
 
     gathered = lax.all_to_all(spread, ("fy", "fp"), split_axis=0, concat_axis=0, tiled=True)
     flat = [shards[0], shards[1], shards[2][0], shards[2][1], shards[3]]

time: 102 us -> 97.1 us (0.952); the launches traced: 100 us -> 96.6 us
  blocking collectives: 24.3 us -> 0 us
  waiting for transfers between devices: 22.9 us -> 39.8 us
  starting transfers between devices: 28.6 us -> 33.4 us
  local copies, waits for them, and re-layouts: 7.7 us -> 6.31 us
    all_to_all x1 -> x0, blocking collectives: 24.3 us -> none  [body(): lax.all_to_all(chunks, ('fy', 'fp'), split_axis=0, concat_axis=0, tiled=T...]
    ppermute x4, waiting for transfers between devices: 3.26 us -> 25.9 us  [shifted(): return lax.ppermute(value, 'fy', pairs)]
    all_to_all x1, waiting for transfers between devices: 12.1 us -> 0.01 us  [body(): lax.all_to_all(spread, ('fy', 'fp'), split_axis=0, concat_axis=0, tiled=T...]
    all_to_all x0 -> x1, starting transfers between devices: none -> 10.3 us  [body(): lax.all_to_all(chunks, ('fy', 'fp'), split_axis=0, concat_axis=0, tiled=T...]
    all_to_all x0 -> x1, waiting for transfers between devices: none -> 6.56 us  [body(): lax.all_to_all(chunks, ('fy', 'fp'), split_axis=0, concat_axis=0, tiled=T...]
    ppermute x1, starting transfers between devices: 4.66 us -> 1.3 us  [passed_along(): lax.ppermute(value, axis, [(source, source + steps) for source in range(i...]
    ppermute x4, starting transfers between devices: 14.1 us -> 13 us  [shifted(): return lax.ppermute(value, 'fy', pairs)]
    all_to_all x1, starting transfers between devices: 5.56 us -> 4.52 us  [body(): lax.all_to_all(spread, ('fy', 'fp'), split_axis=0, concat_axis=0, tiled=T...]
  transfers between devices with their start and end apart: 7 -> 8, of which waited for: 5 -> 4; matrix products, arithmetic and copies ran while one was open for 4% -> 3% of each run, Pallas kernels for 7% -> 0%
where the time goes in v16:
time: 97.1 us; the launch traced here: 96.6 us
  waiting for transfers between devices  39.8 us (41%)
  starting transfers between devices  33.4 us (34%)
  Pallas kernels  14.5 us (15%)
  local copies, waits for them, and re-layouts  6.31 us (6%)
  between operations  2.09 us (2%)
    ppermute x4, waiting for transfers between devices, shifted(): return lax.ppermute(value, 'fy', pairs)  25.9 us
    ppermute x4, starting transfers between devices, shifted(): return lax.ppermute(value, 'fy', pairs)  13 us
    all_to_all x1, starting transfers between devices, body(): lax.all_to_all(chunks, ('fy', 'fp'), split_axis=0, concat_axis=0, tiled=T...  10.3 us
    all_to_all x1, waiting for transfers between devices, body(): lax.all_to_all(total, 'fp', split_axis=0, concat_axis=0, tiled=True)  7.37 us
    all_to_all x1, waiting for transfers between devices, body(): lax.all_to_all(chunks, ('fy', 'fp'), split_axis=0, concat_axis=0, tiled=T...  6.56 us
    pallas_call x1, Pallas kernels, project(): pl.pallas_call(projection_kernel, out_shape=jax.ShapeDtypeStruct((groups,...  5.31 us
    pallas_call x1, Pallas kernels, attend(): pl.pallas_call(attention_kernel, out_shape=jax.ShapeDtypeStruct((outer *...  4.86 us
    all_to_all x1, starting transfers between devices, body(): lax.all_to_all(spread, ('fy', 'fp'), split_axis=0, concat_axis=0, tiled=T...  4.52 us
  transfers between devices with their start and end apart: 8, of which 4 were waited for; matrix products, arithmetic and copies ran while one was open for 3% of the time, Pallas kernels for 0%

profile of v16, /device:TPU:1, one launch (start us, length us, event | category | flops | bytes accessed | tf_op | source)
XLA Modules:
  0.0 96.6 jit_solution(1168183325691375695)
XLA Ops:
  0.0 0.0 copy-start
  0.0 2.2 %shard_map.55 = bf16[16,3,64,128]{3,2,1,0:T(8,128)(2,1)} custom-call(bf16[3,64,2048]{2,1,0:T(8,128)(2,1)} %bitcast.10), custom_call_target="tpu_custom_call" | custom-call | tf_op jit(solution)/shard_map/pallas_call | solution.py:88
  2.2 10.3 %all-to-all-start = ((bf16[16,3,64,128]{3,2,1,0:T(8,128)(2,1)}), bf16[16,3,64,128]{3,2,1,0:T(8,128)(2,1)S(1)}, u32[]{:S(2)}, u32[]{:S(2)}) async-start(bf16[16,3,64,128]{3,2,1,0:T(8,128)(2,1)} %shard_map.55), calls=%async_computation | async-start | bytes 1572864 | tf_op jit(solution)/shard_map/all_to_all | solution.py:165
  12.5 3.3 %collective-permute-start.1 = (bf16[2048,192]{0,1:T(8,128)(2,1)}, bf16[2048,192]{0,1:T(8,128)(2,1)S(1)}, u32[]{:S(2)}, u32[]{:S(2)}) collective-permute-start(bf16[2048,192]{0,1:T(8,128)(2,1)} %param.7), channel_id=1, source_target_pairs={{0,4},{4,8},{8,12},{12,0},{1,5},{5,9},{9,13},{13,1},{2,6},{6,10},{... | collective-permute-start | bytes 2359304 | tf_op jit(solution)/shard_map/ppermute | solution.py:168
  15.8 3.2 %collective-permute-start.2 = (bf16[2048,192]{0,1:T(8,128)(2,1)}, bf16[2048,192]{0,1:T(8,128)(2,1)S(1)}, u32[]{:S(2)}, u32[]{:S(2)}) collective-permute-start(bf16[2048,192]{0,1:T(8,128)(2,1)} %param.7), channel_id=1, source_target_pairs={{0,12},{4,0},{8,4},{12,8},{1,13},{5,1},{9,5},{13,9},{2,14},{6,2},{... | collective-permute-start | bytes 2359304 | tf_op jit(solution)/shard_map/ppermute | solution.py:168
  19.0 6.6 %all-to-all-done.qkv_ref = bf16[16,3,64,128]{3,2,1,0:T(8,128)(2,1)S(1)} async-done(((bf16[16,3,64,128]{3,2,1,0:T(8,128)(2,1)}), bf16[16,3,64,128]{3,2,1,0:T(8,128)(2,1)S(1)}, u32[]{:S(2)}, u32[]{:S(2)}) %all-to-all-start) | async-done | bytes 786464 | tf_op jit(solution)/shard_map/all_to_all | solution.py:165
  25.6 0.0 copy-start.1
  25.6 0.8 slice.12
  26.4 1.3 %collective-permute-start = (bf16[12,2,64,128]{3,2,1,0:T(8,128)(2,1)}, bf16[12,2,64,128]{3,2,1,0:T(8,128)(2,1)S(1)}, u32[]{:S(2)}, u32[]{:S(2)}) collective-permute-start(bf16[12,2,64,128]{3,2,1,0:T(8,128)(2,1)} %slice.12), channel_id=1, source_target_pairs={{0,16},{16,32},{32,48},{48,64},{64,80},{80,96},{96,112},{112,128},... | collective-permute-start | bytes 1179656 | tf_op jit(solution)/shard_map/ppermute | solution.py:16
  27.7 13.7 %collective-permute-done.1 = bf16[2048,192]{0,1:T(8,128)(2,1)S(1)} collective-permute-done((bf16[2048,192]{0,1:T(8,128)(2,1)}, bf16[2048,192]{0,1:T(8,128)(2,1)S(1)}, u32[]{:S(2)}, u32[]{:S(2)}) %collective-permute-start.1) | collective-permute-done | bytes 786464 | tf_op jit(solution)/shard_map/ppermute | solution.py:168
  41.4 0.0 copy-start.4
  41.4 0.0 collective-permute-done.2
  41.4 0.0 copy-start.5
  41.4 0.0 collective-permute-done.halo_ref
  41.4 0.0 copy-start.8
  41.4 0.0 copy-done.1
  41.4 0.8 copy-done.8
  42.2 4.9 %shard_map.56 = bf16[16,256,128]{2,1,0:T(8,128)(2,1)} custom-call(s32[1]{0:T(128)} %bitcast.flag_ref, bf16[16,3,64,128]{3,2,1,0:T(8,128)(2,1)} %copy-done.1, bf16[12,2,64,128]{3,2,1,0:T(8,128)(2,1)} %copy-done.8), custom_call_target="tpu_custom_call" | custom-call | tf_op jit(solution)/shard_map/pallas_call | solution.py:71
  47.1 4.5 %all-to-all-start.1 = ((bf16[16,256,128]{2,1,0:T(8,128)(2,1)}), bf16[16,256,128]{2,1,0:T(8,128)(2,1)S(1)}, u32[]{:S(2)}, u32[]{:S(2)}) async-start(bf16[16,256,128]{2,1,0:T(8,128)(2,1)} %shard_map.56), calls=%async_computation.1 | async-start | bytes 2097152 | tf_op jit(solution)/shard_map/all_to_all | solution.py:184
  51.6 0.0 copy-done.4
  51.6 3.3 %collective-permute-start.3 = (bf16[1024,192]{0,1:T(8,128)(2,1)S(1)}, bf16[1024,192]{0,1:T(8,128)(2,1)S(1)}, u32[]{:S(2)}, u32[]{:S(2)}) collective-permute-start(bf16[1024,192]{0,1:T(8,128)(2,1)S(1)} %slice.13), channel_id=1, source_target_pairs={{0,4},{4,8},{8,12},{12,0},{1,5},{5,9},{9,13},{13,1},{2,6},{6,10},{... | collective-permute-start | bytes 1179656 | tf_op jit(solution)/shard_map/ppermute | solution.py:168
  54.9 0.0 copy-done.5
  54.9 0.8 slice.14
  55.7 3.2 %collective-permute-start.4 = (bf16[1024,192]{0,1:T(8,128)(2,1)}, bf16[1024,192]{0,1:T(8,128)(2,1)S(1)}, u32[]{:S(2)}, u32[]{:S(2)}) collective-permute-start(bf16[1024,192]{0,1:T(8,128)(2,1)} %slice.14), channel_id=1, source_target_pairs={{0,12},{4,0},{8,4},{12,8},{1,13},{5,1},{9,5},{13,9},{2,14},{6,2},{... | collective-permute-start | bytes 1179656 | tf_op jit(solution)/shard_map/ppermute | solution.py:168
  59.0 0.0 copy-start.9
  59.0 0.6 copy-done.9
  59.6 0.6 dynamic_slice.7
  62.2 0.5 and_select_fusion.place_ref
  62.7 12.2 %collective-permute-done.3 = bf16[1024,192]{0,1:T(8,128)(2,1)S(1)} collective-permute-done((bf16[1024,192]{0,1:T(8,128)(2,1)S(1)}, bf16[1024,192]{0,1:T(8,128)(2,1)S(1)}, u32[]{:S(2)}, u32[]{:S(2)}) %collective-permute-start.3) | collective-permute-done | bytes 393248 | tf_op jit(solution)/shard_map/ppermute | solution.py:168
  74.8 0.0 copy-start.6
  74.8 0.0 collective-permute-done.4
  74.8 0.0 copy-start.7
  74.8 0.0 all-to-all-done.1.gathered_ref
  74.8 0.0 copy-start.2
  74.8 0.7 copy-done.6
  75.6 0.2 copy-done.7
  75.7 0.3 copy-done.2
  76.1 5.3 %shard_map.57 = bf16[4,4,64,192]{3,2,1,0:T(8,128)(2,1)} custom-call(s32[4]{0:T(128)} %and_select_fusion.place_ref, bf16[16,256,128]{2,1,0:T(8,128)(2,1)} %copy-done.2, bf16[192,2048]{1,0:T(8,128)(2,1)} %bitcast.2.refs_0_, bf16[192,2048]{1,0:T(8,128)(2,1)} %bitcast.8, bf16[192,1024]{1,0:T(8,128)(2,1)} %bitcast.11, bf16[192,1024]{1,0:T(8,128)(2,1)} %bitcast.12, ...), custom_call_target="tpu_custom_call" | custom-call | tf_op jit(solution)/shard_map/pallas_call | solution.py:125
  81.4 4.3 %all-to-all-start.2 = ((bf16[4,4,64,192]{3,2,1,0:T(8,128)(2,1)}), bf16[4,4,64,192]{3,2,1,0:T(8,128)(2,1)S(1)}, u32[]{:S(2)}, u32[]{:S(2)}) async-start(bf16[4,4,64,192]{3,2,1,0:T(8,128)(2,1)} %shard_map.57), calls=%async_computation.2 | async-start | bytes 1048576 | tf_op jit(solution)/shard_map/all_to_all | solution.py:187
  85.7 0.0 copy-done
  85.7 0.6 constant_dynamic-slice_fusion.gate_ref
  86.3 7.4 %all-to-all-done.2.returned_ref = bf16[4,4,64,192]{3,2,1,0:T(8,128)(2,1)S(1)} async-done(((bf16[4,4,64,192]{3,2,1,0:T(8,128)(2,1)}), bf16[4,4,64,192]{3,2,1,0:T(8,128)(2,1)S(1)}, u32[]{:S(2)}, u32[]{:S(2)}) %all-to-all-start.2) | async-done | bytes 393248 | tf_op jit(solution)/shard_map/all_to_all | solution.py:187
  93.7 0.0 copy-start.3
  93.7 0.8 copy-done.3
  94.5 2.1 %shard_map.58 = bf16[64,3072]{1,0:T(8,128)(2,1)} custom-call(bf16[4,4,64,192]{3,2,1,0:T(8,128)(2,1)} %copy-done.3, bf16[64,3072]{1,0:T(8,128)(2,1)} %latents_ref.1, f32[1,3072]{1,0:T(1,128)} %constant_dynamic-slice_fusion.gate_ref), custom_call_target="tpu_custom_call" | custom-call | tf_op jit(solution)/shard_map/pallas_call | solution.py:148
  (1 shorter events, 0.0 us)
Async XLA Ops:
  0.0 85.7 %copy-start = (f32[40,3072]{1,0:T(8,128)S(1)}, f32[40,3072]{1,0:T(8,128)}, u32[]{:S(2)}) copy-start(f32[40,3072]{1,0:T(8,128)} %param.8) | copy-start | bytes 1474564
  2.2 23.3 %all-to-all-start = ((bf16[16,3,64,128]{3,2,1,0:T(8,128)(2,1)}), bf16[16,3,64,128]{3,2,1,0:T(8,128)(2,1)S(1)}, u32[]{:S(2)}, u32[]{:S(2)}) async-start(bf16[16,3,64,128]{3,2,1,0:T(8,128)(2,1)} %shard_map.55), calls=%async_computation | async-start | bytes 1572864 | tf_op jit(solution)/shard_map/all_to_all | solution.py:165
  12.5 28.9 %collective-permute-start.1 = (bf16[2048,192]{0,1:T(8,128)(2,1)}, bf16[2048,192]{0,1:T(8,128)(2,1)S(1)}, u32[]{:S(2)}, u32[]{:S(2)}) collective-permute-start(bf16[2048,192]{0,1:T(8,128)(2,1)} %param.7), channel_id=1, source_target_pairs={{0,4},{4,8},{8,12},{12,0},{1,5},{5,9},{9,13},{13,1},{2,6},{6,10},{... | collective-permute-start | bytes 2359304 | tf_op jit(solution)/shard_map/ppermute | solution.py:168
  15.8 25.6 %collective-permute-start.2 = (bf16[2048,192]{0,1:T(8,128)(2,1)}, bf16[2048,192]{0,1:T(8,128)(2,1)S(1)}, u32[]{:S(2)}, u32[]{:S(2)}) collective-permute-start(bf16[2048,192]{0,1:T(8,128)(2,1)} %param.7), channel_id=1, source_target_pairs={{0,12},{4,0},{8,4},{12,8},{1,13},{5,1},{9,5},{13,9},{2,14},{6,2},{... | collective-permute-start | bytes 2359304 | tf_op jit(solution)/shard_map/ppermute | solution.py:168
  25.6 15.9 %copy-start.1 = (bf16[16,3,64,128]{3,2,1,0:T(8,128)(2,1)}, bf16[16,3,64,128]{3,2,1,0:T(8,128)(2,1)S(1)}, u32[]{:S(2)}) copy-start(bf16[16,3,64,128]{3,2,1,0:T(8,128)(2,1)S(1)} %all-to-all-done.qkv_ref) | copy-start | bytes 2359300
  26.4 15.0 %collective-permute-start = (bf16[12,2,64,128]{3,2,1,0:T(8,128)(2,1)}, bf16[12,2,64,128]{3,2,1,0:T(8,128)(2,1)S(1)}, u32[]{:S(2)}, u32[]{:S(2)}) collective-permute-start(bf16[12,2,64,128]{3,2,1,0:T(8,128)(2,1)} %slice.12), channel_id=1, source_target_pairs={{0,16},{16,32},{32,48},{48,64},{64,80},{80,96},{96,112},{112,128},... | collective-permute-start | bytes 1179656 | tf_op jit(solution)/shard_map/ppermute | solution.py:16
  41.4 10.2 %copy-start.4 = (bf16[2048,192]{0,1:T(8,128)(2,1)}, bf16[2048,192]{0,1:T(8,128)(2,1)S(1)}, u32[]{:S(2)}) copy-start(bf16[2048,192]{0,1:T(8,128)(2,1)S(1)} %collective-permute-done.1) | copy-start | bytes 2359300
  41.4 13.5 %copy-start.5 = (bf16[2048,192]{0,1:T(8,128)(2,1)}, bf16[2048,192]{0,1:T(8,128)(2,1)S(1)}, u32[]{:S(2)}) copy-start(bf16[2048,192]{0,1:T(8,128)(2,1)S(1)} %collective-permute-done.2) | copy-start | bytes 2359300
  41.4 0.8 copy-start.8
  47.1 27.8 %all-to-all-start.1 = ((bf16[16,256,128]{2,1,0:T(8,128)(2,1)}), bf16[16,256,128]{2,1,0:T(8,128)(2,1)S(1)}, u32[]{:S(2)}, u32[]{:S(2)}) async-start(bf16[16,256,128]{2,1,0:T(8,128)(2,1)} %shard_map.56), calls=%async_computation.1 | async-start | bytes 2097152 | tf_op jit(solution)/shard_map/all_to_all | solution.py:184
  51.6 23.2 %collective-permute-start.3 = (bf16[1024,192]{0,1:T(8,128)(2,1)S(1)}, bf16[1024,192]{0,1:T(8,128)(2,1)S(1)}, u32[]{:S(2)}, u32[]{:S(2)}) collective-permute-start(bf16[1024,192]{0,1:T(8,128)(2,1)S(1)} %slice.13), channel_id=1, source_target_pairs={{0,4},{4,8},{8,12},{12,0},{1,5},{5,9},{9,13},{13,1},{2,6},{6,10},{... | collective-permute-start | bytes 1179656 | tf_op jit(solution)/shard_map/ppermute | solution.py:168
  55.7 19.1 %collective-permute-start.4 = (bf16[1024,192]{0,1:T(8,128)(2,1)}, bf16[1024,192]{0,1:T(8,128)(2,1)S(1)}, u32[]{:S(2)}, u32[]{:S(2)}) collective-permute-start(bf16[1024,192]{0,1:T(8,128)(2,1)} %slice.14), channel_id=1, source_target_pairs={{0,12},{4,0},{8,4},{12,8},{1,13},{5,1},{9,5},{13,9},{2,14},{6,2},{... | collective-permute-start | bytes 1179656 | tf_op jit(solution)/shard_map/ppermute | solution.py:168
  59.0 0.7 copy-start.9
  74.8 0.7 copy-start.6
  74.8 0.9 copy-start.7
  74.8 1.2 %copy-start.2 = (bf16[16,256,128]{2,1,0:T(8,128)(2,1)}, bf16[16,256,128]{2,1,0:T(8,128)(2,1)S(1)}, u32[]{:S(2)}) copy-start(bf16[16,256,128]{2,1,0:T(8,128)(2,1)S(1)} %all-to-all-done.1.gathered_ref) | copy-start | bytes 3145732
  81.4 12.3 %all-to-all-start.2 = ((bf16[4,4,64,192]{3,2,1,0:T(8,128)(2,1)}), bf16[4,4,64,192]{3,2,1,0:T(8,128)(2,1)S(1)}, u32[]{:S(2)}, u32[]{:S(2)}) async-start(bf16[4,4,64,192]{3,2,1,0:T(8,128)(2,1)} %shard_map.57), calls=%async_computation.2 | async-start | bytes 1048576 | tf_op jit(solution)/shard_map/all_to_all | solution.py:187
  93.7 0.8 copy-start.3

commit v17 on v15

--- a/solution.py
+++ b/solution.py
@@ -94,17 +94,26 @@
 
 
 def projection_kernel(place_ref, gathered_ref, *refs):
-    weight_refs, out_ref = refs[:-1], refs[-1]
+    count = (len(refs) - 2) // 2
+    weight_hbm, out_ref = refs[:count], refs[count]
+    weight_vmem, semaphores = refs[count + 1 : 2 * count + 1], refs[2 * count + 1]
+    copies = [
+        pltpu.make_async_copy(weight_hbm[i], weight_vmem[i], semaphores.at[i]) for i in range(count)
+    ]
+    for copy in copies:
+        copy.start()
     heads, head_dim = gathered_ref.shape[0], gathered_ref.shape[2]
     rows = out_ref.shape[2]
     slots = out_ref.shape[1]
-    pieces = [[ref] for ref in weight_refs[:2]] + [list(weight_refs[2:4])] + [[weight_refs[4]]]
+    pieces = [[0], [1], [2, 3], [4]]
     for shift in range(slots):
         parts = pieces[shift]
+        for index in parts:
+            copies[index].wait()
         per_part = heads // len(parts)
         total = None
         for head in range(heads):
-            weight_ref = parts[head // per_part]
+            weight_ref = weight_vmem[parts[head // per_part]]
             column = (head % per_part) * head_dim
             part = lax.dot_general(
                 gathered_ref[head],
@@ -120,13 +129,16 @@
 
 def project(place, gathered, weights_t, groups):
     vmem = pl.BlockSpec(memory_space=pltpu.VMEM)
+    hbm = pl.BlockSpec(memory_space=pl.ANY)
     count, width = 4, weights_t[0].shape[0]
     rows = gathered.shape[1] // groups
     return pl.pallas_call(
         projection_kernel,
         out_shape=jax.ShapeDtypeStruct((groups, count, rows, width), jnp.bfloat16),
-        in_specs=[pl.BlockSpec(memory_space=pltpu.SMEM)] + [vmem] * (len(weights_t) + 1),
-        out_specs=vmem,
+        in_specs=[pl.BlockSpec(memory_space=pltpu.SMEM), vmem] + [hbm] * len(weights_t),
+        out_specs=vmem,
+        scratch_shapes=[pltpu.VMEM(w.shape, w.dtype) for w in weights_t]
+        + [pltpu.SemaphoreType.DMA((len(weights_t),))],
     )(place, gathered, *weights_t)
 
 

time: 94.2 us -> 97.1 us (1.031)
  Pallas kernels: 14.5 us -> 17.4 us
    pallas_call x1, Pallas kernels: 5.31 us -> 8.19 us  [project(): pl.pallas_call(projection_kernel, out_shape=jax.ShapeDtypeStruct((groups,...]
  transfers between devices with their start and end apart: 8 -> 8, of which waited for: 4 -> 4; matrix products, arithmetic and copies ran while one was open for 4% -> 3% of each run, Pallas kernels for 5% -> 5%
where the time goes in v17:
time: 97.1 us; the launch traced here: 96.6 us
  waiting for transfers between devices  38.9 us (40%)
  starting transfers between devices  31.4 us (32%)
  Pallas kernels  17.4 us (18%)
  local copies, waits for them, and re-layouts  6.28 us (6%)
  between operations  2.12 us (2%)
    ppermute x4, starting transfers between devices, shifted(): return lax.ppermute(value, 'fy', pairs)  14.1 us
    ppermute x4, waiting for transfers between devices, shifted(): return lax.ppermute(value, 'fy', pairs)  12.3 us
    ppermute x1, waiting for transfers between devices, passed_along(): lax.ppermute(value, axis, [(source, source + steps) for source in range(i...  11.7 us
    pallas_call x1, Pallas kernels, project(): pl.pallas_call(projection_kernel, out_shape=jax.ShapeDtypeStruct((groups,...  8.19 us
    all_to_all x1, waiting for transfers between devices, body(): lax.all_to_all(total, 'fp', split_axis=0, concat_axis=0, tiled=True)  8.19 us
    all_to_all x1, waiting for transfers between devices, body(): lax.all_to_all(chunks, ('fy', 'fp'), split_axis=0, concat_axis=0, tiled=T...  6.74 us
    all_to_all x1, starting transfers between devices, body(): lax.all_to_all(chunks, ('fy', 'fp'), split_axis=0, concat_axis=0, tiled=T...  5.5 us
    pallas_call x1, Pallas kernels, attend(): pl.pallas_call(attention_kernel, out_shape=jax.ShapeDtypeStruct((outer *...  4.86 us
  transfers between devices with their start and end apart: 8, of which 4 were waited for; matrix products, arithmetic and copies ran while one was open for 3% of the time, Pallas kernels for 5%

profile of v17, /device:TPU:256, one launch (start us, length us, event | category | flops | bytes accessed | tf_op | source)
XLA Modules:
  0.0 96.6 jit_solution(9732865970400888238)
XLA Ops:
  0.0 0.0 copy-start
  0.0 2.2 %shard_map.55 = bf16[16,3,64,128]{3,2,1,0:T(8,128)(2,1)} custom-call(bf16[3,64,2048]{2,1,0:T(8,128)(2,1)} %bitcast.10), custom_call_target="tpu_custom_call" | custom-call | tf_op jit(solution)/shard_map/pallas_call | solution.py:88
  2.2 5.5 %all-to-all-start = ((bf16[16,3,64,128]{3,2,1,0:T(8,128)(2,1)}), bf16[16,3,64,128]{3,2,1,0:T(8,128)(2,1)S(1)}, u32[]{:S(2)}, u32[]{:S(2)}) async-start(bf16[16,3,64,128]{3,2,1,0:T(8,128)(2,1)} %shard_map.55), calls=%async_computation | async-start | bytes 1572864 | tf_op jit(solution)/shard_map/all_to_all | solution.py:177
  7.7 3.8 %collective-permute-start.1 = (bf16[2048,192]{0,1:T(8,128)(2,1)}, bf16[2048,192]{0,1:T(8,128)(2,1)S(1)}, u32[]{:S(2)}, u32[]{:S(2)}) collective-permute-start(bf16[2048,192]{0,1:T(8,128)(2,1)} %param.7), channel_id=1, source_target_pairs={{0,4},{4,8},{8,12},{12,0},{1,5},{5,9},{9,13},{13,1},{2,6},{6,10},{... | collective-permute-start | bytes 2359304 | tf_op jit(solution)/shard_map/ppermute | solution.py:180
  11.6 3.2 %collective-permute-start.2 = (bf16[2048,192]{0,1:T(8,128)(2,1)}, bf16[2048,192]{0,1:T(8,128)(2,1)S(1)}, u32[]{:S(2)}, u32[]{:S(2)}) collective-permute-start(bf16[2048,192]{0,1:T(8,128)(2,1)} %param.7), channel_id=1, source_target_pairs={{0,12},{4,0},{8,4},{12,8},{1,13},{5,1},{9,5},{13,9},{2,14},{6,2},{... | collective-permute-start | bytes 2359304 | tf_op jit(solution)/shard_map/ppermute | solution.py:180
  14.8 6.7 %all-to-all-done.qkv_ref = bf16[16,3,64,128]{3,2,1,0:T(8,128)(2,1)S(1)} async-done(((bf16[16,3,64,128]{3,2,1,0:T(8,128)(2,1)}), bf16[16,3,64,128]{3,2,1,0:T(8,128)(2,1)S(1)}, u32[]{:S(2)}, u32[]{:S(2)}) %all-to-all-start) | async-done | bytes 786464 | tf_op jit(solution)/shard_map/all_to_all | solution.py:177
  21.5 0.0 copy-start.1
  21.5 0.8 slice.12
  22.4 4.6 %collective-permute-start = (bf16[12,2,64,128]{3,2,1,0:T(8,128)(2,1)}, bf16[12,2,64,128]{3,2,1,0:T(8,128)(2,1)S(1)}, u32[]{:S(2)}, u32[]{:S(2)}) collective-permute-start(bf16[12,2,64,128]{3,2,1,0:T(8,128)(2,1)} %slice.12), channel_id=1, source_target_pairs={{0,16},{16,32},{32,48},{48,64},{64,80},{80,96},{96,112},{112,128},... | collective-permute-start | bytes 1179656 | tf_op jit(solution)/shard_map/ppermute | solution.py:16
  27.0 11.7 %collective-permute-done.halo_ref = bf16[12,2,64,128]{3,2,1,0:T(8,128)(2,1)S(1)} collective-permute-done((bf16[12,2,64,128]{3,2,1,0:T(8,128)(2,1)}, bf16[12,2,64,128]{3,2,1,0:T(8,128)(2,1)S(1)}, u32[]{:S(2)}, u32[]{:S(2)}) %collective-permute-start) | collective-permute-done | bytes 393248 | tf_op jit(solution)/shard_map/ppermute | solution.py:16
  38.7 0.0 copy-start.8
  38.7 0.0 copy-done.1
  38.7 0.7 copy-done.8
  39.4 4.9 %shard_map.56 = bf16[16,256,128]{2,1,0:T(8,128)(2,1)} custom-call(s32[1]{0:T(128)} %bitcast.flag_ref, bf16[16,3,64,128]{3,2,1,0:T(8,128)(2,1)} %copy-done.1, bf16[12,2,64,128]{3,2,1,0:T(8,128)(2,1)} %copy-done.8), custom_call_target="tpu_custom_call" | custom-call | tf_op jit(solution)/shard_map/pallas_call | solution.py:71
  44.3 0.0 collective-permute-done.1
  44.3 0.0 copy-start.4
  44.3 0.0 collective-permute-done.2
  44.3 0.0 copy-start.5
  44.3 3.7 %all-to-all-start.1 = ((bf16[16,256,128]{2,1,0:T(8,128)(2,1)}), bf16[16,256,128]{2,1,0:T(8,128)(2,1)S(1)}, u32[]{:S(2)}, u32[]{:S(2)}) async-start(bf16[16,256,128]{2,1,0:T(8,128)(2,1)} %shard_map.56), calls=%async_computation.1 | async-start | bytes 2097152 | tf_op jit(solution)/shard_map/all_to_all | solution.py:196
  48.0 0.0 copy-done.4
  48.0 3.7 %collective-permute-start.3 = (bf16[1024,192]{0,1:T(8,128)(2,1)S(1)}, bf16[1024,192]{0,1:T(8,128)(2,1)S(1)}, u32[]{:S(2)}, u32[]{:S(2)}) collective-permute-start(bf16[1024,192]{0,1:T(8,128)(2,1)S(1)} %slice.13), channel_id=1, source_target_pairs={{0,4},{4,8},{8,12},{12,0},{1,5},{5,9},{9,13},{13,1},{2,6},{6,10},{... | collective-permute-start | bytes 1179656 | tf_op jit(solution)/shard_map/ppermute | solution.py:180
  51.8 0.0 copy-done.5
  51.8 0.8 slice.14
  52.6 3.3 %collective-permute-start.4 = (bf16[1024,192]{0,1:T(8,128)(2,1)}, bf16[1024,192]{0,1:T(8,128)(2,1)S(1)}, u32[]{:S(2)}, u32[]{:S(2)}) collective-permute-start(bf16[1024,192]{0,1:T(8,128)(2,1)} %slice.14), channel_id=1, source_target_pairs={{0,12},{4,0},{8,4},{12,8},{1,13},{5,1},{9,5},{13,9},{2,14},{6,2},{... | collective-permute-start | bytes 1179656 | tf_op jit(solution)/shard_map/ppermute | solution.py:180
  55.9 0.0 copy-start.9
  55.9 0.6 copy-done.9
  56.6 0.6 dynamic_slice.7
  59.1 0.5 and_select_fusion.place_ref
  59.6 12.3 %collective-permute-done.3 = bf16[1024,192]{0,1:T(8,128)(2,1)S(1)} collective-permute-done((bf16[1024,192]{0,1:T(8,128)(2,1)S(1)}, bf16[1024,192]{0,1:T(8,128)(2,1)S(1)}, u32[]{:S(2)}, u32[]{:S(2)}) %collective-permute-start.3) | collective-permute-done | bytes 393248 | tf_op jit(solution)/shard_map/ppermute | solution.py:180
  71.9 0.0 copy-start.6
  71.9 0.0 collective-permute-done.4
  71.9 0.0 copy-start.7
  71.9 0.0 all-to-all-done.1.gathered_ref
  71.9 0.0 copy-start.2
  71.9 0.7 copy-done.6
  72.7 0.2 copy-done.7
  72.8 0.3 copy-done.2
  73.2 8.2 %shard_map.57 = bf16[4,4,64,192]{3,2,1,0:T(8,128)(2,1)} custom-call(s32[4]{0:T(128)} %and_select_fusion.place_ref, bf16[16,256,128]{2,1,0:T(8,128)(2,1)} %copy-done.2, bf16[192,2048]{1,0:T(8,128)(2,1)} %bitcast.2.refs_0_, bf16[192,2048]{1,0:T(8,128)(2,1)} %bitcast.8, bf16[192,1024]{1,0:T(8,128)(2,1)} %bitcast.11, bf16[192,1024]{1,0:T(8,128)(2,1)} %bitcast.12, ...), custom_call_target="tpu_custom_call" | custom-call | tf_op jit(solution)/shard_map/pallas_call | solution.py:135
  81.4 3.5 %all-to-all-start.2 = ((bf16[4,4,64,192]{3,2,1,0:T(8,128)(2,1)}), bf16[4,4,64,192]{3,2,1,0:T(8,128)(2,1)S(1)}, u32[]{:S(2)}, u32[]{:S(2)}) async-start(bf16[4,4,64,192]{3,2,1,0:T(8,128)(2,1)} %shard_map.57), calls=%async_computation.2 | async-start | bytes 1048576 | tf_op jit(solution)/shard_map/all_to_all | solution.py:199
  84.9 0.0 copy-done
  84.9 0.6 constant_dynamic-slice_fusion.gate_ref
  85.5 8.2 %all-to-all-done.2.returned_ref = bf16[4,4,64,192]{3,2,1,0:T(8,128)(2,1)S(1)} async-done(((bf16[4,4,64,192]{3,2,1,0:T(8,128)(2,1)}), bf16[4,4,64,192]{3,2,1,0:T(8,128)(2,1)S(1)}, u32[]{:S(2)}, u32[]{:S(2)}) %all-to-all-start.2) | async-done | bytes 393248 | tf_op jit(solution)/shard_map/all_to_all | solution.py:199
  93.7 0.0 copy-start.3
  93.7 0.8 copy-done.3
  94.5 2.1 %shard_map.58 = bf16[64,3072]{1,0:T(8,128)(2,1)} custom-call(bf16[4,4,64,192]{3,2,1,0:T(8,128)(2,1)} %copy-done.3, bf16[64,3072]{1,0:T(8,128)(2,1)} %latents_ref.1, f32[1,3072]{1,0:T(1,128)} %constant_dynamic-slice_fusion.gate_ref), custom_call_target="tpu_custom_call" | custom-call | tf_op jit(solution)/shard_map/pallas_call | solution.py:160
  (1 shorter events, 0.0 us)
Async XLA Ops:
  0.0 84.9 %copy-start = (f32[40,3072]{1,0:T(8,128)S(1)}, f32[40,3072]{1,0:T(8,128)}, u32[]{:S(2)}) copy-start(f32[40,3072]{1,0:T(8,128)} %param.8) | copy-start | bytes 1474564
  2.2 19.3 %all-to-all-start = ((bf16[16,3,64,128]{3,2,1,0:T(8,128)(2,1)}), bf16[16,3,64,128]{3,2,1,0:T(8,128)(2,1)S(1)}, u32[]{:S(2)}, u32[]{:S(2)}) async-start(bf16[16,3,64,128]{3,2,1,0:T(8,128)(2,1)} %shard_map.55), calls=%async_computation | async-start | bytes 1572864 | tf_op jit(solution)/shard_map/all_to_all | solution.py:177
  7.7 36.6 %collective-permute-start.1 = (bf16[2048,192]{0,1:T(8,128)(2,1)}, bf16[2048,192]{0,1:T(8,128)(2,1)S(1)}, u32[]{:S(2)}, u32[]{:S(2)}) collective-permute-start(bf16[2048,192]{0,1:T(8,128)(2,1)} %param.7), channel_id=1, source_target_pairs={{0,4},{4,8},{8,12},{12,0},{1,5},{5,9},{9,13},{13,1},{2,6},{6,10},{... | collective-permute-start | bytes 2359304 | tf_op jit(solution)/shard_map/ppermute | solution.py:180
  11.6 32.7 %collective-permute-start.2 = (bf16[2048,192]{0,1:T(8,128)(2,1)}, bf16[2048,192]{0,1:T(8,128)(2,1)S(1)}, u32[]{:S(2)}, u32[]{:S(2)}) collective-permute-start(bf16[2048,192]{0,1:T(8,128)(2,1)} %param.7), channel_id=1, source_target_pairs={{0,12},{4,0},{8,4},{12,8},{1,13},{5,1},{9,5},{13,9},{2,14},{6,2},{... | collective-permute-start | bytes 2359304 | tf_op jit(solution)/shard_map/ppermute | solution.py:180
  21.5 17.1 %copy-start.1 = (bf16[16,3,64,128]{3,2,1,0:T(8,128)(2,1)}, bf16[16,3,64,128]{3,2,1,0:T(8,128)(2,1)S(1)}, u32[]{:S(2)}) copy-start(bf16[16,3,64,128]{3,2,1,0:T(8,128)(2,1)S(1)} %all-to-all-done.qkv_ref) | copy-start | bytes 2359300
  22.4 16.3 %collective-permute-start = (bf16[12,2,64,128]{3,2,1,0:T(8,128)(2,1)}, bf16[12,2,64,128]{3,2,1,0:T(8,128)(2,1)S(1)}, u32[]{:S(2)}, u32[]{:S(2)}) collective-permute-start(bf16[12,2,64,128]{3,2,1,0:T(8,128)(2,1)} %slice.12), channel_id=1, source_target_pairs={{0,16},{16,32},{32,48},{48,64},{64,80},{80,96},{96,112},{112,128},... | collective-permute-start | bytes 1179656 | tf_op jit(solution)/shard_map/ppermute | solution.py:16
  38.7 0.7 copy-start.8
  44.3 3.7 %copy-start.4 = (bf16[2048,192]{0,1:T(8,128)(2,1)}, bf16[2048,192]{0,1:T(8,128)(2,1)S(1)}, u32[]{:S(2)}) copy-start(bf16[2048,192]{0,1:T(8,128)(2,1)S(1)} %collective-permute-done.1) | copy-start | bytes 2359300
  44.3 7.5 %copy-start.5 = (bf16[2048,192]{0,1:T(8,128)(2,1)}, bf16[2048,192]{0,1:T(8,128)(2,1)S(1)}, u32[]{:S(2)}) copy-start(bf16[2048,192]{0,1:T(8,128)(2,1)S(1)} %collective-permute-done.2) | copy-start | bytes 2359300
  44.3 27.6 %all-to-all-start.1 = ((bf16[16,256,128]{2,1,0:T(8,128)(2,1)}), bf16[16,256,128]{2,1,0:T(8,128)(2,1)S(1)}, u32[]{:S(2)}, u32[]{:S(2)}) async-start(bf16[16,256,128]{2,1,0:T(8,128)(2,1)} %shard_map.56), calls=%async_computation.1 | async-start | bytes 2097152 | tf_op jit(solution)/shard_map/all_to_all | solution.py:196
  48.0 23.9 %collective-permute-start.3 = (bf16[1024,192]{0,1:T(8,128)(2,1)S(1)}, bf16[1024,192]{0,1:T(8,128)(2,1)S(1)}, u32[]{:S(2)}, u32[]{:S(2)}) collective-permute-start(bf16[1024,192]{0,1:T(8,128)(2,1)S(1)} %slice.13), channel_id=1, source_target_pairs={{0,4},{4,8},{8,12},{12,0},{1,5},{5,9},{9,13},{13,1},{2,6},{6,10},{... | collective-permute-start | bytes 1179656 | tf_op jit(solution)/shard_map/ppermute | solution.py:180
  52.6 19.4 %collective-permute-start.4 = (bf16[1024,192]{0,1:T(8,128)(2,1)}, bf16[1024,192]{0,1:T(8,128)(2,1)S(1)}, u32[]{:S(2)}, u32[]{:S(2)}) collective-permute-start(bf16[1024,192]{0,1:T(8,128)(2,1)} %slice.14), channel_id=1, source_target_pairs={{0,12},{4,0},{8,4},{12,8},{1,13},{5,1},{9,5},{13,9},{2,14},{6,2},{... | collective-permute-start | bytes 1179656 | tf_op jit(solution)/shard_map/ppermute | solution.py:180
  55.9 0.7 copy-start.9
  71.9 0.7 copy-start.6
  71.9 0.9 copy-start.7
  71.9 1.2 %copy-start.2 = (bf16[16,256,128]{2,1,0:T(8,128)(2,1)}, bf16[16,256,128]{2,1,0:T(8,128)(2,1)S(1)}, u32[]{:S(2)}) copy-start(bf16[16,256,128]{2,1,0:T(8,128)(2,1)S(1)} %all-to-all-done.1.gathered_ref) | copy-start | bytes 3145732
  81.4 12.3 %all-to-all-start.2 = ((bf16[4,4,64,192]{3,2,1,0:T(8,128)(2,1)}), bf16[4,4,64,192]{3,2,1,0:T(8,128)(2,1)S(1)}, u32[]{:S(2)}, u32[]{:S(2)}) async-start(bf16[4,4,64,192]{3,2,1,0:T(8,128)(2,1)} %shard_map.57), calls=%async_computation.2 | async-start | bytes 1048576 | tf_op jit(solution)/shard_map/all_to_all | solution.py:199
  93.7 0.8 copy-start.3

commit v18 on v15

--- a/solution.py
+++ b/solution.py
@@ -1,3 +1,5 @@
+import functools
+
 import jax
 import jax.numpy as jnp
 from jax import lax
@@ -16,7 +18,10 @@
     return lax.ppermute(value, axis, [(source, source + steps) for source in range(initial, last)])
 
 
-def attention_kernel(flag_ref, qkv_ref, halo_ref, out_ref):
+def attention_kernel(frames, flag_ref, qkv_ref, halo_ref, *refs):
+    out_ref = refs[-1]
+    if len(refs) > 1:
+        out_ref[...] = refs[0][...]
     row_count = qkv_ref.shape[2]
     per_frame = FRAME_TOK // row_count
     frame_count = qkv_ref.shape[0] // per_frame
@@ -27,7 +32,7 @@
     def frame_rows(ref, block, plane):
         return ref[pl.ds(block, per_frame), plane].reshape(FRAME_TOK, ref.shape[3])
 
-    for frame in range(frame_count):
+    for frame in frames:
         query = frame_rows(qkv_ref, frame * per_frame, 0)
         blocks = []
         for back in range(WINDOW):
@@ -67,13 +72,24 @@
 
 def attend(flag, qkv, halo, outer, inner):
     width = qkv.shape[3]
-    vmem = pl.BlockSpec(memory_space=pltpu.VMEM)
-    return pl.pallas_call(
-        attention_kernel,
-        out_shape=jax.ShapeDtypeStruct((outer * inner, FRAME_TOK, width), jnp.bfloat16),
-        in_specs=[pl.BlockSpec(memory_space=pltpu.SMEM), vmem, vmem],
-        out_specs=vmem,
-    )(flag, qkv, halo)
+    frame_count = qkv.shape[0] * qkv.shape[2] // FRAME_TOK
+    vmem = pl.BlockSpec(memory_space=pltpu.VMEM)
+    smem = pl.BlockSpec(memory_space=pltpu.SMEM)
+    out_shape = jax.ShapeDtypeStruct((outer * inner, FRAME_TOK, width), jnp.bfloat16)
+    local = tuple(range(WINDOW - 1, frame_count))
+    first = pl.pallas_call(
+        functools.partial(attention_kernel, local),
+        out_shape=out_shape,
+        in_specs=[smem, vmem, vmem],
+        out_specs=vmem,
+    )(flag, qkv, qkv)
+    return pl.pallas_call(
+        functools.partial(attention_kernel, tuple(range(WINDOW - 1))),
+        out_shape=out_shape,
+        in_specs=[smem, vmem, vmem, vmem],
+        out_specs=vmem,
+        input_output_aliases={3: 0},
+    )(flag, qkv, halo, first)
 
 
 def chunk_kernel(rows_ref, out_ref):

time: 94.2 us -> 92.4 us (0.981)
  the two profiles are of different devices: /device:TPU:256 before, /device:TPU:1 now
where the time goes in v18:
time: 92.4 us; the launch traced here: 90.9 us
  starting transfers between devices  34.2 us (37%)
  waiting for transfers between devices  32 us (35%)
  Pallas kernels  17.4 us (19%)
  local copies, waits for them, and re-layouts  4.71 us (5%)
  between operations  2.06 us (2%)
    ppermute x4, waiting for transfers between devices, shifted(): return lax.ppermute(value, 'fy', pairs)  14.3 us
    ppermute x4, starting transfers between devices, shifted(): return lax.ppermute(value, 'fy', pairs)  13 us
    all_to_all x1, starting transfers between devices, body(): lax.all_to_all(chunks, ('fy', 'fp'), split_axis=0, concat_axis=0, tiled=T...  10.3 us
    all_to_all x1, waiting for transfers between devices, body(): lax.all_to_all(total, 'fp', split_axis=0, concat_axis=0, tiled=True)  7.37 us
    all_to_all x1, waiting for transfers between devices, body(): lax.all_to_all(chunks, ('fy', 'fp'), split_axis=0, concat_axis=0, tiled=T...  6.56 us
    pallas_call x1, Pallas kernels, project(): pl.pallas_call(projection_kernel, out_shape=jax.ShapeDtypeStruct((groups,...  5.31 us
    pallas_call x1, Pallas kernels, attend(): pl.pallas_call(functools.partial(attention_kernel, tuple(range(WINDOW - 1...  4.58 us
    all_to_all x1, starting transfers between devices, body(): lax.all_to_all(spread, ('fy', 'fp'), split_axis=0, concat_axis=0, tiled=T...  4.53 us
  transfers between devices with their start and end apart: 8, of which 5 were waited for; matrix products, arithmetic and copies ran while one was open for 3% of the time, Pallas kernels for 9%

profile of v18, /device:TPU:1, one launch (start us, length us, event | category | flops | bytes accessed | tf_op | source)
XLA Modules:
  0.0 90.9 jit_solution(5591058624753946668)
XLA Ops:
  0.0 0.0 copy-start
  0.0 2.2 %shard_map.55 = bf16[16,3,64,128]{3,2,1,0:T(8,128)(2,1)} custom-call(bf16[3,64,2048]{2,1,0:T(8,128)(2,1)} %bitcast.10), custom_call_target="tpu_custom_call" | custom-call | tf_op jit(solution)/shard_map/pallas_call | solution.py:104
  2.2 10.3 %all-to-all-start = ((bf16[16,3,64,128]{3,2,1,0:T(8,128)(2,1)}), bf16[16,3,64,128]{3,2,1,0:T(8,128)(2,1)S(1)}, u32[]{:S(2)}, u32[]{:S(2)}) async-start(bf16[16,3,64,128]{3,2,1,0:T(8,128)(2,1)} %shard_map.55), calls=%async_computation | async-start | bytes 1572864 | tf_op jit(solution)/shard_map/all_to_all | solution.py:181
  12.5 3.3 %collective-permute-start.1 = (bf16[2048,192]{0,1:T(8,128)(2,1)}, bf16[2048,192]{0,1:T(8,128)(2,1)S(1)}, u32[]{:S(2)}, u32[]{:S(2)}) collective-permute-start(bf16[2048,192]{0,1:T(8,128)(2,1)} %param.7), channel_id=1, source_target_pairs={{0,4},{4,8},{8,12},{12,0},{1,5},{5,9},{9,13},{13,1},{2,6},{6,10},{... | collective-permute-start | bytes 2359304 | tf_op jit(solution)/shard_map/ppermute | solution.py:184
  15.8 3.2 %collective-permute-start.2 = (bf16[2048,192]{0,1:T(8,128)(2,1)}, bf16[2048,192]{0,1:T(8,128)(2,1)S(1)}, u32[]{:S(2)}, u32[]{:S(2)}) collective-permute-start(bf16[2048,192]{0,1:T(8,128)(2,1)} %param.7), channel_id=1, source_target_pairs={{0,12},{4,0},{8,4},{12,8},{1,13},{5,1},{9,5},{13,9},{2,14},{6,2},{... | collective-permute-start | bytes 2359304 | tf_op jit(solution)/shard_map/ppermute | solution.py:184
  19.0 6.6 %all-to-all-done.qkv_ref.halo_ref = bf16[16,3,64,128]{3,2,1,0:T(8,128)(2,1)S(1)} async-done(((bf16[16,3,64,128]{3,2,1,0:T(8,128)(2,1)}), bf16[16,3,64,128]{3,2,1,0:T(8,128)(2,1)S(1)}, u32[]{:S(2)}, u32[]{:S(2)}) %all-to-all-start) | async-done | bytes 786464 | tf_op jit(solution)/shard_map/all_to_all | solution.py:181
  25.6 0.0 copy-start.1
  25.6 2.0 %collective-permute-start = (bf16[12,2,64,128]{3,2,1,0:T(8,128)(2,1)S(1)}, bf16[12,2,64,128]{3,2,1,0:T(8,128)(2,1)}, u32[]{:S(2)}, u32[]{:S(2)}) collective-permute-start(bf16[12,2,64,128]{3,2,1,0:T(8,128)(2,1)S(1)} %slice.12), channel_id=1, source_target_pairs={{0,16},{16,32},{32,48},{48,64},{64,80},{80,96},{96,112},{112,128},... | collective-permute-start | bytes 1179656 | tf_op jit(solution)/shard_map/ppermute | solution.py:18
  27.6 0.0 copy-done.1
  27.6 3.2 %shard_map.56.refs_0_ = bf16[16,256,128]{2,1,0:T(8,128)(2,1)} custom-call(s32[1]{0:T(128)} %bitcast.flag_ref, bf16[16,3,64,128]{3,2,1,0:T(8,128)(2,1)} %copy-done.1, bf16[16,3,64,128]{3,2,1,0:T(8,128)(2,1)} %copy-done.1), custom_call_target="tpu_custom_call" | custom-call | tf_op jit(solution)/shard_map/pallas_call | solution.py:80
  30.9 3.8 %collective-permute-done.halo_ref = bf16[12,2,64,128]{3,2,1,0:T(8,128)(2,1)} collective-permute-done((bf16[12,2,64,128]{3,2,1,0:T(8,128)(2,1)S(1)}, bf16[12,2,64,128]{3,2,1,0:T(8,128)(2,1)}, u32[]{:S(2)}, u32[]{:S(2)}) %collective-permute-start) | collective-permute-done | bytes 393248 | tf_op jit(solution)/shard_map/ppermute | solution.py:18
  34.7 4.6 %shard_map.57 = bf16[16,256,128]{2,1,0:T(8,128)(2,1)} custom-call(s32[1]{0:T(128)} %bitcast.flag_ref, bf16[16,3,64,128]{3,2,1,0:T(8,128)(2,1)} %copy-done.1, bf16[12,2,64,128]{3,2,1,0:T(8,128)(2,1)} %collective-permute-done.halo_ref, bf16[16,256,128]{2,1,0:T(8,128)(2,1)} %shard_map.56.refs_0_), custom_call_target="tpu_custom_call", output_to_operand_aliasing={{}: (3, {})} | custom-call | tf_op jit(solution)/shard_map/pallas_call | solution.py:86
  39.3 2.1 %collective-permute-done.1 = bf16[2048,192]{0,1:T(8,128)(2,1)S(1)} collective-permute-done((bf16[2048,192]{0,1:T(8,128)(2,1)}, bf16[2048,192]{0,1:T(8,128)(2,1)S(1)}, u32[]{:S(2)}, u32[]{:S(2)}) %collective-permute-start.1) | collective-permute-done | bytes 786464 | tf_op jit(solution)/shard_map/ppermute | solution.py:184
  41.4 0.0 copy-start.4
  41.4 0.0 collective-permute-done.2
  41.4 0.0 copy-start.5
  41.4 4.5 %all-to-all-start.1 = ((bf16[16,256,128]{2,1,0:T(8,128)(2,1)}), bf16[16,256,128]{2,1,0:T(8,128)(2,1)S(1)}, u32[]{:S(2)}, u32[]{:S(2)}) async-start(bf16[16,256,128]{2,1,0:T(8,128)(2,1)} %shard_map.57), calls=%async_computation.1 | async-start | bytes 2097152 | tf_op jit(solution)/shard_map/all_to_all | solution.py:200
  46.0 0.0 copy-done.4
  46.0 3.3 %collective-permute-start.3 = (bf16[1024,192]{0,1:T(8,128)(2,1)S(1)}, bf16[1024,192]{0,1:T(8,128)(2,1)S(1)}, u32[]{:S(2)}, u32[]{:S(2)}) collective-permute-start(bf16[1024,192]{0,1:T(8,128)(2,1)S(1)} %slice.13), channel_id=1, source_target_pairs={{0,4},{4,8},{8,12},{12,0},{1,5},{5,9},{9,13},{13,1},{2,6},{6,10},{... | collective-permute-start | bytes 1179656 | tf_op jit(solution)/shard_map/ppermute | solution.py:184
  49.3 0.0 copy-done.5
  49.3 0.8 slice.14
  50.1 3.2 %collective-permute-start.4 = (bf16[1024,192]{0,1:T(8,128)(2,1)}, bf16[1024,192]{0,1:T(8,128)(2,1)S(1)}, u32[]{:S(2)}, u32[]{:S(2)}) collective-permute-start(bf16[1024,192]{0,1:T(8,128)(2,1)} %slice.14), channel_id=1, source_target_pairs={{0,12},{4,0},{8,4},{12,8},{1,13},{5,1},{9,5},{13,9},{2,14},{6,2},{... | collective-permute-start | bytes 1179656 | tf_op jit(solution)/shard_map/ppermute | solution.py:184
  53.3 0.0 copy-start.8
  53.4 0.6 copy-done.8
  54.0 0.6 dynamic_slice.7
  56.5 0.5 and_select_fusion.place_ref
  57.1 12.1 %collective-permute-done.3 = bf16[1024,192]{0,1:T(8,128)(2,1)S(1)} collective-permute-done((bf16[1024,192]{0,1:T(8,128)(2,1)S(1)}, bf16[1024,192]{0,1:T(8,128)(2,1)S(1)}, u32[]{:S(2)}, u32[]{:S(2)}) %collective-permute-start.3) | collective-permute-done | bytes 393248 | tf_op jit(solution)/shard_map/ppermute | solution.py:184
  69.2 0.0 copy-start.6
  69.2 0.0 collective-permute-done.4
  69.2 0.0 copy-start.7
  69.2 0.0 all-to-all-done.1.gathered_ref
  69.2 0.0 copy-start.2
  69.2 0.7 copy-done.6
  69.9 0.2 copy-done.7
  70.1 0.3 copy-done.2
  70.4 5.3 %shard_map.58 = bf16[4,4,64,192]{3,2,1,0:T(8,128)(2,1)} custom-call(s32[4]{0:T(128)} %and_select_fusion.place_ref, bf16[16,256,128]{2,1,0:T(8,128)(2,1)} %copy-done.2, bf16[192,2048]{1,0:T(8,128)(2,1)} %bitcast.2.refs_0_, bf16[192,2048]{1,0:T(8,128)(2,1)} %bitcast.8, bf16[192,1024]{1,0:T(8,128)(2,1)} %bitcast.11, bf16[192,1024]{1,0:T(8,128)(2,1)} %bitcast.12, ...), custom_call_target="tpu_custom_call" | custom-call | tf_op jit(solution)/shard_map/pallas_call | solution.py:141
  75.7 4.3 %all-to-all-start.2 = ((bf16[4,4,64,192]{3,2,1,0:T(8,128)(2,1)}), bf16[4,4,64,192]{3,2,1,0:T(8,128)(2,1)S(1)}, u32[]{:S(2)}, u32[]{:S(2)}) async-start(bf16[4,4,64,192]{3,2,1,0:T(8,128)(2,1)} %shard_map.58), calls=%async_computation.2 | async-start | bytes 1048576 | tf_op jit(solution)/shard_map/all_to_all | solution.py:203
  80.0 0.0 copy-done
  80.0 0.6 constant_dynamic-slice_fusion.gate_ref
  80.7 7.4 %all-to-all-done.2.returned_ref = bf16[4,4,64,192]{3,2,1,0:T(8,128)(2,1)S(1)} async-done(((bf16[4,4,64,192]{3,2,1,0:T(8,128)(2,1)}), bf16[4,4,64,192]{3,2,1,0:T(8,128)(2,1)S(1)}, u32[]{:S(2)}, u32[]{:S(2)}) %all-to-all-start.2) | async-done | bytes 393248 | tf_op jit(solution)/shard_map/all_to_all | solution.py:203
  88.0 0.0 copy-start.3
  88.0 0.8 copy-done.3
  88.8 2.1 %shard_map.59 = bf16[64,3072]{1,0:T(8,128)(2,1)} custom-call(bf16[4,4,64,192]{3,2,1,0:T(8,128)(2,1)} %copy-done.3, bf16[64,3072]{1,0:T(8,128)(2,1)} %latents_ref.1, f32[1,3072]{1,0:T(1,128)} %constant_dynamic-slice_fusion.gate_ref), custom_call_target="tpu_custom_call" | custom-call | tf_op jit(solution)/shard_map/pallas_call | solution.py:164
  (2 shorter events, 0.1 us)
Async XLA Ops:
  0.0 80.0 %copy-start = (f32[40,3072]{1,0:T(8,128)S(1)}, f32[40,3072]{1,0:T(8,128)}, u32[]{:S(2)}) copy-start(f32[40,3072]{1,0:T(8,128)} %param.8) | copy-start | bytes 1474564
  2.2 23.3 %all-to-all-start = ((bf16[16,3,64,128]{3,2,1,0:T(8,128)(2,1)}), bf16[16,3,64,128]{3,2,1,0:T(8,128)(2,1)S(1)}, u32[]{:S(2)}, u32[]{:S(2)}) async-start(bf16[16,3,64,128]{3,2,1,0:T(8,128)(2,1)} %shard_map.55), calls=%async_computation | async-start | bytes 1572864 | tf_op jit(solution)/shard_map/all_to_all | solution.py:181
  12.5 28.9 %collective-permute-start.1 = (bf16[2048,192]{0,1:T(8,128)(2,1)}, bf16[2048,192]{0,1:T(8,128)(2,1)S(1)}, u32[]{:S(2)}, u32[]{:S(2)}) collective-permute-start(bf16[2048,192]{0,1:T(8,128)(2,1)} %param.7), channel_id=1, source_target_pairs={{0,4},{4,8},{8,12},{12,0},{1,5},{5,9},{9,13},{13,1},{2,6},{6,10},{... | collective-permute-start | bytes 2359304 | tf_op jit(solution)/shard_map/ppermute | solution.py:184
  15.8 25.6 %collective-permute-start.2 = (bf16[2048,192]{0,1:T(8,128)(2,1)}, bf16[2048,192]{0,1:T(8,128)(2,1)S(1)}, u32[]{:S(2)}, u32[]{:S(2)}) collective-permute-start(bf16[2048,192]{0,1:T(8,128)(2,1)} %param.7), channel_id=1, source_target_pairs={{0,12},{4,0},{8,4},{12,8},{1,13},{5,1},{9,5},{13,9},{2,14},{6,2},{... | collective-permute-start | bytes 2359304 | tf_op jit(solution)/shard_map/ppermute | solution.py:184
  25.6 2.1 %copy-start.1 = (bf16[16,3,64,128]{3,2,1,0:T(8,128)(2,1)}, bf16[16,3,64,128]{3,2,1,0:T(8,128)(2,1)S(1)}, u32[]{:S(2)}) copy-start(bf16[16,3,64,128]{3,2,1,0:T(8,128)(2,1)S(1)} %all-to-all-done.qkv_ref.halo_ref) | copy-start | bytes 2359300
  25.6 9.1 %collective-permute-start = (bf16[12,2,64,128]{3,2,1,0:T(8,128)(2,1)S(1)}, bf16[12,2,64,128]{3,2,1,0:T(8,128)(2,1)}, u32[]{:S(2)}, u32[]{:S(2)}) collective-permute-start(bf16[12,2,64,128]{3,2,1,0:T(8,128)(2,1)S(1)} %slice.12), channel_id=1, source_target_pairs={{0,16},{16,32},{32,48},{48,64},{64,80},{80,96},{96,112},{112,128},... | collective-permute-start | bytes 1179656 | tf_op jit(solution)/shard_map/ppermute | solution.py:18
  41.4 4.5 %copy-start.4 = (bf16[2048,192]{0,1:T(8,128)(2,1)}, bf16[2048,192]{0,1:T(8,128)(2,1)S(1)}, u32[]{:S(2)}) copy-start(bf16[2048,192]{0,1:T(8,128)(2,1)S(1)} %collective-permute-done.1) | copy-start | bytes 2359300
  41.4 7.9 %copy-start.5 = (bf16[2048,192]{0,1:T(8,128)(2,1)}, bf16[2048,192]{0,1:T(8,128)(2,1)S(1)}, u32[]{:S(2)}) copy-start(bf16[2048,192]{0,1:T(8,128)(2,1)S(1)} %collective-permute-done.2) | copy-start | bytes 2359300
  41.4 27.8 %all-to-all-start.1 = ((bf16[16,256,128]{2,1,0:T(8,128)(2,1)}), bf16[16,256,128]{2,1,0:T(8,128)(2,1)S(1)}, u32[]{:S(2)}, u32[]{:S(2)}) async-start(bf16[16,256,128]{2,1,0:T(8,128)(2,1)} %shard_map.57), calls=%async_computation.1 | async-start | bytes 2097152 | tf_op jit(solution)/shard_map/all_to_all | solution.py:200
  46.0 23.2 %collective-permute-start.3 = (bf16[1024,192]{0,1:T(8,128)(2,1)S(1)}, bf16[1024,192]{0,1:T(8,128)(2,1)S(1)}, u32[]{:S(2)}, u32[]{:S(2)}) collective-permute-start(bf16[1024,192]{0,1:T(8,128)(2,1)S(1)} %slice.13), channel_id=1, source_target_pairs={{0,4},{4,8},{8,12},{12,0},{1,5},{5,9},{9,13},{13,1},{2,6},{6,10},{... | collective-permute-start | bytes 1179656 | tf_op jit(solution)/shard_map/ppermute | solution.py:184
  50.1 19.1 %collective-permute-start.4 = (bf16[1024,192]{0,1:T(8,128)(2,1)}, bf16[1024,192]{0,1:T(8,128)(2,1)S(1)}, u32[]{:S(2)}, u32[]{:S(2)}) collective-permute-start(bf16[1024,192]{0,1:T(8,128)(2,1)} %slice.14), channel_id=1, source_target_pairs={{0,12},{4,0},{8,4},{12,8},{1,13},{5,1},{9,5},{13,9},{2,14},{6,2},{... | collective-permute-start | bytes 1179656 | tf_op jit(solution)/shard_map/ppermute | solution.py:184
  53.3 0.7 copy-start.8
  69.2 0.7 copy-start.6
  69.2 0.9 copy-start.7
  69.2 1.2 %copy-start.2 = (bf16[16,256,128]{2,1,0:T(8,128)(2,1)}, bf16[16,256,128]{2,1,0:T(8,128)(2,1)S(1)}, u32[]{:S(2)}) copy-start(bf16[16,256,128]{2,1,0:T(8,128)(2,1)S(1)} %all-to-all-done.1.gathered_ref) | copy-start | bytes 3145732
  75.7 12.3 %all-to-all-start.2 = ((bf16[4,4,64,192]{3,2,1,0:T(8,128)(2,1)}), bf16[4,4,64,192]{3,2,1,0:T(8,128)(2,1)S(1)}, u32[]{:S(2)}, u32[]{:S(2)}) async-start(bf16[4,4,64,192]{3,2,1,0:T(8,128)(2,1)} %shard_map.58), calls=%async_computation.2 | async-start | bytes 1048576 | tf_op jit(solution)/shard_map/all_to_all | solution.py:203
  88.0 0.8 copy-start.3
